TPU v7x, 128 devices: a whole 4x4x4 slice. The times are simulated.
128 devices in a mesh: row: 8 (over x, core), col: 16 (over y, z).
Axes of the slice: x: 4, y: 4, z: 4, core: 2. Of those that a mesh axis runs over, the one named last changes fastest.
Arguments:
- density_values: bfloat16 [512, 8, 128, 128], P(('row', 'col')), may hold values from -0.59765625 to 0.59765625
- density_cols: int32 [512, 8], P(('row', 'col')), may hold values from -4 to 4, as said below
- density_counts: int32 [512], P(('row', 'col')), may hold values from 1 to 8, 3072 in all
- square_cols: int32 [512, 16], P(('row', 'col')), may hold values from -8 to 8, as said below
- update_cols: int32 [512, 16], P(('row', 'col')), may hold values from -12 to 12, as said below
- target_trace: float32 [1], replicated, may hold values from -8388608 to -1048576
Outputs:
- square: bfloat16 [512, 16, 128, 128], P(('row', 'col'))
- purified: bfloat16 [512, 16, 128, 128], P(('row', 'col'))
Inputs may be any that keep to these rules, and one draw needn't show every extreme that they name: `density_cols`: distinct within a block row; every even block row holds -4, every odd one 4. `density_counts`: the live blocks of a row are its first slots. `square_cols`: distinct within a block row; every even block row holds -8, every odd one 2 * 4. `update_cols`: distinct within a block row; every even block row holds -12, every odd one 3 * 4.
All inputs are finite; a program needn't handle non-finite values.
Results may differ from a plain program's by a relative error of at most 0.0058.
Values may be sent and summed in bfloat16 or wider, within the bound.
No kernel may reach another device: no remote copies, remote signals or barrier semaphores. Data moves between devices by JAX's collectives and lax.ppermute only.
A program may use at most 192 MiB of HBM per device.

v0:
```python
import jax
import jax.numpy as jnp
from jax import lax
from jax.sharding import PartitionSpec as P

HALF = 4
BF16 = jnp.bfloat16
F32 = jnp.float32


def passed_along(value, axis, steps):
    count = lax.axis_size(axis)
    pairs = [(source, (source + steps) % count) for source in range(count)]
    return lax.ppermute(value, axis, pairs)


def assemble(earlier, own_parts, later):
    joined = []
    for member in range(len(own_parts)):
        pieces = (
            [arrival[member] for arrival in reversed(earlier)]
            + [own_parts[member]]
            + [arrival[member] for arrival in later]
        )
        joined.append(jnp.concatenate(pieces, axis=0))
    return tuple(joined)


def spread(blocks, columns, reach_devices):
    earlier, later = ([], [])
    for heading, arrivals in ((1, earlier), (-1, later)):
        carried = (blocks, columns)
        for _ in range(reach_devices):
            carried = passed_along(carried, ("row", "col"), heading)
            arrivals.append(carried)
    return assemble(earlier, (blocks, columns), later)


def butterfly_sum(value, axes):
    count = 1
    for axis in axes:
        count *= lax.axis_size(axis)
    step = 1
    while step < count:
        pairs = [(source, source ^ step) for source in range(count)]
        value = value + lax.ppermute(value, axes, pairs)
        step *= 2
    return value


def place_onehot(first_row, row_count, columns, low, width):
    rows = jnp.arange(row_count, dtype=jnp.int32)[:, None, None] + first_row
    target = rows + columns[:, None, :] - low
    places = jnp.arange(width, dtype=jnp.int32)[None, :, None]
    return (target == places).astype(BF16)


def densify(blocks, columns, first_row, low, width):
    onehot = place_onehot(first_row, blocks.shape[0], columns, low, width)
    dense = jnp.einsum("rcs,rsyz->rycz", onehot, blocks, preferred_element_type=F32)
    return dense.astype(BF16)


def slab_matmul(left, right):
    r, b, k, _ = left.shape
    n = right.shape[2]
    out = jnp.dot(
        left.reshape(r * b, k * b), right.reshape(k * b, n * b), preferred_element_type=F32
    )
    return out.reshape(r, b, n, b)


def extract(dense, columns, low):
    onehot = place_onehot(0, dense.shape[0], columns, low, dense.shape[2])
    picked = jnp.einsum("rcs,rxcz->rsxz", onehot, dense, preferred_element_type=F32)
    return picked.astype(BF16)


def shards(density_values, density_cols, density_counts, square_cols, update_cols, target_trace):
    rows_here = density_values.shape[0]
    reach_devices = (2 * HALF + rows_here - 1) // rows_here
    margin = reach_devices * rows_here
    is_live = (
        jnp.arange(density_values.shape[1], dtype=jnp.int32)[None, :] < density_counts[:, None]
    )
    masked = jnp.where(is_live[:, :, None, None], density_values, jnp.zeros_like(density_values))
    masked_wide, cols_wide = spread(masked, density_cols, reach_devices)

    d_local = densify(masked, density_cols, 0, -HALF, rows_here + 2 * HALF)
    near = slice(margin - HALF, margin + rows_here + HALF)
    d_near = densify(masked_wide[near], cols_wide[near], -HALF, -2 * HALF, rows_here + 4 * HALF)
    square_dense = slab_matmul(d_local, d_near).astype(BF16)
    pattern = jnp.max(place_onehot(0, rows_here, square_cols, -2 * HALF, rows_here + 4 * HALF), axis=2)
    s_local = jnp.where(pattern[:, None, :, None] > 0, square_dense, jnp.zeros_like(square_dense))
    square = extract(s_local, square_cols, -2 * HALF)

    square_wide, square_cols_wide = spread(square, square_cols, reach_devices)
    far = slice(margin - 2 * HALF, margin + rows_here + 2 * HALF)
    d_far = densify(masked_wide[far], cols_wide[far], -2 * HALF, -3 * HALF, rows_here + 6 * HALF)
    s_far = densify(
        square_wide[far], square_cols_wide[far], -2 * HALF, -3 * HALF, rows_here + 6 * HALF
    )

    trace_two = jnp.sum(jnp.square(masked.astype(F32)))
    trace_three = jnp.sum(
        s_local[:, :, HALF : HALF + rows_here + 2 * HALF, :].astype(F32) * d_local.astype(F32)
    )
    trace_four = jnp.sum(jnp.square(s_local.astype(F32)))
    local_sums, _ = lax.optimization_barrier(
        (jnp.stack([trace_two, trace_three, trace_four]), square_wide)
    )
    sums = butterfly_sum(local_sums, ("row", "col"))
    total_two, total_three, total_four = sums[0], sums[1], sums[2]

    cube_dense = slab_matmul(s_local, d_far)
    quartic_dense = slab_matmul(s_local, s_far)
    gamma_mix = (target_trace[0] - 4.0 * total_three + 3.0 * total_four) / (
        total_two - 2.0 * total_three + total_four + 1e-06
    )
    carried = jnp.pad(s_local, ((0, 0), (0, 0), (HALF, HALF), (0, 0))).astype(F32)
    purified_dense = (
        (4.0 - 2.0 * gamma_mix) * cube_dense
        + (gamma_mix - 3.0) * quartic_dense
        + gamma_mix * carried
    ).astype(BF16)
    purified = extract(purified_dense, update_cols, -3 * HALF)
    return (square, purified)


def solution(mesh):
    return jax.shard_map(
        shards,
        mesh=mesh,
        in_specs=(
            P(("row", "col"), None, None, None),
            P(("row", "col"), None),
            P(("row", "col")),
            P(("row", "col"), None),
            P(("row", "col"), None),
            P(),
        ),
        out_specs=(P(("row", "col"), None, None, None), P(("row", "col"), None, None, None)),
        check_vma=False,
    )
```

profile of v0, /device:TPU:30, one launch (start us, length us, event | category | flops | bytes accessed | tf_op | source)
XLA Modules:
  0.0 391.8 jit_solution(11788214970546222981)
XLA Ops:
  9.0 4.1 %collective-permute-start.1 = (bf16[4,8,128,128]{3,1,2,0:T(8,128)(2,1)S(1)}, bf16[4,8,128,128]{3,1,2,0:T(8,128)(2,1)}, u32[]{:S(2)}, u32[]{:S(2)}) collective-permute-start(bf16[4,8,128,128]{3,1,2,0:T(8,128)(2,1)S(1)} %get-tuple-element.13), channel_id=1, source_target_pairs={{0,127},{1,0},{2,1},{3,2},{4,3},{5,4},{6,5},{7,6},{8,7},{9,8},{10,... | collective-permute-start | bytes 3145736 | tf_op jit(solution)/shard_map/ppermute | solution.py:14
  18.8 4.2 %collective-permute-start.21 = (s32[4,16]{1,0:T(4,128)S(1)}, s32[4,16]{1,0:T(4,128)S(1)}, u32[]{:S(2)}, u32[]{:S(2)}) collective-permute-start(s32[4,16]{1,0:T(4,128)S(1)} %copy-done.4), channel_id=1, source_target_pairs={{0,127},{1,0},{2,1},{3,2},{4,3},{5,4},{6,5},{7,6},{8,7},{9,8},{10,... | collective-permute-start | bytes 776 | tf_op jit(solution)/shard_map/ppermute | solution.py:14
  23.2 12.6 %collective-permute-done.19 = s32[4,16]{1,0:T(4,128)S(1)} collective-permute-done((s32[4,16]{1,0:T(4,128)}, s32[4,16]{1,0:T(4,128)S(1)}, u32[]{:S(2)}, u32[]{:S(2)}) %collective-permute-start.19) | collective-permute-done | bytes 288 | tf_op jit(solution)/shard_map/ppermute | solution.py:14
  42.0 7.9 %convolution_convert_fusion.2 = bf16[12,128,128,20]{2,3,1,0:T(8,128)(2,1)} fusion(bf16[4,8,128,128]{3,1,2,0:T(8,128)(2,1)} %collective-permute-done.1, bf16[4,8,128,128]{3,1,2,0:T(8,128)(2,1)S(1)} %get-tuple-element.13, bf16[4,8,128,128]{3,1,2,0:T(8,128)(2,1)} %collective-permute-done, s32[12,8]{1,0:T(8,128)S(1)} %copy.42), kind=kOutput, calls=%fused_computation.10 | convolution fusion | flops 69994368 | bytes 11010432 | tf_op jit(solution)/shard_map/rcs,rsyz->rycz/dot_general | solution.py:60
  50.0 8.7 %copy.98 = bf16[192,8,20,128]{3,1,2,0:T(8,128)(2,1)} copy(bf16[192,8,20,128]{3,2,1,0:T(8,128)(2,1)} %bitcast.97) | data formatting | bytes 15728640
  58.7 10.6 %copy.43 = bf16[2560,1536]{1,0:T(8,128)(2,1)} copy(bf16[2560,1536]{0,1:T(8,128)(2,1)} %bitcast.98) | data formatting | bytes 15728640 | tf_op jit(solution)/shard_map/dot_general | solution.py:67
  69.3 7.9 %fusion.37 = bf16[4,128,20,128]{1,3,2,0:T(8,128)(2,1)S(1)} fusion(bf16[4,128,1536,1]{1,2,3,0:T(8,128)(2,1)} %bitcast.104, bf16[20,128,1536,1]{2,1,0,3:T(8,128)(2,1)} %bitcast.101), kind=kOutput, calls=%fused_computation.70 | convolution fusion | flops 4026531840 | bytes 12058624 | tf_op jit(solution)/shard_map/dot_general | solution.py:67
  80.3 4.4 %collective-permute-start.15 = (bf16[4,8,128,128]{3,1,2,0:T(8,128)(2,1)}, bf16[4,8,128,128]{3,1,2,0:T(8,128)(2,1)}, u32[]{:S(2)}, u32[]{:S(2)}) collective-permute-start(bf16[4,8,128,128]{3,1,2,0:T(8,128)(2,1)} %collective-permute-done), channel_id=1, source_target_pairs={{0,1},{1,2},{2,3},{3,4},{4,5},{5,6},{6,7},{7,8},{8,9},{9,10},{10,1... | collective-permute-start | bytes 3145736 | tf_op jit(solution)/shard_map/ppermute | solution.py:14
  84.7 4.3 %multiply_reduce_fusion = (f32[]{:T(128)}, bf16[4,128,20,128]{3,2,1,0:T(8,128)(2,1)S(1)}) fusion(bf16[4,128,20,128]{3,2,1,0:T(8,128)(2,1)} %copy.45, pred[4,20]{1,0:T(4,128)(4,1)S(1)} %broadcast_compare_fusion), kind=kLoop, calls=%fused_computation.11 | loop fusion | flops 5242879 | bytes 5242964 | tf_op jit(solution)/shard_map/reduce_sum | solution.py:108
  98.3 3.6 copy.55
  117.0 46.8 %collective-permute-done.16 = bf16[4,8,128,128]{3,1,2,0:T(8,128)(2,1)S(1)} collective-permute-done((bf16[4,8,128,128]{3,1,2,0:T(8,128)(2,1)}, bf16[4,8,128,128]{3,1,2,0:T(8,128)(2,1)S(1)}, u32[]{:S(2)}, u32[]{:S(2)}) %collective-permute-start.16) | collective-permute-done | bytes 1048608 | tf_op jit(solution)/shard_map/ppermute | solution.py:14
  165.0 11.7 %convolution_convert_fusion.1 = bf16[20,128,128,28]{2,3,1,0:T(8,128)(2,1)} fusion(bf16[20,8,128,128]{3,1,2,0:T(8,128)(2,1)} %constant_dynamic-update-slice_fusion.5, s32[20,8]{1,0:T(8,128)S(1)} %copy.48), kind=kOutput, calls=%fused_computation.3 | convolution fusion | flops 155980160 | bytes 23593600 | tf_op jit(solution)/shard_map/rcs,rsyz->rycz/dot_general | solution.py:60
  176.7 19.5 %copy.97 = bf16[320,8,28,128]{3,1,2,0:T(8,128)(2,1)} copy(bf16[320,8,28,128]{3,2,1,0:T(8,128)(2,1)} %bitcast.93) | data formatting | bytes 36700160
  196.2 24.1 %copy.49 = bf16[3584,2560]{1,0:T(8,128)(2,1)} copy(bf16[3584,2560]{0,1:T(8,128)(2,1)} %bitcast.95) | data formatting | bytes 36700160 | tf_op jit(solution)/shard_map/dot_general | solution.py:67
  224.6 16.1 %fusion.38 = f32[4,128,28,128]{3,1,2,0:T(8,128)} fusion(bf16[4,128,2560,1]{1,2,3,0:T(8,128)(2,1)} %bitcast.102, bf16[28,128,2560,1]{2,1,0,3:T(8,128)(2,1)} %bitcast.99), kind=kOutput, calls=%fused_computation.71 | convolution fusion | flops 9395240960 | bytes 28311552 | tf_op jit(solution)/shard_map/dot_general | solution.py:67
  240.7 30.2 %collective-permute-done.5 = bf16[4,16,128,128]{3,1,2,0:T(8,128)(2,1)S(1)} collective-permute-done((bf16[4,16,128,128]{3,1,2,0:T(8,128)(2,1)}, bf16[4,16,128,128]{3,1,2,0:T(8,128)(2,1)S(1)}, u32[]{:S(2)}, u32[]{:S(2)}) %collective-permute-start.5) | collective-permute-done | bytes 2097184 | tf_op jit(solution)/shard_map/ppermute | solution.py:14
  278.4 9.9 %convolution_convert_fusion = bf16[20,128,128,28]{2,3,1,0:T(8,128)(2,1)} fusion(bf16[20,16,128,128]{3,1,2,0:T(8,128)(2,1)S(1)} %constant_dynamic-update-slice_fusion, s32[20,16]{1,0:T(8,128)S(1)} %add_add_fusion), kind=kOutput, calls=%fused_computation.2 | convolution fusion | flops 302785280 | bytes 28837120 | tf_op jit(solution)/shard_map/rcs,rsyz->rycz/dot_general | solution.py:60
  288.3 19.5 %copy.96 = bf16[320,8,28,128]{3,1,2,0:T(8,128)(2,1)} copy(bf16[320,8,28,128]{3,2,1,0:T(8,128)(2,1)} %bitcast.94) | data formatting | bytes 36700160
  307.8 24.1 %copy.52 = bf16[3584,2560]{1,0:T(8,128)(2,1)} copy(bf16[3584,2560]{0,1:T(8,128)(2,1)} %bitcast.96) | data formatting | bytes 36700160 | tf_op jit(solution)/shard_map/dot_general | solution.py:67
  331.9 16.2 %fusion.39 = f32[4,128,28,128]{3,1,2,0:T(8,128)} fusion(bf16[4,128,2560,1]{1,2,3,0:T(8,128)(2,1)} %bitcast.103, bf16[28,128,2560,1]{2,1,0,3:T(8,128)(2,1)} %bitcast.100), kind=kOutput, calls=%fused_computation.72 | convolution fusion | flops 9395240960 | bytes 28311552 | tf_op jit(solution)/shard_map/dot_general | solution.py:67
  348.8 4.7 %collective-permute-done.9 = f32[3]{0:T(128)S(1)} collective-permute-done((f32[3]{0:T(128)S(1)}, f32[3]{0:T(128)S(1)}, u32[]{:S(2)}, u32[]{:S(2)}) %collective-permute-start.9) | collective-permute-done | bytes 44 | tf_op jit(solution)/shard_map/ppermute | solution.py:46
  357.1 5.1 %collective-permute-done.11 = f32[3]{0:T(128)S(1)} collective-permute-done((f32[3]{0:T(128)S(1)}, f32[3]{0:T(128)S(1)}, u32[]{:S(2)}, u32[]{:S(2)}) %collective-permute-start.11) | collective-permute-done | bytes 44 | tf_op jit(solution)/shard_map/ppermute | solution.py:46
  366.9 5.1 %collective-permute-done.14 = f32[3]{0:T(128)S(1)} collective-permute-done((f32[3]{0:T(128)S(1)}, f32[3]{0:T(128)S(1)}, u32[]{:S(2)}, u32[]{:S(2)}) %collective-permute-start.14) | collective-permute-done | bytes 44 | tf_op jit(solution)/shard_map/ppermute | solution.py:46
  375.6 13.9 %fusion.10 = bf16[4,16,128,128]{3,1,2,0:T(8,128)(2,1)S(1)} fusion(f32[4,128,28,128]{3,1,2,0:T(8,128)} %fusion.39, f32[4,128,28,128]{3,1,2,0:T(8,128)} %fusion.38, bf16[4,128,20,128]{3,2,1,0:T(8,128)(2,1)S(1)} %get-tuple-element.15, f32[]{:T(128)} %bitcast.18, f32[]{:T(128)S(6)} %sub.46, f32[]{:T(128)S(6)} %sub.44, s32[4,16]{1,0:T(4,128)S(1)} %add_add_fusion.3), kind=kOutput, calls=%fused_computation.22 | convolution fusion | flops 72615680 | bytes 19398924 | tf_op jit(solution)/shard_map/rcs,rxcz->rsxz/dot_general | solution.py:75
  (92 shorter events, 71.6 us)
Async XLA Ops:
  1.4 17.4 %collective-permute-start.2 = (s32[4,8]{0,1:T(8,128)S(1)}, s32[4,8]{0,1:T(8,128)S(1)}, u32[]{:S(2)}, u32[]{:S(2)}) collective-permute-start(s32[4,8]{0,1:T(8,128)S(1)} %copy.39), channel_id=1, source_target_pairs={{0,1},{1,2},{2,3},{3,4},{4,5},{5,6},{6,7},{7,8},{8,9},{9,10},{10,1... | collective-permute-start | bytes 392 | tf_op jit(solution)/shard_map/ppermute | solution.py:14
  3.3 19.7 %collective-permute-start.3 = (s32[4,8]{0,1:T(8,128)S(1)}, s32[4,8]{0,1:T(8,128)S(1)}, u32[]{:S(2)}, u32[]{:S(2)}) collective-permute-start(s32[4,8]{0,1:T(8,128)S(1)} %copy.39), channel_id=1, source_target_pairs={{0,127},{1,0},{2,1},{3,2},{4,3},{5,4},{6,5},{7,6},{8,7},{9,8},{10,... | collective-permute-start | bytes 392 | tf_op jit(solution)/shard_map/ppermute | solution.py:14
  8.9 41.0 %copy-start.2 = (bf16[4,8,128,128]{3,1,2,0:T(8,128)(2,1)}, bf16[4,8,128,128]{3,1,2,0:T(8,128)(2,1)S(1)}, u32[]{:S(2)}) copy-start(bf16[4,8,128,128]{3,1,2,0:T(8,128)(2,1)S(1)} %get-tuple-element.13) | copy-start | bytes 3145732
  8.9 33.1 %collective-permute-start = (bf16[4,8,128,128]{3,1,2,0:T(8,128)(2,1)S(1)}, bf16[4,8,128,128]{3,1,2,0:T(8,128)(2,1)}, u32[]{:S(2)}, u32[]{:S(2)}) collective-permute-start(bf16[4,8,128,128]{3,1,2,0:T(8,128)(2,1)S(1)} %get-tuple-element.13), channel_id=1, source_target_pairs={{0,1},{1,2},{2,3},{3,4},{4,5},{5,6},{6,7},{7,8},{8,9},{9,10},{10,1... | collective-permute-start | bytes 3145736 | tf_op jit(solution)/shard_map/ppermute | solution.py:14
  9.0 33.1 %collective-permute-start.1 = (bf16[4,8,128,128]{3,1,2,0:T(8,128)(2,1)S(1)}, bf16[4,8,128,128]{3,1,2,0:T(8,128)(2,1)}, u32[]{:S(2)}, u32[]{:S(2)}) collective-permute-start(bf16[4,8,128,128]{3,1,2,0:T(8,128)(2,1)S(1)} %get-tuple-element.13), channel_id=1, source_target_pairs={{0,127},{1,0},{2,1},{3,2},{4,3},{5,4},{6,5},{7,6},{8,7},{9,8},{10,... | collective-permute-start | bytes 3145736 | tf_op jit(solution)/shard_map/ppermute | solution.py:14
  13.1 22.8 %collective-permute-start.19 = (s32[4,16]{1,0:T(4,128)}, s32[4,16]{1,0:T(4,128)S(1)}, u32[]{:S(2)}, u32[]{:S(2)}) collective-permute-start(s32[4,16]{1,0:T(4,128)} %param.9), channel_id=1, source_target_pairs={{0,1},{1,2},{2,3},{3,4},{4,5},{5,6},{6,7},{7,8},{8,9},{9,10},{10,1... | collective-permute-start | bytes 776 | tf_op jit(solution)/shard_map/ppermute | solution.py:14
  18.8 17.0 %collective-permute-start.21 = (s32[4,16]{1,0:T(4,128)S(1)}, s32[4,16]{1,0:T(4,128)S(1)}, u32[]{:S(2)}, u32[]{:S(2)}) collective-permute-start(s32[4,16]{1,0:T(4,128)S(1)} %copy-done.4), channel_id=1, source_target_pairs={{0,127},{1,0},{2,1},{3,2},{4,3},{5,4},{6,5},{7,6},{8,7},{9,8},{10,... | collective-permute-start | bytes 776 | tf_op jit(solution)/shard_map/ppermute | solution.py:14
  23.2 14.7 %collective-permute-start.17 = (s32[4,8]{0,1:T(8,128)S(1)}, s32[4,8]{0,1:T(8,128)S(1)}, u32[]{:S(2)}, u32[]{:S(2)}) collective-permute-start(s32[4,8]{0,1:T(8,128)S(1)} %collective-permute-done.2), channel_id=1, source_target_pairs={{0,1},{1,2},{2,3},{3,4},{4,5},{5,6},{6,7},{7,8},{8,9},{9,10},{10,1... | collective-permute-start | bytes 392 | tf_op jit(solution)/shard_map/ppermute | solution.py:14
  35.8 4.6 %collective-permute-start.18 = (s32[4,8]{0,1:T(8,128)S(1)}, s32[4,8]{0,1:T(8,128)S(1)}, u32[]{:S(2)}, u32[]{:S(2)}) collective-permute-start(s32[4,8]{0,1:T(8,128)S(1)} %collective-permute-done.3), channel_id=1, source_target_pairs={{0,127},{1,0},{2,1},{3,2},{4,3},{5,4},{6,5},{7,6},{8,7},{9,8},{10,... | collective-permute-start | bytes 392 | tf_op jit(solution)/shard_map/ppermute | solution.py:14
  35.9 5.7 %collective-permute-start.20 = (s32[4,16]{1,0:T(4,128)S(1)}, s32[4,16]{1,0:T(4,128)S(1)}, u32[]{:S(2)}, u32[]{:S(2)}) collective-permute-start(s32[4,16]{1,0:T(4,128)S(1)} %collective-permute-done.19), channel_id=1, source_target_pairs={{0,1},{1,2},{2,3},{3,4},{4,5},{5,6},{6,7},{7,8},{8,9},{9,10},{10,1... | collective-permute-start | bytes 776 | tf_op jit(solution)/shard_map/ppermute | solution.py:14
  37.9 4.0 %collective-permute-start.22 = (s32[4,16]{1,0:T(4,128)S(1)}, s32[4,16]{1,0:T(4,128)S(1)}, u32[]{:S(2)}, u32[]{:S(2)}) collective-permute-start(s32[4,16]{1,0:T(4,128)S(1)} %collective-permute-done.21), channel_id=1, source_target_pairs={{0,127},{1,0},{2,1},{3,2},{4,3},{5,4},{6,5},{7,6},{8,7},{9,8},{10,... | collective-permute-start | bytes 776 | tf_op jit(solution)/shard_map/ppermute | solution.py:14
  80.3 28.7 %collective-permute-start.15 = (bf16[4,8,128,128]{3,1,2,0:T(8,128)(2,1)}, bf16[4,8,128,128]{3,1,2,0:T(8,128)(2,1)}, u32[]{:S(2)}, u32[]{:S(2)}) collective-permute-start(bf16[4,8,128,128]{3,1,2,0:T(8,128)(2,1)} %collective-permute-done), channel_id=1, source_target_pairs={{0,1},{1,2},{2,3},{3,4},{4,5},{5,6},{6,7},{7,8},{8,9},{9,10},{10,1... | collective-permute-start | bytes 3145736 | tf_op jit(solution)/shard_map/ppermute | solution.py:14
  91.2 129.1 %collective-permute-start.4 = (bf16[4,16,128,128]{3,1,2,0:T(8,128)(2,1)}, bf16[4,16,128,128]{3,1,2,0:T(8,128)(2,1)}, u32[]{:S(2)}, u32[]{:S(2)}) collective-permute-start(bf16[4,16,128,128]{3,1,2,0:T(8,128)(2,1)} %convolution_convert_fusion.3), channel_id=1, source_target_pairs={{0,1},{1,2},{2,3},{3,4},{4,5},{5,6},{6,7},{7,8},{8,9},{9,10},{10,1... | collective-permute-start | bytes 6291464 | tf_op jit(solution)/shard_map/ppermute | solution.py:14
  93.2 129.3 %collective-permute-start.6 = (bf16[4,16,128,128]{3,1,2,0:T(8,128)(2,1)}, bf16[4,16,128,128]{3,1,2,0:T(8,128)(2,1)}, u32[]{:S(2)}, u32[]{:S(2)}) collective-permute-start(bf16[4,16,128,128]{3,1,2,0:T(8,128)(2,1)} %convolution_convert_fusion.3), channel_id=1, source_target_pairs={{0,127},{1,0},{2,1},{3,2},{4,3},{5,4},{6,5},{7,6},{8,7},{9,8},{10,... | collective-permute-start | bytes 6291464 | tf_op jit(solution)/shard_map/ppermute | solution.py:14
  101.9 61.9 %collective-permute-start.16 = (bf16[4,8,128,128]{3,1,2,0:T(8,128)(2,1)}, bf16[4,8,128,128]{3,1,2,0:T(8,128)(2,1)S(1)}, u32[]{:S(2)}, u32[]{:S(2)}) collective-permute-start(bf16[4,8,128,128]{3,1,2,0:T(8,128)(2,1)} %collective-permute-done.1), channel_id=1, source_target_pairs={{0,127},{1,0},{2,1},{3,2},{4,3},{5,4},{6,5},{7,6},{8,7},{9,8},{10,... | collective-permute-start | bytes 3145736 | tf_op jit(solution)/shard_map/ppermute | solution.py:14
  220.3 50.6 %collective-permute-start.5 = (bf16[4,16,128,128]{3,1,2,0:T(8,128)(2,1)}, bf16[4,16,128,128]{3,1,2,0:T(8,128)(2,1)S(1)}, u32[]{:S(2)}, u32[]{:S(2)}) collective-permute-start(bf16[4,16,128,128]{3,1,2,0:T(8,128)(2,1)} %collective-permute-done.4), channel_id=1, source_target_pairs={{0,1},{1,2},{2,3},{3,4},{4,5},{5,6},{6,7},{7,8},{8,9},{9,10},{10,1... | collective-permute-start | bytes 6291464 | tf_op jit(solution)/shard_map/ppermute | solution.py:14
  222.5 55.0 %collective-permute-start.7 = (bf16[4,16,128,128]{3,1,2,0:T(8,128)(2,1)}, bf16[4,16,128,128]{3,1,2,0:T(8,128)(2,1)S(1)}, u32[]{:S(2)}, u32[]{:S(2)}) collective-permute-start(bf16[4,16,128,128]{3,1,2,0:T(8,128)(2,1)} %collective-permute-done.6), channel_id=1, source_target_pairs={{0,127},{1,0},{2,1},{3,2},{4,3},{5,4},{6,5},{7,6},{8,7},{9,8},{10,... | collective-permute-start | bytes 6291464 | tf_op jit(solution)/shard_map/ppermute | solution.py:14
  278.0 70.1 %collective-permute-start.8 = (f32[3]{0:T(128)S(1)}, f32[3]{0:T(128)S(1)}, u32[]{:S(2)}, u32[]{:S(2)}) collective-permute-start(f32[3]{0:T(128)S(1)} %pad_maximum_fusion), channel_id=1, source_target_pairs={{0,1},{1,0},{2,3},{3,2},{4,5},{5,4},{6,7},{7,6},{8,9},{9,8},{10,11... | collective-permute-start | bytes 44 | tf_op jit(solution)/shard_map/ppermute | solution.py:46
  348.1 5.4 %collective-permute-start.9 = (f32[3]{0:T(128)S(1)}, f32[3]{0:T(128)S(1)}, u32[]{:S(2)}, u32[]{:S(2)}) collective-permute-start(f32[3]{0:T(128)S(1)} %add.160), channel_id=1, source_target_pairs={{0,2},{1,3},{2,0},{3,1},{4,6},{5,7},{6,4},{7,5},{8,10},{9,11},{10,... | collective-permute-start | bytes 44 | tf_op jit(solution)/shard_map/ppermute | solution.py:46
  353.5 3.6 collective-permute-start.10
  357.1 5.1 %collective-permute-start.11 = (f32[3]{0:T(128)S(1)}, f32[3]{0:T(128)S(1)}, u32[]{:S(2)}, u32[]{:S(2)}) collective-permute-start(f32[3]{0:T(128)S(1)} %add.162), channel_id=1, source_target_pairs={{0,8},{1,9},{2,10},{3,11},{4,12},{5,13},{6,14},{7,15},{8,0},{9,1},... | collective-permute-start | bytes 44 | tf_op jit(solution)/shard_map/ppermute | solution.py:46
  362.1 1.2 collective-permute-start.12
  363.3 3.6 collective-permute-start.13
  366.9 5.1 %collective-permute-start.14 = (f32[3]{0:T(128)S(1)}, f32[3]{0:T(128)S(1)}, u32[]{:S(2)}, u32[]{:S(2)}) collective-permute-start(f32[3]{0:T(128)S(1)} %add.165), channel_id=1, source_target_pairs={{0,64},{1,65},{2,66},{3,67},{4,68},{5,69},{6,70},{7,71},{8,72},{9,... | collective-permute-start | bytes 44 | tf_op jit(solution)/shard_map/ppermute | solution.py:46
  (5 other events, 85.7 us)
where the time goes:
time: 399 us; the launch traced here: 392 us
  local copies, waits for them, and re-layouts  139 us (35%)
  waiting for transfers between devices  117 us (29%)
  matrix products  86.5 us (22%)
  starting transfers between devices  31.1 us (8%)
  other arithmetic  13.4 us (3%)
  between operations  4.92 us (1%)
    ppermute x16, waiting for transfers between devices, passed_along(): return lax.ppermute(value, axis, pairs)  94 us
    unnamed x26, local copies, waits for them, and re-layouts  68.6 us
    dot_general x4, local copies, waits for them, and re-layouts, slab_matmul(): jnp.dot(left.reshape(r * b, k * b), right.reshape(k * b, n * b), preferre...  61.9 us
    dot_general x3, matrix products, slab_matmul(): jnp.dot(left.reshape(r * b, k * b), right.reshape(k * b, n * b), preferre...  40.2 us
    dot_general x4, matrix products, densify(): jnp.einsum('rcs,rsyz->rycz', onehot, blocks, preferred_element_type=F32)  30.3 us
    ppermute x16, starting transfers between devices, passed_along(): return lax.ppermute(value, axis, pairs)  30 us
    ppermute x7, waiting for transfers between devices, butterfly_sum(): value = value + lax.ppermute(value, axes, pairs)  23.2 us
    dot_general x2, matrix products, extract(): jnp.einsum('rcs,rxcz->rsxz', onehot, dense, preferred_element_type=F32)  16 us
  transfers between devices with their start and end apart: 23, of which 12 were waited for; matrix products, arithmetic and copies ran while one was open for 47% of the time, Pallas kernels for 0%

commit v1 on v0

--- a/solution.py
+++ b/solution.py
@@ -1,6 +1,8 @@
 import jax
 import jax.numpy as jnp
 from jax import lax
+from jax.experimental import pallas as pl
+from jax.experimental.pallas import tpu as pltpu
 from jax.sharding import PartitionSpec as P
 
 HALF = 4
@@ -61,6 +63,59 @@
     return dense.astype(BF16)
 
 
+def densify_transposed(blocks, columns, first_row, low, width):
+    count, slots, b, _ = blocks.shape
+    rows = jnp.arange(count, dtype=jnp.int32)[:, None] + first_row
+    place = rows + columns - low
+    valid = ((place >= 0) & (place < width)).astype(jnp.int32)
+    place = jnp.where(valid > 0, place, 0).astype(jnp.int32)
+
+    def kernel(place_ref, valid_ref, blocks_ref, out_ref):
+        def clear(c, carry):
+            start = pl.multiple_of(c * b, b)
+            out_ref[pl.ds(start, b), :] = jnp.zeros((b, count * b), out_ref.dtype)
+            return carry
+
+        lax.fori_loop(0, width, clear, 0)
+
+        def put(i, carry):
+            r = i // slots
+            s = i % slots
+
+            @pl.when(valid_ref[r, s] > 0)
+            def _():
+                top = pl.multiple_of(place_ref[r, s] * b, b)
+                left = pl.multiple_of(r * b, b)
+                block = blocks_ref[r, s].astype(F32).T.astype(out_ref.dtype)
+                out_ref[pl.ds(top, b), pl.ds(left, b)] = block
+
+            return carry
+
+        lax.fori_loop(0, count * slots, put, 0)
+
+    moved = blocks.size * 2 + width * b * count * b * 2
+    return pl.pallas_call(
+        kernel,
+        out_shape=jax.ShapeDtypeStruct((width * b, count * b), BF16),
+        in_specs=[
+            pl.BlockSpec(memory_space=pltpu.SMEM),
+            pl.BlockSpec(memory_space=pltpu.SMEM),
+            pl.BlockSpec(memory_space=pltpu.VMEM),
+        ],
+        out_specs=pl.BlockSpec(memory_space=pltpu.VMEM),
+        cost_estimate=pl.CostEstimate(flops=0, bytes_accessed=moved, transcendentals=0),
+    )(place, valid, blocks)
+
+
+def slab_matmul_nt(left, right_t):
+    r, b, k, _ = left.shape
+    n = right_t.shape[0] // b
+    out = lax.dot_general(
+        left.reshape(r * b, k * b), right_t, (((1,), (1,)), ((), ())), preferred_element_type=F32
+    )
+    return out.reshape(r, b, n, b)
+
+
 def slab_matmul(left, right):
     r, b, k, _ = left.shape
     n = right.shape[2]
@@ -88,16 +143,20 @@
 
     d_local = densify(masked, density_cols, 0, -HALF, rows_here + 2 * HALF)
     near = slice(margin - HALF, margin + rows_here + HALF)
-    d_near = densify(masked_wide[near], cols_wide[near], -HALF, -2 * HALF, rows_here + 4 * HALF)
-    square_dense = slab_matmul(d_local, d_near).astype(BF16)
+    d_near = densify_transposed(
+        masked_wide[near], cols_wide[near], -HALF, -2 * HALF, rows_here + 4 * HALF
+    )
+    square_dense = slab_matmul_nt(d_local, d_near).astype(BF16)
     pattern = jnp.max(place_onehot(0, rows_here, square_cols, -2 * HALF, rows_here + 4 * HALF), axis=2)
     s_local = jnp.where(pattern[:, None, :, None] > 0, square_dense, jnp.zeros_like(square_dense))
     square = extract(s_local, square_cols, -2 * HALF)
 
     square_wide, square_cols_wide = spread(square, square_cols, reach_devices)
     far = slice(margin - 2 * HALF, margin + rows_here + 2 * HALF)
-    d_far = densify(masked_wide[far], cols_wide[far], -2 * HALF, -3 * HALF, rows_here + 6 * HALF)
-    s_far = densify(
+    d_far = densify_transposed(
+        masked_wide[far], cols_wide[far], -2 * HALF, -3 * HALF, rows_here + 6 * HALF
+    )
+    s_far = densify_transposed(
         square_wide[far], square_cols_wide[far], -2 * HALF, -3 * HALF, rows_here + 6 * HALF
     )
 
@@ -112,8 +171,8 @@
     sums = butterfly_sum(local_sums, ("row", "col"))
     total_two, total_three, total_four = sums[0], sums[1], sums[2]
 
-    cube_dense = slab_matmul(s_local, d_far)
-    quartic_dense = slab_matmul(s_local, s_far)
+    cube_dense = slab_matmul_nt(s_local, d_far)
+    quartic_dense = slab_matmul_nt(s_local, s_far)
     gamma_mix = (target_trace[0] - 4.0 * total_three + 3.0 * total_four) / (
         total_two - 2.0 * total_three + total_four + 1e-06
     )

time: 399 us -> 365 us (0.915)
  the two profiles are of different devices: /device:TPU:30 before, /device:TPU:6 now
where the time goes in v1:
time: 365 us; the launch traced here: 359 us
  waiting for transfers between devices  94.6 us (26%)
  Pallas kernels  91.5 us (25%)
  matrix products  55.9 us (15%)
  starting transfers between devices  54.7 us (15%)
  local copies, waits for them, and re-layouts  35 us (10%)
  other arithmetic  21.8 us (6%)
  between operations  5.16 us (1%)
    pallas_call x3, Pallas kernels, densify_transposed(): pl.pallas_call(kernel, out_shape=jax.ShapeDtypeStruct((width * b, count *...  91.5 us
    ppermute x16, waiting for transfers between devices, passed_along(): return lax.ppermute(value, axis, pairs)  76 us
    ppermute x16, starting transfers between devices, passed_along(): return lax.ppermute(value, axis, pairs)  47.1 us
    dot_general x3, matrix products, slab_matmul_nt(): lax.dot_general(left.reshape(r * b, k * b), right_t, (((1,), (1,)), ((),...  40.2 us
    unnamed x25, local copies, waits for them, and re-layouts  21 us
    ppermute x7, waiting for transfers between devices, butterfly_sum(): value = value + lax.ppermute(value, axes, pairs)  18.6 us
    dot_general x2, matrix products, extract(): jnp.einsum('rcs,rxcz->rsxz', onehot, dense, preferred_element_type=F32)  14.7 us
    ppermute x7, starting transfers between devices, butterfly_sum(): value = value + lax.ppermute(value, axes, pairs)  7.6 us
  transfers between devices with their start and end apart: 23, of which 10 were waited for; matrix products, arithmetic and copies ran while one was open for 25% of the time, Pallas kernels for 26%

profile of v1, /device:TPU:6, one launch (start us, length us, event | category | flops | bytes accessed | tf_op | source)
XLA Modules:
  0.0 358.6 jit_solution(16605910476634523021)
XLA Ops:
  6.0 4.3 %collective-permute-start.3 = (bf16[4,8,128,128]{3,2,1,0:T(8,128)(2,1)S(1)}, bf16[4,8,128,128]{3,2,1,0:T(8,128)(2,1)}, u32[]{:S(2)}, u32[]{:S(2)}) collective-permute-start(bf16[4,8,128,128]{3,2,1,0:T(8,128)(2,1)S(1)} %get-tuple-element.13), channel_id=1, source_target_pairs={{0,127},{1,0},{2,1},{3,2},{4,3},{5,4},{6,5},{7,6},{8,7},{9,8},{10,... | collective-permute-start | bytes 3145736 | tf_op jit(solution)/shard_map/ppermute | solution.py:16
  10.2 6.0 %collective-permute-start.1 = (s32[4,8]{1,0:T(4,128)}, s32[4,8]{1,0:T(4,128)S(1)}, u32[]{:S(2)}, u32[]{:S(2)}) collective-permute-start(s32[4,8]{1,0:T(4,128)} %param.7), channel_id=1, source_target_pairs={{0,127},{1,0},{2,1},{3,2},{4,3},{5,4},{6,5},{7,6},{8,7},{9,8},{10,... | collective-permute-start | bytes 392 | tf_op jit(solution)/shard_map/ppermute | solution.py:16
  22.3 6.2 %collective-permute-done = s32[4,8]{1,0:T(4,128)S(1)} collective-permute-done((s32[4,8]{1,0:T(4,128)}, s32[4,8]{1,0:T(4,128)S(1)}, u32[]{:S(2)}, u32[]{:S(2)}) %collective-permute-start) | collective-permute-done | bytes 160 | tf_op jit(solution)/shard_map/ppermute | solution.py:16
  28.4 6.0 %collective-permute-start.21 = (s32[4,16]{1,0:T(4,128)S(1)}, s32[4,16]{1,0:T(4,128)S(1)}, u32[]{:S(2)}, u32[]{:S(2)}) collective-permute-start(s32[4,16]{1,0:T(4,128)S(1)} %copy-done.6), channel_id=1, source_target_pairs={{0,127},{1,0},{2,1},{3,2},{4,3},{5,4},{6,5},{7,6},{8,7},{9,8},{10,... | collective-permute-start | bytes 776 | tf_op jit(solution)/shard_map/ppermute | solution.py:16
  35.8 6.0 %collective-permute-start.16 = (s32[4,8]{1,0:T(4,128)S(1)}, s32[4,8]{1,0:T(4,128)S(1)}, u32[]{:S(2)}, u32[]{:S(2)}) collective-permute-start(s32[4,8]{1,0:T(4,128)S(1)} %collective-permute-done.1), channel_id=1, source_target_pairs={{0,127},{1,0},{2,1},{3,2},{4,3},{5,4},{6,5},{7,6},{8,7},{9,8},{10,... | collective-permute-start | bytes 392 | tf_op jit(solution)/shard_map/ppermute | solution.py:16
  43.0 4.9 %collective-permute-start.22 = (s32[4,16]{1,0:T(4,128)S(1)}, s32[4,16]{1,0:T(4,128)S(1)}, u32[]{:S(2)}, u32[]{:S(2)}) collective-permute-start(s32[4,16]{1,0:T(4,128)S(1)} %collective-permute-done.21), channel_id=1, source_target_pairs={{0,127},{1,0},{2,1},{3,2},{4,3},{5,4},{6,5},{7,6},{8,7},{9,8},{10,... | collective-permute-start | bytes 776 | tf_op jit(solution)/shard_map/ppermute | solution.py:16
  51.1 16.5 %shard_map.77 = bf16[2560,1536]{1,0:T(8,128)(2,1)} custom-call(s32[12,8]{1,0:T(8,128)} %compare_select_fusion.2.place_ref, s32[12,8]{1,0:T(8,128)} %and_convert_fusion.2.valid_ref, bf16[12,8,128,128]{3,2,1,0:T(8,128)(2,1)} %pad_maximum_fusion.blocks_ref), custom_call_target="tpu_custom_call" | custom-call | bytes 11010048 | tf_op jit(solution)/shard_map/pallas_call | solution.py:97
  67.6 7.9 %fusion.24 = bf16[4,128,20,128]{1,3,2,0:T(8,128)(2,1)S(1)} fusion(bf16[4,128,1536,1]{1,2,3,0:T(8,128)(2,1)} %bitcast.53, bf16[20,128,1536,1]{2,1,0,3:T(8,128)(2,1)} %bitcast.50), kind=kOutput, calls=%fused_computation.58 | convolution fusion | flops 4026531840 | bytes 12058624 | tf_op jit(solution)/shard_map/dot_general | solution.py:113
  78.6 4.3 %multiply_reduce_fusion = (f32[]{:T(128)}, bf16[4,128,20,128]{3,2,1,0:T(8,128)(2,1)S(1)}) fusion(bf16[4,128,20,128]{3,2,1,0:T(8,128)(2,1)} %copy.39, pred[4,20]{1,0:T(4,128)(4,1)S(1)} %broadcast_compare_fusion), kind=kLoop, calls=%fused_computation.5 | loop fusion | flops 5242879 | bytes 5242964 | tf_op jit(solution)/shard_map/reduce_sum | solution.py:167
  87.0 6.0 %collective-permute-start.6 = (bf16[4,16,128,128]{3,2,1,0:T(8,128)(2,1)}, bf16[4,16,128,128]{3,2,1,0:T(8,128)(2,1)}, u32[]{:S(2)}, u32[]{:S(2)}) collective-permute-start(bf16[4,16,128,128]{3,2,1,0:T(8,128)(2,1)} %copy.78), channel_id=1, source_target_pairs={{0,127},{1,0},{2,1},{3,2},{4,3},{5,4},{6,5},{7,6},{8,7},{9,8},{10,... | collective-permute-start | bytes 6291464 | tf_op jit(solution)/shard_map/ppermute | solution.py:16
  98.7 6.0 %collective-permute-start.18 = (bf16[4,8,128,128]{3,2,1,0:T(8,128)(2,1)}, bf16[4,8,128,128]{3,2,1,0:T(8,128)(2,1)S(1)}, u32[]{:S(2)}, u32[]{:S(2)}) collective-permute-start(bf16[4,8,128,128]{3,2,1,0:T(8,128)(2,1)} %collective-permute-done.3), channel_id=1, source_target_pairs={{0,127},{1,0},{2,1},{3,2},{4,3},{5,4},{6,5},{7,6},{8,7},{9,8},{10,... | collective-permute-start | bytes 3145736 | tf_op jit(solution)/shard_map/ppermute | solution.py:16
  104.6 3.4 multiply_reduce_fusion.1
  110.0 44.6 %collective-permute-done.17 = bf16[4,8,128,128]{3,2,1,0:T(8,128)(2,1)} collective-permute-done((bf16[4,8,128,128]{3,2,1,0:T(8,128)(2,1)}, bf16[4,8,128,128]{3,2,1,0:T(8,128)(2,1)}, u32[]{:S(2)}, u32[]{:S(2)}) %collective-permute-start.17) | collective-permute-done | bytes 1048608 | tf_op jit(solution)/shard_map/ppermute | solution.py:16
  163.7 28.4 %shard_map.78 = bf16[3584,2560]{1,0:T(8,128)(2,1)} custom-call(s32[20,8]{1,0:T(8,128)} %compare_select_fusion.1.place_ref, s32[20,8]{1,0:T(8,128)} %and_convert_fusion.1.valid_ref, bf16[20,8,128,128]{3,2,1,0:T(8,128)(2,1)} %constant_dynamic-update-slice_fusion.5.blocks_ref), custom_call_target="tpu_custom_call" | custom-call | bytes 23592960 | tf_op jit(solution)/shard_map/pallas_call | solution.py:97
  194.8 3.5 collective-permute-start.7
  198.3 16.2 %fusion.25 = f32[4,128,28,128]{3,1,2,0:T(8,128)} fusion(bf16[4,128,2560,1]{1,2,3,0:T(8,128)(2,1)} %bitcast.51, bf16[28,128,2560,1]{2,1,0,3:T(8,128)(2,1)} %bitcast.48), kind=kOutput, calls=%fused_computation.59 | convolution fusion | flops 9395240960 | bytes 28311552 | tf_op jit(solution)/shard_map/dot_general | solution.py:113
  214.4 23.9 %collective-permute-done.5 = bf16[4,16,128,128]{3,2,1,0:T(8,128)(2,1)S(1)} collective-permute-done((bf16[4,16,128,128]{3,2,1,0:T(8,128)(2,1)}, bf16[4,16,128,128]{3,2,1,0:T(8,128)(2,1)S(1)}, u32[]{:S(2)}, u32[]{:S(2)}) %collective-permute-start.5) | collective-permute-done | bytes 2097184 | tf_op jit(solution)/shard_map/ppermute | solution.py:16
  252.0 46.5 %shard_map.79 = bf16[3584,2560]{1,0:T(8,128)(2,1)} custom-call(s32[20,16]{1,0:T(8,128)} %compare_select_fusion.place_ref, s32[20,16]{1,0:T(8,128)} %and_convert_fusion.valid_ref, bf16[20,16,128,128]{3,2,1,0:T(8,128)(2,1)} %constant_dynamic-update-slice_fusion.blocks_ref), custom_call_target="tpu_custom_call" | custom-call | bytes 28835840 | tf_op jit(solution)/shard_map/pallas_call | solution.py:97
  298.5 16.1 %fusion.26 = f32[4,128,28,128]{3,1,2,0:T(8,128)} fusion(bf16[4,128,2560,1]{1,2,3,0:T(8,128)(2,1)} %bitcast.52, bf16[28,128,2560,1]{2,1,0,3:T(8,128)(2,1)} %bitcast.49), kind=kOutput, calls=%fused_computation.60 | convolution fusion | flops 9395240960 | bytes 28311552 | tf_op jit(solution)/shard_map/dot_general | solution.py:113
  315.8 4.0 %collective-permute-done.9 = f32[3]{0:T(128)S(1)} collective-permute-done((f32[3]{0:T(128)S(1)}, f32[3]{0:T(128)S(1)}, u32[]{:S(2)}, u32[]{:S(2)}) %collective-permute-start.9) | collective-permute-done | bytes 44 | tf_op jit(solution)/shard_map/ppermute | solution.py:48
  319.8 3.6 collective-permute-done.10
  324.7 3.7 %collective-permute-done.11 = f32[3]{0:T(128)S(1)} collective-permute-done((f32[3]{0:T(128)S(1)}, f32[3]{0:T(128)S(1)}, u32[]{:S(2)}, u32[]{:S(2)}) %collective-permute-start.11) | collective-permute-done | bytes 44 | tf_op jit(solution)/shard_map/ppermute | solution.py:48
  334.8 3.7 %collective-permute-done.14 = f32[3]{0:T(128)S(1)} collective-permute-done((f32[3]{0:T(128)S(1)}, f32[3]{0:T(128)S(1)}, u32[]{:S(2)}, u32[]{:S(2)}) %collective-permute-start.14) | collective-permute-done | bytes 44 | tf_op jit(solution)/shard_map/ppermute | solution.py:48
  342.4 13.9 %fusion.5 = bf16[4,16,128,128]{3,1,2,0:T(8,128)(2,1)S(1)} fusion(f32[4,128,28,128]{3,1,2,0:T(8,128)} %fusion.26, f32[4,128,28,128]{3,1,2,0:T(8,128)} %fusion.25, bf16[4,128,20,128]{3,2,1,0:T(8,128)(2,1)S(1)} %get-tuple-element.15, f32[]{:T(128)} %bitcast.14, f32[]{:T(128)S(6)} %sub.46, f32[]{:T(128)S(6)} %sub.44, s32[4,16]{1,0:T(4,128)S(1)} %add_add_fusion.3), kind=kOutput, calls=%fused_computation.13 | convolution fusion | flops 72615680 | bytes 19398924 | tf_op jit(solution)/shard_map/rcs,rxcz->rsxz/dot_general | solution.py:130
  (91 shorter events, 68.2 us)
Async XLA Ops:
  4.0 43.9 %collective-permute-start.2 = (bf16[4,8,128,128]{3,2,1,0:T(8,128)(2,1)S(1)}, bf16[4,8,128,128]{3,2,1,0:T(8,128)(2,1)}, u32[]{:S(2)}, u32[]{:S(2)}) collective-permute-start(bf16[4,8,128,128]{3,2,1,0:T(8,128)(2,1)S(1)} %get-tuple-element.13), channel_id=1, source_target_pairs={{0,1},{1,2},{2,3},{3,4},{4,5},{5,6},{6,7},{7,8},{8,9},{9,10},{10,1... | collective-permute-start | bytes 3145736 | tf_op jit(solution)/shard_map/ppermute | solution.py:16
  6.0 42.0 %collective-permute-start.3 = (bf16[4,8,128,128]{3,2,1,0:T(8,128)(2,1)S(1)}, bf16[4,8,128,128]{3,2,1,0:T(8,128)(2,1)}, u32[]{:S(2)}, u32[]{:S(2)}) collective-permute-start(bf16[4,8,128,128]{3,2,1,0:T(8,128)(2,1)S(1)} %get-tuple-element.13), channel_id=1, source_target_pairs={{0,127},{1,0},{2,1},{3,2},{4,3},{5,4},{6,5},{7,6},{8,7},{9,8},{10,... | collective-permute-start | bytes 3145736 | tf_op jit(solution)/shard_map/ppermute | solution.py:16
  10.2 18.2 %collective-permute-start = (s32[4,8]{1,0:T(4,128)}, s32[4,8]{1,0:T(4,128)S(1)}, u32[]{:S(2)}, u32[]{:S(2)}) collective-permute-start(s32[4,8]{1,0:T(4,128)} %param.7), channel_id=1, source_target_pairs={{0,1},{1,2},{2,3},{3,4},{4,5},{5,6},{6,7},{7,8},{8,9},{9,10},{10,1... | collective-permute-start | bytes 392 | tf_op jit(solution)/shard_map/ppermute | solution.py:16
  10.2 24.2 %collective-permute-start.1 = (s32[4,8]{1,0:T(4,128)}, s32[4,8]{1,0:T(4,128)S(1)}, u32[]{:S(2)}, u32[]{:S(2)}) collective-permute-start(s32[4,8]{1,0:T(4,128)} %param.7), channel_id=1, source_target_pairs={{0,127},{1,0},{2,1},{3,2},{4,3},{5,4},{6,5},{7,6},{8,7},{9,8},{10,... | collective-permute-start | bytes 392 | tf_op jit(solution)/shard_map/ppermute | solution.py:16
  16.2 19.6 %collective-permute-start.19 = (s32[4,16]{1,0:T(4,128)}, s32[4,16]{1,0:T(4,128)S(1)}, u32[]{:S(2)}, u32[]{:S(2)}) collective-permute-start(s32[4,16]{1,0:T(4,128)} %param.9), channel_id=1, source_target_pairs={{0,1},{1,2},{2,3},{3,4},{4,5},{5,6},{6,7},{7,8},{8,9},{9,10},{10,1... | collective-permute-start | bytes 776 | tf_op jit(solution)/shard_map/ppermute | solution.py:16
  28.4 13.3 %collective-permute-start.21 = (s32[4,16]{1,0:T(4,128)S(1)}, s32[4,16]{1,0:T(4,128)S(1)}, u32[]{:S(2)}, u32[]{:S(2)}) collective-permute-start(s32[4,16]{1,0:T(4,128)S(1)} %copy-done.6), channel_id=1, source_target_pairs={{0,127},{1,0},{2,1},{3,2},{4,3},{5,4},{6,5},{7,6},{8,7},{9,8},{10,... | collective-permute-start | bytes 776 | tf_op jit(solution)/shard_map/ppermute | solution.py:16
  35.8 7.2 %collective-permute-start.15 = (s32[4,8]{1,0:T(4,128)S(1)}, s32[4,8]{1,0:T(4,128)S(1)}, u32[]{:S(2)}, u32[]{:S(2)}) collective-permute-start(s32[4,8]{1,0:T(4,128)S(1)} %collective-permute-done), channel_id=1, source_target_pairs={{0,1},{1,2},{2,3},{3,4},{4,5},{5,6},{6,7},{7,8},{8,9},{9,10},{10,1... | collective-permute-start | bytes 392 | tf_op jit(solution)/shard_map/ppermute | solution.py:16
  35.8 12.1 %collective-permute-start.16 = (s32[4,8]{1,0:T(4,128)S(1)}, s32[4,8]{1,0:T(4,128)S(1)}, u32[]{:S(2)}, u32[]{:S(2)}) collective-permute-start(s32[4,8]{1,0:T(4,128)S(1)} %collective-permute-done.1), channel_id=1, source_target_pairs={{0,127},{1,0},{2,1},{3,2},{4,3},{5,4},{6,5},{7,6},{8,7},{9,8},{10,... | collective-permute-start | bytes 392 | tf_op jit(solution)/shard_map/ppermute | solution.py:16
  41.8 52.5 %collective-permute-start.20 = (s32[4,16]{1,0:T(4,128)S(1)}, s32[4,16]{1,0:T(4,128)S(1)}, u32[]{:S(2)}, u32[]{:S(2)}) collective-permute-start(s32[4,16]{1,0:T(4,128)S(1)} %collective-permute-done.19), channel_id=1, source_target_pairs={{0,1},{1,2},{2,3},{3,4},{4,5},{5,6},{6,7},{7,8},{8,9},{9,10},{10,1... | collective-permute-start | bytes 776 | tf_op jit(solution)/shard_map/ppermute | solution.py:16
  43.0 51.3 %collective-permute-start.22 = (s32[4,16]{1,0:T(4,128)S(1)}, s32[4,16]{1,0:T(4,128)S(1)}, u32[]{:S(2)}, u32[]{:S(2)}) collective-permute-start(s32[4,16]{1,0:T(4,128)S(1)} %collective-permute-done.21), channel_id=1, source_target_pairs={{0,127},{1,0},{2,1},{3,2},{4,3},{5,4},{6,5},{7,6},{8,7},{9,8},{10,... | collective-permute-start | bytes 776 | tf_op jit(solution)/shard_map/ppermute | solution.py:16
  87.0 105.2 %collective-permute-start.4 = (bf16[4,16,128,128]{3,2,1,0:T(8,128)(2,1)}, bf16[4,16,128,128]{3,2,1,0:T(8,128)(2,1)}, u32[]{:S(2)}, u32[]{:S(2)}) collective-permute-start(bf16[4,16,128,128]{3,2,1,0:T(8,128)(2,1)} %copy.78), channel_id=1, source_target_pairs={{0,1},{1,2},{2,3},{3,4},{4,5},{5,6},{6,7},{7,8},{8,9},{9,10},{10,1... | collective-permute-start | bytes 6291464 | tf_op jit(solution)/shard_map/ppermute | solution.py:16
  87.0 107.8 %collective-permute-start.6 = (bf16[4,16,128,128]{3,2,1,0:T(8,128)(2,1)}, bf16[4,16,128,128]{3,2,1,0:T(8,128)(2,1)}, u32[]{:S(2)}, u32[]{:S(2)}) collective-permute-start(bf16[4,16,128,128]{3,2,1,0:T(8,128)(2,1)} %copy.78), channel_id=1, source_target_pairs={{0,127},{1,0},{2,1},{3,2},{4,3},{5,4},{6,5},{7,6},{8,7},{9,8},{10,... | collective-permute-start | bytes 6291464 | tf_op jit(solution)/shard_map/ppermute | solution.py:16
  93.6 61.0 %collective-permute-start.17 = (bf16[4,8,128,128]{3,2,1,0:T(8,128)(2,1)}, bf16[4,8,128,128]{3,2,1,0:T(8,128)(2,1)}, u32[]{:S(2)}, u32[]{:S(2)}) collective-permute-start(bf16[4,8,128,128]{3,2,1,0:T(8,128)(2,1)} %collective-permute-done.2), channel_id=1, source_target_pairs={{0,1},{1,2},{2,3},{3,4},{4,5},{5,6},{6,7},{7,8},{8,9},{9,10},{10,1... | collective-permute-start | bytes 3145736 | tf_op jit(solution)/shard_map/ppermute | solution.py:16
  98.7 60.5 %copy-start.4 = (bf16[4,8,128,128]{3,2,1,0:T(8,128)(2,1)S(1)}, bf16[4,8,128,128]{3,2,1,0:T(8,128)(2,1)}, u32[]{:S(2)}) copy-start(bf16[4,8,128,128]{3,2,1,0:T(8,128)(2,1)} %copy-done.3) | copy-start | bytes 3145732
  98.7 63.9 %collective-permute-start.18 = (bf16[4,8,128,128]{3,2,1,0:T(8,128)(2,1)}, bf16[4,8,128,128]{3,2,1,0:T(8,128)(2,1)S(1)}, u32[]{:S(2)}, u32[]{:S(2)}) collective-permute-start(bf16[4,8,128,128]{3,2,1,0:T(8,128)(2,1)} %collective-permute-done.3), channel_id=1, source_target_pairs={{0,127},{1,0},{2,1},{3,2},{4,3},{5,4},{6,5},{7,6},{8,7},{9,8},{10,... | collective-permute-start | bytes 3145736 | tf_op jit(solution)/shard_map/ppermute | solution.py:16
  192.1 46.3 %collective-permute-start.5 = (bf16[4,16,128,128]{3,2,1,0:T(8,128)(2,1)}, bf16[4,16,128,128]{3,2,1,0:T(8,128)(2,1)S(1)}, u32[]{:S(2)}, u32[]{:S(2)}) collective-permute-start(bf16[4,16,128,128]{3,2,1,0:T(8,128)(2,1)} %collective-permute-done.4), channel_id=1, source_target_pairs={{0,1},{1,2},{2,3},{3,4},{4,5},{5,6},{6,7},{7,8},{8,9},{9,10},{10,1... | collective-permute-start | bytes 6291464 | tf_op jit(solution)/shard_map/ppermute | solution.py:16
  194.8 53.3 %collective-permute-start.7 = (bf16[4,16,128,128]{3,2,1,0:T(8,128)(2,1)}, bf16[4,16,128,128]{3,2,1,0:T(8,128)(2,1)S(1)}, u32[]{:S(2)}, u32[]{:S(2)}) collective-permute-start(bf16[4,16,128,128]{3,2,1,0:T(8,128)(2,1)} %collective-permute-done.6), channel_id=1, source_target_pairs={{0,127},{1,0},{2,1},{3,2},{4,3},{5,4},{6,5},{7,6},{8,7},{9,8},{10,... | collective-permute-start | bytes 6291464 | tf_op jit(solution)/shard_map/ppermute | solution.py:16
  249.6 65.0 %collective-permute-start.8 = (f32[3]{0:T(128)S(1)}, f32[3]{0:T(128)S(1)}, u32[]{:S(2)}, u32[]{:S(2)}) collective-permute-start(f32[3]{0:T(128)S(1)} %pad_maximum_fusion.1), channel_id=1, source_target_pairs={{0,1},{1,0},{2,3},{3,2},{4,5},{5,4},{6,7},{7,6},{8,9},{9,8},{10,11... | collective-permute-start | bytes 44 | tf_op jit(solution)/shard_map/ppermute | solution.py:48
  314.6 5.2 %collective-permute-start.9 = (f32[3]{0:T(128)S(1)}, f32[3]{0:T(128)S(1)}, u32[]{:S(2)}, u32[]{:S(2)}) collective-permute-start(f32[3]{0:T(128)S(1)} %add.138), channel_id=1, source_target_pairs={{0,2},{1,3},{2,0},{3,1},{4,6},{5,7},{6,4},{7,5},{8,10},{9,11},{10,... | collective-permute-start | bytes 44 | tf_op jit(solution)/shard_map/ppermute | solution.py:48
  319.8 3.6 collective-permute-start.10
  323.3 5.1 %collective-permute-start.11 = (f32[3]{0:T(128)S(1)}, f32[3]{0:T(128)S(1)}, u32[]{:S(2)}, u32[]{:S(2)}) collective-permute-start(f32[3]{0:T(128)S(1)} %add.140), channel_id=1, source_target_pairs={{0,8},{1,9},{2,10},{3,11},{4,12},{5,13},{6,14},{7,15},{8,0},{9,1},... | collective-permute-start | bytes 44 | tf_op jit(solution)/shard_map/ppermute | solution.py:48
  328.4 1.2 collective-permute-start.12
  329.6 3.6 collective-permute-start.13
  333.2 5.3 %collective-permute-start.14 = (f32[3]{0:T(128)S(1)}, f32[3]{0:T(128)S(1)}, u32[]{:S(2)}, u32[]{:S(2)}) collective-permute-start(f32[3]{0:T(128)S(1)} %add.143), channel_id=1, source_target_pairs={{0,64},{1,65},{2,66},{3,67},{4,68},{5,69},{6,70},{7,71},{8,72},{9,... | collective-permute-start | bytes 44 | tf_op jit(solution)/shard_map/ppermute | solution.py:48
  (7 other events, 208.5 us)

commit v2 on v1

--- a/solution.py
+++ b/solution.py
@@ -86,8 +86,7 @@
             def _():
                 top = pl.multiple_of(place_ref[r, s] * b, b)
                 left = pl.multiple_of(r * b, b)
-                block = blocks_ref[r, s].astype(F32).T.astype(out_ref.dtype)
-                out_ref[pl.ds(top, b), pl.ds(left, b)] = block
+                out_ref[pl.ds(top, b), pl.ds(left, b)] = blocks_ref[r, s]
 
             return carry
 
@@ -139,7 +138,7 @@
         jnp.arange(density_values.shape[1], dtype=jnp.int32)[None, :] < density_counts[:, None]
     )
     masked = jnp.where(is_live[:, :, None, None], density_values, jnp.zeros_like(density_values))
-    masked_wide, cols_wide = spread(masked, density_cols, reach_devices)
+    masked_wide, cols_wide = spread(jnp.swapaxes(masked, 2, 3), density_cols, reach_devices)
 
     d_local = densify(masked, density_cols, 0, -HALF, rows_here + 2 * HALF)
     near = slice(margin - HALF, margin + rows_here + HALF)
@@ -151,7 +150,7 @@
     s_local = jnp.where(pattern[:, None, :, None] > 0, square_dense, jnp.zeros_like(square_dense))
     square = extract(s_local, square_cols, -2 * HALF)
 
-    square_wide, square_cols_wide = spread(square, square_cols, reach_devices)
+    square_wide, square_cols_wide = spread(jnp.swapaxes(square, 2, 3), square_cols, reach_devices)
     far = slice(margin - 2 * HALF, margin + rows_here + 2 * HALF)
     d_far = densify_transposed(
         masked_wide[far], cols_wide[far], -2 * HALF, -3 * HALF, rows_here + 6 * HALF

time: 365 us -> 319 us (0.87)
  Pallas kernels: 91.5 us -> 43.7 us
  local copies, waits for them, and re-layouts: 35 us -> 43 us
    pallas_call x3, Pallas kernels: 91.5 us -> 43.7 us  [densify_transposed(): pl.pallas_call(kernel, out_shape=jax.ShapeDtypeStruct((width * b, count *...]
    ppermute x16, waiting for transfers between devices: 76 us -> 71 us  [passed_along(): return lax.ppermute(value, axis, pairs)]
    unnamed x25, local copies, waits for them, and re-layouts: 21 us -> 24.8 us
  transfers between devices with their start and end apart: 23 -> 23, of which waited for: 10 -> 12; matrix products, arithmetic and copies ran while one was open for 25% -> 31% of each run, Pallas kernels for 26% -> 14%
where the time goes in v2:
time: 319 us; the launch traced here: 314 us
  waiting for transfers between devices  92.6 us (29%)
  matrix products  58.3 us (18%)
  starting transfers between devices  51.9 us (16%)
  Pallas kernels  43.7 us (14%)
  local copies, waits for them, and re-layouts  43 us (13%)
  other arithmetic  19.1 us (6%)
  between operations  5.14 us (2%)
    ppermute x16, waiting for transfers between devices, passed_along(): return lax.ppermute(value, axis, pairs)  71 us
    ppermute x16, starting transfers between devices, passed_along(): return lax.ppermute(value, axis, pairs)  47.2 us
    pallas_call x3, Pallas kernels, densify_transposed(): pl.pallas_call(kernel, out_shape=jax.ShapeDtypeStruct((width * b, count *...  43.7 us
    dot_general x3, matrix products, slab_matmul_nt(): lax.dot_general(left.reshape(r * b, k * b), right_t, (((1,), (1,)), ((),...  40.2 us
    unnamed x25, local copies, waits for them, and re-layouts  24.8 us
    ppermute x7, waiting for transfers between devices, butterfly_sum(): value = value + lax.ppermute(value, axes, pairs)  21.5 us
    dot_general x2, matrix products, extract(): jnp.einsum('rcs,rxcz->rsxz', onehot, dense, preferred_element_type=F32)  16 us
  transfers between devices with their start and end apart: 23, of which 12 were waited for; matrix products, arithmetic and copies ran while one was open for 31% of the time, Pallas kernels for 14%

profile of v2, /device:TPU:6, one launch (start us, length us, event | category | flops | bytes accessed | tf_op | source)
XLA Modules:
  0.0 313.6 jit_solution(9604831737521450500)
XLA Ops:
  6.4 4.3 %collective-permute-start.3 = (bf16[4,8,128,128]{3,2,1,0:T(8,128)(2,1)S(1)}, bf16[4,8,128,128]{3,2,1,0:T(8,128)(2,1)}, u32[]{:S(2)}, u32[]{:S(2)}) collective-permute-start(bf16[4,8,128,128]{3,2,1,0:T(8,128)(2,1)S(1)} %bitcast.58), channel_id=1, source_target_pairs={{0,127},{1,0},{2,1},{3,2},{4,3},{5,4},{6,5},{7,6},{8,7},{9,8},{10,... | collective-permute-start | bytes 3145736 | tf_op jit(solution)/shard_map/ppermute | solution.py:16
  10.7 6.0 %collective-permute-start.1 = (s32[4,8]{1,0:T(4,128)}, s32[4,8]{1,0:T(4,128)S(1)}, u32[]{:S(2)}, u32[]{:S(2)}) collective-permute-start(s32[4,8]{1,0:T(4,128)} %param.7), channel_id=1, source_target_pairs={{0,127},{1,0},{2,1},{3,2},{4,3},{5,4},{6,5},{7,6},{8,7},{9,8},{10,... | collective-permute-start | bytes 392 | tf_op jit(solution)/shard_map/ppermute | solution.py:16
  23.9 5.1 %collective-permute-done = s32[4,8]{1,0:T(4,128)S(1)} collective-permute-done((s32[4,8]{1,0:T(4,128)}, s32[4,8]{1,0:T(4,128)S(1)}, u32[]{:S(2)}, u32[]{:S(2)}) %collective-permute-start) | collective-permute-done | bytes 160 | tf_op jit(solution)/shard_map/ppermute | solution.py:16
  32.8 3.4 %collective-permute-start.16 = (s32[4,8]{1,0:T(4,128)S(1)}, s32[4,8]{1,0:T(4,128)S(1)}, u32[]{:S(2)}, u32[]{:S(2)}) collective-permute-start(s32[4,8]{1,0:T(4,128)S(1)} %collective-permute-done.1), channel_id=1, source_target_pairs={{0,127},{1,0},{2,1},{3,2},{4,3},{5,4},{6,5},{7,6},{8,7},{9,8},{10,... | collective-permute-start | bytes 392 | tf_op jit(solution)/shard_map/ppermute | solution.py:16
  41.1 8.3 %shard_map.77 = bf16[2560,1536]{1,0:T(8,128)(2,1)} custom-call(s32[12,8]{1,0:T(8,128)} %compare_select_fusion.2.place_ref, s32[12,8]{1,0:T(8,128)} %and_convert_fusion.2.valid_ref, bf16[12,8,128,128]{3,2,1,0:T(8,128)(2,1)} %pad_maximum_fusion.blocks_ref), custom_call_target="tpu_custom_call" | custom-call | bytes 11010048 | tf_op jit(solution)/shard_map/pallas_call | solution.py:96
  49.4 7.9 %fusion.23 = bf16[4,128,20,128]{1,3,2,0:T(8,128)(2,1)S(1)} fusion(bf16[4,128,1536,1]{1,2,3,0:T(8,128)(2,1)} %bitcast.63, bf16[20,128,1536,1]{2,1,0,3:T(8,128)(2,1)} %bitcast.60), kind=kOutput, calls=%fused_computation.56 | convolution fusion | flops 4026531840 | bytes 12058624 | tf_op jit(solution)/shard_map/dot_general | solution.py:112
  60.4 4.2 %multiply_reduce_fusion = (f32[]{:T(128)}, bf16[4,128,20,128]{3,2,1,0:T(8,128)(2,1)S(1)}) fusion(bf16[4,128,20,128]{3,2,1,0:T(8,128)(2,1)} %copy.46, pred[4,20]{1,0:T(4,128)(4,1)S(1)} %broadcast_compare_fusion), kind=kLoop, calls=%fused_computation.5 | loop fusion | flops 5242879 | bytes 5242964 | tf_op jit(solution)/shard_map/reduce_sum | solution.py:166
  66.8 4.5 %copy.47 = bf16[4,16,128,128]{2,3,1,0:T(8,128)(2,1)} copy(bf16[4,16,128,128]{3,1,2,0:T(8,128)(2,1)} %fusion.10) | data formatting | bytes 4194304 | tf_op jit(solution)/shard_map/rcs,rxcz->rsxz/dot_general | solution.py:129
  71.8 5.4 %collective-permute-start.6 = (bf16[4,16,128,128]{3,2,1,0:T(8,128)(2,1)}, bf16[4,16,128,128]{3,2,1,0:T(8,128)(2,1)}, u32[]{:S(2)}, u32[]{:S(2)}) collective-permute-start(bf16[4,16,128,128]{3,2,1,0:T(8,128)(2,1)} %bitcast.54), channel_id=1, source_target_pairs={{0,127},{1,0},{2,1},{3,2},{4,3},{5,4},{6,5},{7,6},{8,7},{9,8},{10,... | collective-permute-start | bytes 6291464 | tf_op jit(solution)/shard_map/ppermute | solution.py:16
  77.9 6.0 %collective-permute-start.22 = (s32[4,16]{1,0:T(4,128)S(1)}, s32[4,16]{1,0:T(4,128)S(1)}, u32[]{:S(2)}, u32[]{:S(2)}) collective-permute-start(s32[4,16]{1,0:T(4,128)S(1)} %collective-permute-done.21), channel_id=1, source_target_pairs={{0,127},{1,0},{2,1},{3,2},{4,3},{5,4},{6,5},{7,6},{8,7},{9,8},{10,... | collective-permute-start | bytes 776 | tf_op jit(solution)/shard_map/ppermute | solution.py:16
  84.6 29.7 %collective-permute-done.20 = s32[4,16]{1,0:T(4,128)S(1)} collective-permute-done((s32[4,16]{1,0:T(4,128)S(1)}, s32[4,16]{1,0:T(4,128)S(1)}, u32[]{:S(2)}, u32[]{:S(2)}) %collective-permute-start.20) | collective-permute-done | bytes 288 | tf_op jit(solution)/shard_map/ppermute | solution.py:16
  121.5 3.9 %copy.53 = bf16[4,16,128,128]{3,2,1,0:T(8,128)(2,1)} copy(bf16[4,16,128,128]{2,3,1,0:T(8,128)(2,1)} %copy.47) | data formatting | bytes 4194304
  128.5 3.3 %multiply_reduce_fusion.1 = f32[]{:T(128)} fusion(bf16[4,128,12,128]{3,2,1,0:T(8,128)(2,1)} %copy-done, bf16[4,128,20,128]{3,2,1,0:T(8,128)(2,1)S(1)} %get-tuple-element.15), kind=kLoop, calls=%fused_computation.6 | loop fusion | flops 3145727 | bytes 3145732 | tf_op jit(solution)/shard_map/reduce_sum | solution.py:163
  147.2 14.7 %shard_map.78 = bf16[3584,2560]{1,0:T(8,128)(2,1)} custom-call(s32[20,8]{1,0:T(8,128)} %compare_select_fusion.1.place_ref, s32[20,8]{1,0:T(8,128)} %and_convert_fusion.1.valid_ref, bf16[20,8,128,128]{3,2,1,0:T(8,128)(2,1)} %constant_dynamic-update-slice_fusion.5.blocks_ref), custom_call_target="tpu_custom_call" | custom-call | bytes 23592960 | tf_op jit(solution)/shard_map/pallas_call | solution.py:96
  161.9 12.4 %collective-permute-start.5 = (bf16[4,16,128,128]{3,2,1,0:T(8,128)(2,1)}, bf16[4,16,128,128]{3,2,1,0:T(8,128)(2,1)S(1)}, u32[]{:S(2)}, u32[]{:S(2)}) collective-permute-start(bf16[4,16,128,128]{3,2,1,0:T(8,128)(2,1)} %collective-permute-done.4), channel_id=1, source_target_pairs={{0,1},{1,2},{2,3},{3,4},{4,5},{5,6},{6,7},{7,8},{8,9},{9,10},{10,1... | collective-permute-start | bytes 6291464 | tf_op jit(solution)/shard_map/ppermute | solution.py:16
  174.3 16.1 %fusion.24 = f32[4,128,28,128]{3,1,2,0:T(8,128)} fusion(bf16[4,128,2560,1]{1,2,3,0:T(8,128)(2,1)} %bitcast.61, bf16[28,128,2560,1]{2,1,0,3:T(8,128)(2,1)} %bitcast.55), kind=kOutput, calls=%fused_computation.57 | convolution fusion | flops 9395240960 | bytes 28311552 | tf_op jit(solution)/shard_map/dot_general | solution.py:112
  190.5 29.2 %collective-permute-done.5 = bf16[4,16,128,128]{3,2,1,0:T(8,128)(2,1)S(1)} collective-permute-done((bf16[4,16,128,128]{3,2,1,0:T(8,128)(2,1)}, bf16[4,16,128,128]{3,2,1,0:T(8,128)(2,1)S(1)}, u32[]{:S(2)}, u32[]{:S(2)}) %collective-permute-start.5) | collective-permute-done | bytes 2097184 | tf_op jit(solution)/shard_map/ppermute | solution.py:16
  232.8 20.7 %shard_map.79 = bf16[3584,2560]{1,0:T(8,128)(2,1)} custom-call(s32[20,16]{1,0:T(8,128)} %compare_select_fusion.place_ref, s32[20,16]{1,0:T(8,128)} %and_convert_fusion.valid_ref, bf16[20,16,128,128]{3,2,1,0:T(8,128)(2,1)} %constant_dynamic-update-slice_fusion.blocks_ref), custom_call_target="tpu_custom_call" | custom-call | bytes 28835840 | tf_op jit(solution)/shard_map/pallas_call | solution.py:96
  253.5 16.1 %fusion.25 = f32[4,128,28,128]{3,1,2,0:T(8,128)} fusion(bf16[4,128,2560,1]{1,2,3,0:T(8,128)(2,1)} %bitcast.62, bf16[28,128,2560,1]{2,1,0,3:T(8,128)(2,1)} %bitcast.56), kind=kOutput, calls=%fused_computation.58 | convolution fusion | flops 9395240960 | bytes 28311552 | tf_op jit(solution)/shard_map/dot_general | solution.py:112
  270.1 4.7 %collective-permute-done.9 = f32[3]{0:T(128)S(1)} collective-permute-done((f32[3]{0:T(128)S(1)}, f32[3]{0:T(128)S(1)}, u32[]{:S(2)}, u32[]{:S(2)}) %collective-permute-start.9) | collective-permute-done | bytes 44 | tf_op jit(solution)/shard_map/ppermute | solution.py:48
  274.8 3.6 %collective-permute-done.10 = f32[3]{0:T(128)S(1)} collective-permute-done((f32[3]{0:T(128)S(1)}, f32[3]{0:T(128)S(1)}, u32[]{:S(2)}, u32[]{:S(2)}) %collective-permute-start.10) | collective-permute-done | bytes 44 | tf_op jit(solution)/shard_map/ppermute | solution.py:48
  278.4 5.1 %collective-permute-done.11 = f32[3]{0:T(128)S(1)} collective-permute-done((f32[3]{0:T(128)S(1)}, f32[3]{0:T(128)S(1)}, u32[]{:S(2)}, u32[]{:S(2)}) %collective-permute-start.11) | collective-permute-done | bytes 44 | tf_op jit(solution)/shard_map/ppermute | solution.py:48
  289.5 4.0 %collective-permute-done.14 = f32[3]{0:T(128)S(1)} collective-permute-done((f32[3]{0:T(128)S(1)}, f32[3]{0:T(128)S(1)}, u32[]{:S(2)}, u32[]{:S(2)}) %collective-permute-start.14) | collective-permute-done | bytes 44 | tf_op jit(solution)/shard_map/ppermute | solution.py:48
  297.5 13.9 %fusion.5 = bf16[4,16,128,128]{3,1,2,0:T(8,128)(2,1)S(1)} fusion(f32[4,128,28,128]{3,1,2,0:T(8,128)} %fusion.25, f32[4,128,28,128]{3,1,2,0:T(8,128)} %fusion.24, bf16[4,128,20,128]{3,2,1,0:T(8,128)(2,1)S(1)} %get-tuple-element.15, f32[]{:T(128)} %bitcast.16, f32[]{:T(128)S(6)} %sub.46, f32[]{:T(128)S(6)} %sub.44, s32[4,16]{1,0:T(4,128)S(1)} %add_add_fusion.3), kind=kOutput, calls=%fused_computation.12 | convolution fusion | flops 72615680 | bytes 19398924 | tf_op jit(solution)/shard_map/rcs,rxcz->rsxz/dot_general | solution.py:129
  (92 shorter events, 75.9 us)
Async XLA Ops:
  4.5 36.6 %copy-start.2 = (bf16[4,8,128,128]{2,3,1,0:T(8,128)(2,1)}, bf16[4,8,128,128]{2,3,1,0:T(8,128)(2,1)S(1)}, u32[]{:S(2)}) copy-start(bf16[4,8,128,128]{2,3,1,0:T(8,128)(2,1)S(1)} %get-tuple-element.13) | copy-start | bytes 3145732
  4.5 33.4 %collective-permute-start.2 = (bf16[4,8,128,128]{3,2,1,0:T(8,128)(2,1)S(1)}, bf16[4,8,128,128]{3,2,1,0:T(8,128)(2,1)}, u32[]{:S(2)}, u32[]{:S(2)}) collective-permute-start(bf16[4,8,128,128]{3,2,1,0:T(8,128)(2,1)S(1)} %bitcast.57), channel_id=1, source_target_pairs={{0,1},{1,2},{2,3},{3,4},{4,5},{5,6},{6,7},{7,8},{8,9},{9,10},{10,1... | collective-permute-start | bytes 3145736 | tf_op jit(solution)/shard_map/ppermute | solution.py:16
  6.4 31.5 %collective-permute-start.3 = (bf16[4,8,128,128]{3,2,1,0:T(8,128)(2,1)S(1)}, bf16[4,8,128,128]{3,2,1,0:T(8,128)(2,1)}, u32[]{:S(2)}, u32[]{:S(2)}) collective-permute-start(bf16[4,8,128,128]{3,2,1,0:T(8,128)(2,1)S(1)} %bitcast.58), channel_id=1, source_target_pairs={{0,127},{1,0},{2,1},{3,2},{4,3},{5,4},{6,5},{7,6},{8,7},{9,8},{10,... | collective-permute-start | bytes 3145736 | tf_op jit(solution)/shard_map/ppermute | solution.py:16
  10.7 18.2 %collective-permute-start = (s32[4,8]{1,0:T(4,128)}, s32[4,8]{1,0:T(4,128)S(1)}, u32[]{:S(2)}, u32[]{:S(2)}) collective-permute-start(s32[4,8]{1,0:T(4,128)} %param.7), channel_id=1, source_target_pairs={{0,1},{1,2},{2,3},{3,4},{4,5},{5,6},{6,7},{7,8},{8,9},{9,10},{10,1... | collective-permute-start | bytes 392 | tf_op jit(solution)/shard_map/ppermute | solution.py:16
  10.7 20.8 %collective-permute-start.1 = (s32[4,8]{1,0:T(4,128)}, s32[4,8]{1,0:T(4,128)S(1)}, u32[]{:S(2)}, u32[]{:S(2)}) collective-permute-start(s32[4,8]{1,0:T(4,128)} %param.7), channel_id=1, source_target_pairs={{0,127},{1,0},{2,1},{3,2},{4,3},{5,4},{6,5},{7,6},{8,7},{9,8},{10,... | collective-permute-start | bytes 392 | tf_op jit(solution)/shard_map/ppermute | solution.py:16
  16.7 61.3 %collective-permute-start.19 = (s32[4,16]{1,0:T(4,128)}, s32[4,16]{1,0:T(4,128)S(1)}, u32[]{:S(2)}, u32[]{:S(2)}) collective-permute-start(s32[4,16]{1,0:T(4,128)} %param.9), channel_id=1, source_target_pairs={{0,1},{1,2},{2,3},{3,4},{4,5},{5,6},{6,7},{7,8},{8,9},{9,10},{10,1... | collective-permute-start | bytes 776 | tf_op jit(solution)/shard_map/ppermute | solution.py:16
  28.9 7.3 %collective-permute-start.15 = (s32[4,8]{1,0:T(4,128)S(1)}, s32[4,8]{1,0:T(4,128)S(1)}, u32[]{:S(2)}, u32[]{:S(2)}) collective-permute-start(s32[4,8]{1,0:T(4,128)S(1)} %collective-permute-done), channel_id=1, source_target_pairs={{0,1},{1,2},{2,3},{3,4},{4,5},{5,6},{6,7},{7,8},{8,9},{9,10},{10,1... | collective-permute-start | bytes 392 | tf_op jit(solution)/shard_map/ppermute | solution.py:16
  32.8 5.1 %collective-permute-start.16 = (s32[4,8]{1,0:T(4,128)S(1)}, s32[4,8]{1,0:T(4,128)S(1)}, u32[]{:S(2)}, u32[]{:S(2)}) collective-permute-start(s32[4,8]{1,0:T(4,128)S(1)} %collective-permute-done.1), channel_id=1, source_target_pairs={{0,127},{1,0},{2,1},{3,2},{4,3},{5,4},{6,5},{7,6},{8,7},{9,8},{10,... | collective-permute-start | bytes 392 | tf_op jit(solution)/shard_map/ppermute | solution.py:16
  36.3 41.7 %collective-permute-start.21 = (s32[4,16]{1,0:T(4,128)S(1)}, s32[4,16]{1,0:T(4,128)S(1)}, u32[]{:S(2)}, u32[]{:S(2)}) collective-permute-start(s32[4,16]{1,0:T(4,128)S(1)} %copy-done.5), channel_id=1, source_target_pairs={{0,127},{1,0},{2,1},{3,2},{4,3},{5,4},{6,5},{7,6},{8,7},{9,8},{10,... | collective-permute-start | bytes 776 | tf_op jit(solution)/shard_map/ppermute | solution.py:16
  71.3 90.6 %collective-permute-start.4 = (bf16[4,16,128,128]{3,2,1,0:T(8,128)(2,1)}, bf16[4,16,128,128]{3,2,1,0:T(8,128)(2,1)}, u32[]{:S(2)}, u32[]{:S(2)}) collective-permute-start(bf16[4,16,128,128]{3,2,1,0:T(8,128)(2,1)} %bitcast.53), channel_id=1, source_target_pairs={{0,1},{1,2},{2,3},{3,4},{4,5},{5,6},{6,7},{7,8},{8,9},{9,10},{10,1... | collective-permute-start | bytes 6291464 | tf_op jit(solution)/shard_map/ppermute | solution.py:16
  71.8 102.5 %collective-permute-start.6 = (bf16[4,16,128,128]{3,2,1,0:T(8,128)(2,1)}, bf16[4,16,128,128]{3,2,1,0:T(8,128)(2,1)}, u32[]{:S(2)}, u32[]{:S(2)}) collective-permute-start(bf16[4,16,128,128]{3,2,1,0:T(8,128)(2,1)} %bitcast.54), channel_id=1, source_target_pairs={{0,127},{1,0},{2,1},{3,2},{4,3},{5,4},{6,5},{7,6},{8,7},{9,8},{10,... | collective-permute-start | bytes 6291464 | tf_op jit(solution)/shard_map/ppermute | solution.py:16
  77.9 36.4 %collective-permute-start.20 = (s32[4,16]{1,0:T(4,128)S(1)}, s32[4,16]{1,0:T(4,128)S(1)}, u32[]{:S(2)}, u32[]{:S(2)}) collective-permute-start(s32[4,16]{1,0:T(4,128)S(1)} %collective-permute-done.19), channel_id=1, source_target_pairs={{0,1},{1,2},{2,3},{3,4},{4,5},{5,6},{6,7},{7,8},{8,9},{9,10},{10,1... | collective-permute-start | bytes 776 | tf_op jit(solution)/shard_map/ppermute | solution.py:16
  77.9 39.1 %collective-permute-start.22 = (s32[4,16]{1,0:T(4,128)S(1)}, s32[4,16]{1,0:T(4,128)S(1)}, u32[]{:S(2)}, u32[]{:S(2)}) collective-permute-start(s32[4,16]{1,0:T(4,128)S(1)} %collective-permute-done.21), channel_id=1, source_target_pairs={{0,127},{1,0},{2,1},{3,2},{4,3},{5,4},{6,5},{7,6},{8,7},{9,8},{10,... | collective-permute-start | bytes 776 | tf_op jit(solution)/shard_map/ppermute | solution.py:16
  83.9 52.9 %collective-permute-start.17 = (bf16[4,8,128,128]{3,2,1,0:T(8,128)(2,1)}, bf16[4,8,128,128]{3,2,1,0:T(8,128)(2,1)}, u32[]{:S(2)}, u32[]{:S(2)}) collective-permute-start(bf16[4,8,128,128]{3,2,1,0:T(8,128)(2,1)} %collective-permute-done.2), channel_id=1, source_target_pairs={{0,1},{1,2},{2,3},{3,4},{4,5},{5,6},{6,7},{7,8},{8,9},{9,10},{10,1... | collective-permute-start | bytes 3145736 | tf_op jit(solution)/shard_map/ppermute | solution.py:16
  125.4 20.7 %collective-permute-start.18 = (bf16[4,8,128,128]{3,2,1,0:T(8,128)(2,1)}, bf16[4,8,128,128]{3,2,1,0:T(8,128)(2,1)S(1)}, u32[]{:S(2)}, u32[]{:S(2)}) collective-permute-start(bf16[4,8,128,128]{3,2,1,0:T(8,128)(2,1)} %collective-permute-done.3), channel_id=1, source_target_pairs={{0,127},{1,0},{2,1},{3,2},{4,3},{5,4},{6,5},{7,6},{8,7},{9,8},{10,... | collective-permute-start | bytes 3145736 | tf_op jit(solution)/shard_map/ppermute | solution.py:16
  161.9 57.8 %collective-permute-start.5 = (bf16[4,16,128,128]{3,2,1,0:T(8,128)(2,1)}, bf16[4,16,128,128]{3,2,1,0:T(8,128)(2,1)S(1)}, u32[]{:S(2)}, u32[]{:S(2)}) collective-permute-start(bf16[4,16,128,128]{3,2,1,0:T(8,128)(2,1)} %collective-permute-done.4), channel_id=1, source_target_pairs={{0,1},{1,2},{2,3},{3,4},{4,5},{5,6},{6,7},{7,8},{8,9},{9,10},{10,1... | collective-permute-start | bytes 6291464 | tf_op jit(solution)/shard_map/ppermute | solution.py:16
  174.3 54.7 %collective-permute-start.7 = (bf16[4,16,128,128]{3,2,1,0:T(8,128)(2,1)}, bf16[4,16,128,128]{3,2,1,0:T(8,128)(2,1)S(1)}, u32[]{:S(2)}, u32[]{:S(2)}) collective-permute-start(bf16[4,16,128,128]{3,2,1,0:T(8,128)(2,1)} %collective-permute-done.6), channel_id=1, source_target_pairs={{0,127},{1,0},{2,1},{3,2},{4,3},{5,4},{6,5},{7,6},{8,7},{9,8},{10,... | collective-permute-start | bytes 6291464 | tf_op jit(solution)/shard_map/ppermute | solution.py:16
  230.4 39.2 %collective-permute-start.8 = (f32[3]{0:T(128)S(1)}, f32[3]{0:T(128)S(1)}, u32[]{:S(2)}, u32[]{:S(2)}) collective-permute-start(f32[3]{0:T(128)S(1)} %pad_maximum_fusion.1), channel_id=1, source_target_pairs={{0,1},{1,0},{2,3},{3,2},{4,5},{5,4},{6,7},{7,6},{8,9},{9,8},{10,11... | collective-permute-start | bytes 44 | tf_op jit(solution)/shard_map/ppermute | solution.py:48
  269.7 5.2 %collective-permute-start.9 = (f32[3]{0:T(128)S(1)}, f32[3]{0:T(128)S(1)}, u32[]{:S(2)}, u32[]{:S(2)}) collective-permute-start(f32[3]{0:T(128)S(1)} %add.138), channel_id=1, source_target_pairs={{0,2},{1,3},{2,0},{3,1},{4,6},{5,7},{6,4},{7,5},{8,10},{9,11},{10,... | collective-permute-start | bytes 44 | tf_op jit(solution)/shard_map/ppermute | solution.py:48
  274.8 3.6 %collective-permute-start.10 = (f32[3]{0:T(128)S(1)}, f32[3]{0:T(128)S(1)}, u32[]{:S(2)}, u32[]{:S(2)}) collective-permute-start(f32[3]{0:T(128)S(1)} %add.139), channel_id=1, source_target_pairs={{0,4},{1,5},{2,6},{3,7},{4,0},{5,1},{6,2},{7,3},{8,12},{9,13},{10,... | collective-permute-start | bytes 44 | tf_op jit(solution)/shard_map/ppermute | solution.py:48
  278.4 5.1 %collective-permute-start.11 = (f32[3]{0:T(128)S(1)}, f32[3]{0:T(128)S(1)}, u32[]{:S(2)}, u32[]{:S(2)}) collective-permute-start(f32[3]{0:T(128)S(1)} %add.140), channel_id=1, source_target_pairs={{0,8},{1,9},{2,10},{3,11},{4,12},{5,13},{6,14},{7,15},{8,0},{9,1},... | collective-permute-start | bytes 44 | tf_op jit(solution)/shard_map/ppermute | solution.py:48
  283.5 1.2 collective-permute-start.12
  284.6 3.6 %collective-permute-start.13 = (f32[3]{0:T(128)S(1)}, f32[3]{0:T(128)S(1)}, u32[]{:S(2)}, u32[]{:S(2)}) collective-permute-start(f32[3]{0:T(128)S(1)} %add.142), channel_id=1, source_target_pairs={{0,32},{1,33},{2,34},{3,35},{4,36},{5,37},{6,38},{7,39},{8,40},{9,... | collective-permute-start | bytes 44 | tf_op jit(solution)/shard_map/ppermute | solution.py:48
  288.2 5.3 %collective-permute-start.14 = (f32[3]{0:T(128)S(1)}, f32[3]{0:T(128)S(1)}, u32[]{:S(2)}, u32[]{:S(2)}) collective-permute-start(f32[3]{0:T(128)S(1)} %add.143), channel_id=1, source_target_pairs={{0,64},{1,65},{2,66},{3,67},{4,68},{5,69},{6,70},{7,71},{8,72},{9,... | collective-permute-start | bytes 44 | tf_op jit(solution)/shard_map/ppermute | solution.py:48
  (6 other events, 134.2 us)

commit v3 on v2

--- a/solution.py
+++ b/solution.py
@@ -130,6 +130,12 @@
     return picked.astype(BF16)
 
 
+def pick(dense, columns, low):
+    places = jnp.arange(dense.shape[0], dtype=jnp.int32)[:, None] + columns - low
+    picked = jnp.take_along_axis(dense, places[:, None, :, None], axis=2)
+    return jnp.transpose(picked, (0, 2, 1, 3))
+
+
 def shards(density_values, density_cols, density_counts, square_cols, update_cols, target_trace):
     rows_here = density_values.shape[0]
     reach_devices = (2 * HALF + rows_here - 1) // rows_here
@@ -175,13 +181,16 @@
     gamma_mix = (target_trace[0] - 4.0 * total_three + 3.0 * total_four) / (
         total_two - 2.0 * total_three + total_four + 1e-06
     )
-    carried = jnp.pad(s_local, ((0, 0), (0, 0), (HALF, HALF), (0, 0))).astype(F32)
-    purified_dense = (
-        (4.0 - 2.0 * gamma_mix) * cube_dense
-        + (gamma_mix - 3.0) * quartic_dense
+    carried = pick(
+        jnp.pad(s_local, ((0, 0), (0, 0), (HALF, HALF), (0, 0))), update_cols, -3 * HALF
+    ).astype(F32)
+    cube_part = pick(cube_dense, update_cols, -3 * HALF)
+    quartic_part = pick(quartic_dense, update_cols, -3 * HALF)
+    purified = (
+        (4.0 - 2.0 * gamma_mix) * cube_part
+        + (gamma_mix - 3.0) * quartic_part
         + gamma_mix * carried
     ).astype(BF16)
-    purified = extract(purified_dense, update_cols, -3 * HALF)
     return (square, purified)
 
 

time: 319 us -> 323 us (1.013); the launches traced: 314 us -> 322 us
  local copies, waits for them, and re-layouts: 43 us -> 67 us
  matrix products: 58.3 us -> 42.9 us
  other arithmetic: 19.1 us -> 24.6 us
  waiting for transfers between devices: 92.6 us -> 87.1 us
    gather x0 -> x5, local copies, waits for them, and re-layouts: none -> 16.2 us  [pick(): picked = jnp.take_along_axis(dense, places[:, None, :, None], axis=2)]
    dot_general x2 -> x1, matrix products: 16 us -> 2.13 us  [extract(): jnp.einsum('rcs,rxcz->rsxz', onehot, dense, preferred_element_type=F32)]
    ppermute x16, waiting for transfers between devices: 71 us -> 65.7 us  [passed_along(): return lax.ppermute(value, axis, pairs)]
    add x0 -> x1, other arithmetic: none -> 5.22 us  [shards(): (4.0 - 2.0 * gamma_mix) * cube_part + (gamma_mix - 3.0) * quartic_part]
    pad x0 -> x1, local copies, waits for them, and re-layouts: none -> 4.19 us  [shards(): jnp.pad(s_local, ((0, 0), (0, 0), (HALF, HALF), (0, 0)))]
    unnamed x25 -> x29, local copies, waits for them, and re-layouts: 24.8 us -> 26.8 us
  transfers between devices with their start and end apart: 23 -> 23, of which waited for: 12 -> 11; matrix products, arithmetic and copies ran while one was open for 31% -> 38% of each run, Pallas kernels for 14% -> 14%
where the time goes in v3:
time: 323 us; the launch traced here: 322 us
  waiting for transfers between devices  87.1 us (27%)
  local copies, waits for them, and re-layouts  67 us (21%)
  starting transfers between devices  51.6 us (16%)
  Pallas kernels  43.8 us (14%)
  matrix products  42.9 us (13%)
  other arithmetic  24.6 us (8%)
  between operations  4.66 us (1%)
    ppermute x16, waiting for transfers between devices, passed_along(): return lax.ppermute(value, axis, pairs)  65.7 us
    ppermute x16, starting transfers between devices, passed_along(): return lax.ppermute(value, axis, pairs)  46.9 us
    pallas_call x3, Pallas kernels, densify_transposed(): pl.pallas_call(kernel, out_shape=jax.ShapeDtypeStruct((width * b, count *...  43.8 us
    dot_general x3, matrix products, slab_matmul_nt(): lax.dot_general(left.reshape(r * b, k * b), right_t, (((1,), (1,)), ((),...  38.7 us
    unnamed x29, local copies, waits for them, and re-layouts  26.8 us
    ppermute x7, waiting for transfers between devices, butterfly_sum(): value = value + lax.ppermute(value, axes, pairs)  21.4 us
    gather x5, local copies, waits for them, and re-layouts, pick(): picked = jnp.take_along_axis(dense, places[:, None, :, None], axis=2)  16.2 us
  transfers between devices with their start and end apart: 23, of which 11 were waited for; matrix products, arithmetic and copies ran while one was open for 38% of the time, Pallas kernels for 14%

profile of v3, /device:TPU:6, one launch (start us, length us, event | category | flops | bytes accessed | tf_op | source)
XLA Modules:
  0.0 321.6 jit_solution(6150875811241139165)
XLA Ops:
  6.5 4.3 %collective-permute-start.3 = (bf16[4,8,128,128]{3,2,1,0:T(8,128)(2,1)S(1)}, bf16[4,8,128,128]{3,2,1,0:T(8,128)(2,1)}, u32[]{:S(2)}, u32[]{:S(2)}) collective-permute-start(bf16[4,8,128,128]{3,2,1,0:T(8,128)(2,1)S(1)} %bitcast.98), channel_id=1, source_target_pairs={{0,127},{1,0},{2,1},{3,2},{4,3},{5,4},{6,5},{7,6},{8,7},{9,8},{10,... | collective-permute-start | bytes 3145736 | tf_op jit(solution)/shard_map/ppermute | solution.py:16
  10.8 6.0 %collective-permute-start.1 = (s32[4,8]{1,0:T(4,128)S(1)}, s32[4,8]{1,0:T(4,128)S(1)}, u32[]{:S(2)}, u32[]{:S(2)}) collective-permute-start(s32[4,8]{1,0:T(4,128)S(1)} %copy-done.6), channel_id=1, source_target_pairs={{0,127},{1,0},{2,1},{3,2},{4,3},{5,4},{6,5},{7,6},{8,7},{9,8},{10,... | collective-permute-start | bytes 392 | tf_op jit(solution)/shard_map/ppermute | solution.py:16
  24.1 4.9 %collective-permute-done = s32[4,8]{1,0:T(4,128)S(1)} collective-permute-done((s32[4,8]{1,0:T(4,128)S(1)}, s32[4,8]{1,0:T(4,128)S(1)}, u32[]{:S(2)}, u32[]{:S(2)}) %collective-permute-start) | collective-permute-done | bytes 160 | tf_op jit(solution)/shard_map/ppermute | solution.py:16
  41.0 8.3 %shard_map.77 = bf16[2560,1536]{1,0:T(8,128)(2,1)} custom-call(s32[12,8]{1,0:T(8,128)} %compare_select_fusion.2.place_ref, s32[12,8]{1,0:T(8,128)} %and_convert_fusion.2.valid_ref, bf16[12,8,128,128]{3,2,1,0:T(8,128)(2,1)} %pad_maximum_fusion.blocks_ref), custom_call_target="tpu_custom_call" | custom-call | bytes 11010048 | tf_op jit(solution)/shard_map/pallas_call | solution.py:96
  49.3 7.9 %fusion.15 = bf16[4,128,20,128]{1,3,2,0:T(8,128)(2,1)S(1)} fusion(bf16[4,128,1536,1]{1,2,3,0:T(8,128)(2,1)} %bitcast.104, bf16[20,128,1536,1]{2,1,0,3:T(8,128)(2,1)} %bitcast.101), kind=kOutput, calls=%fused_computation.62 | convolution fusion | flops 4026531840 | bytes 12058624 | tf_op jit(solution)/shard_map/dot_general | solution.py:112
  60.3 4.3 %multiply_reduce_fusion = (f32[]{:T(128)}, bf16[4,128,20,128]{3,2,1,0:T(8,128)(2,1)S(1)}) fusion(bf16[4,128,20,128]{3,2,1,0:T(8,128)(2,1)} %copy.46, pred[4,20]{1,0:T(4,128)(4,1)S(1)} %broadcast_compare_fusion), kind=kLoop, calls=%fused_computation.3 | loop fusion | flops 5242879 | bytes 5242964 | tf_op jit(solution)/shard_map/reduce_sum | solution.py:172
  66.8 4.5 %copy.47 = bf16[4,16,128,128]{2,3,1,0:T(8,128)(2,1)} copy(bf16[4,16,128,128]{3,1,2,0:T(8,128)(2,1)} %fusion.5) | data formatting | bytes 4194304 | tf_op jit(solution)/shard_map/rcs,rxcz->rsxz/dot_general | solution.py:129
  71.9 5.4 %collective-permute-start.6 = (bf16[4,16,128,128]{3,2,1,0:T(8,128)(2,1)}, bf16[4,16,128,128]{3,2,1,0:T(8,128)(2,1)}, u32[]{:S(2)}, u32[]{:S(2)}) collective-permute-start(bf16[4,16,128,128]{3,2,1,0:T(8,128)(2,1)} %bitcast.92), channel_id=1, source_target_pairs={{0,127},{1,0},{2,1},{3,2},{4,3},{5,4},{6,5},{7,6},{8,7},{9,8},{10,... | collective-permute-start | bytes 6291464 | tf_op jit(solution)/shard_map/ppermute | solution.py:16
  78.0 6.0 %collective-permute-start.22 = (s32[4,16]{1,0:T(4,128)S(1)}, s32[4,16]{1,0:T(4,128)S(1)}, u32[]{:S(2)}, u32[]{:S(2)}) collective-permute-start(s32[4,16]{1,0:T(4,128)S(1)} %collective-permute-done.21), channel_id=1, source_target_pairs={{0,127},{1,0},{2,1},{3,2},{4,3},{5,4},{6,5},{7,6},{8,7},{9,8},{10,... | collective-permute-start | bytes 776 | tf_op jit(solution)/shard_map/ppermute | solution.py:16
  84.6 29.8 %collective-permute-done.20 = s32[4,16]{1,0:T(4,128)S(1)} collective-permute-done((s32[4,16]{1,0:T(4,128)S(1)}, s32[4,16]{1,0:T(4,128)S(1)}, u32[]{:S(2)}, u32[]{:S(2)}) %collective-permute-start.20) | collective-permute-done | bytes 288 | tf_op jit(solution)/shard_map/ppermute | solution.py:16
  127.7 4.2 %pad.4.clone = bf16[4,128,28,128]{3,1,2,0:T(8,128)(2,1)} pad(bf16[4,128,20,128]{3,1,2,0:T(8,128)(2,1)} %copy.64, bf16[]{:T(256)} %constant.20.clone.1), padding=0_0x0_0x4_4x0_0 | pad | bytes 6291458 | tf_op jit(solution)/shard_map/jit(_pad)/pad | solution.py:185
  131.9 4.2 %gather_fusion = bf16[64,128,128]{2,1,0:T(8,128)(2,1)} fusion(bf16[4,128,28,128]{3,1,2,0:T(8,128)(2,1)} %pad.4.clone, s32[64]{0:T(128)S(1)} %reshape.127), kind=kCustom, calls=%fused_computation.2 | custom fusion | bytes 4194816 | tf_op jit(solution)/shard_map/jit(take_along_axis)/gather | solution.py:135
  152.5 3.9 %collective-permute-done.18 = bf16[4,8,128,128]{3,2,1,0:T(8,128)(2,1)S(1)} collective-permute-done((bf16[4,8,128,128]{3,2,1,0:T(8,128)(2,1)}, bf16[4,8,128,128]{3,2,1,0:T(8,128)(2,1)S(1)}, u32[]{:S(2)}, u32[]{:S(2)}) %collective-permute-start.18) | collective-permute-done | bytes 1048608 | tf_op jit(solution)/shard_map/ppermute | solution.py:16
  157.5 14.8 %shard_map.78 = bf16[3584,2560]{1,0:T(8,128)(2,1)} custom-call(s32[20,8]{1,0:T(8,128)} %compare_select_fusion.1.place_ref, s32[20,8]{1,0:T(8,128)} %and_convert_fusion.1.valid_ref, bf16[20,8,128,128]{3,2,1,0:T(8,128)(2,1)} %constant_dynamic-update-slice_fusion.5.blocks_ref), custom_call_target="tpu_custom_call" | custom-call | bytes 23592960 | tf_op jit(solution)/shard_map/pallas_call | solution.py:96
  172.4 12.4 %collective-permute-start.5 = (bf16[4,16,128,128]{3,2,1,0:T(8,128)(2,1)}, bf16[4,16,128,128]{3,2,1,0:T(8,128)(2,1)}, u32[]{:S(2)}, u32[]{:S(2)}) collective-permute-start(bf16[4,16,128,128]{3,2,1,0:T(8,128)(2,1)} %collective-permute-done.4), channel_id=1, source_target_pairs={{0,1},{1,2},{2,3},{3,4},{4,5},{5,6},{6,7},{7,8},{8,9},{9,10},{10,1... | collective-permute-start | bytes 6291464 | tf_op jit(solution)/shard_map/ppermute | solution.py:16
  184.8 15.4 %fusion.16 = f32[4,128,28,128]{3,1,2,0:T(8,128)} fusion(bf16[4,128,2560,1]{1,2,3,0:T(8,128)(2,1)S(1)} %bitcast.102, bf16[28,128,2560,1]{2,1,0,3:T(8,128)(2,1)} %bitcast.93), kind=kOutput, calls=%fused_computation.63 | convolution fusion | flops 9395240960 | bytes 28311552 | tf_op jit(solution)/shard_map/dot_general | solution.py:112
  200.2 5.8 %gather_fusion.1 = f32[64,128,128]{2,1,0:T(8,128)} fusion(f32[4,128,28,128]{3,1,2,0:T(8,128)} %fusion.16, s32[64]{0:T(128)S(1)} %reshape.149), kind=kCustom, calls=%fused_computation.clone | custom fusion | bytes 8389120 | tf_op jit(solution)/shard_map/jit(take_along_axis)/gather | solution.py:135
  206.0 24.3 %collective-permute-done.5 = bf16[4,16,128,128]{3,2,1,0:T(8,128)(2,1)} collective-permute-done((bf16[4,16,128,128]{3,2,1,0:T(8,128)(2,1)}, bf16[4,16,128,128]{3,2,1,0:T(8,128)(2,1)}, u32[]{:S(2)}, u32[]{:S(2)}) %collective-permute-start.5) | collective-permute-done | bytes 2097184 | tf_op jit(solution)/shard_map/ppermute | solution.py:16
  246.9 20.7 %shard_map.79 = bf16[3584,2560]{1,0:T(8,128)(2,1)} custom-call(s32[20,16]{1,0:T(8,128)} %compare_select_fusion.place_ref, s32[20,16]{1,0:T(8,128)} %and_convert_fusion.valid_ref, bf16[20,16,128,128]{3,2,1,0:T(8,128)(2,1)} %constant_dynamic-update-slice_fusion.blocks_ref), custom_call_target="tpu_custom_call" | custom-call | bytes 28835840 | tf_op jit(solution)/shard_map/pallas_call | solution.py:96
  267.6 15.4 %fusion.17 = f32[4,128,28,128]{3,1,2,0:T(8,128)} fusion(bf16[4,128,2560,1]{1,2,3,0:T(8,128)(2,1)S(1)} %bitcast.103, bf16[28,128,2560,1]{2,1,0,3:T(8,128)(2,1)} %bitcast.94), kind=kOutput, calls=%fused_computation.64 | convolution fusion | flops 9395240960 | bytes 28311552 | tf_op jit(solution)/shard_map/dot_general | solution.py:112
  283.0 6.0 %gather_fusion.2 = f32[64,128,128]{2,1,0:T(8,128)} fusion(f32[4,128,28,128]{3,1,2,0:T(8,128)} %fusion.17, s32[64]{0:T(128)S(1)} %reshape.149), kind=kCustom, calls=%fused_computation.1.clone | custom fusion | bytes 8389120 | tf_op jit(solution)/shard_map/jit(take_along_axis)/gather | solution.py:135
  289.3 4.7 %collective-permute-done.9 = f32[3]{0:T(128)S(1)} collective-permute-done((f32[3]{0:T(128)S(1)}, f32[3]{0:T(128)S(1)}, u32[]{:S(2)}, u32[]{:S(2)}) %collective-permute-start.9) | collective-permute-done | bytes 44 | tf_op jit(solution)/shard_map/ppermute | solution.py:48
  297.6 5.1 %collective-permute-done.11 = f32[3]{0:T(128)S(1)} collective-permute-done((f32[3]{0:T(128)S(1)}, f32[3]{0:T(128)S(1)}, u32[]{:S(2)}, u32[]{:S(2)}) %collective-permute-start.11) | collective-permute-done | bytes 44 | tf_op jit(solution)/shard_map/ppermute | solution.py:48
  316.4 5.2 %fusion.2 = bf16[4,16,128,128]{3,2,1,0:T(8,128)(2,1)} fusion(f32[4,16,128,128]{3,2,1,0:T(8,128)} %bitcast.96, f32[4,16,128,128]{3,2,1,0:T(8,128)} %bitcast.95, f32[]{:T(128)} %bitcast.14, bf16[4,16,128,128]{3,2,1,0:T(8,128)(2,1)S(1)} %bitcast.100, f32[]{:T(128)S(6)} %sub.47, f32[]{:T(128)S(6)} %sub.44, pred[4,16]{1,0:T(4,128)(4,1)S(1)} %and_bitcast_fusion, ...), kind=kLoop, calls=%fused_computation.12 | loop fusion | flops 10485760 | bytes 12583052 | tf_op jit(solution)/shard_map/add | solution.py:190
  (104 shorter events, 93.4 us)
Async XLA Ops:
  4.5 33.3 %collective-permute-start.2 = (bf16[4,8,128,128]{3,2,1,0:T(8,128)(2,1)S(1)}, bf16[4,8,128,128]{3,2,1,0:T(8,128)(2,1)}, u32[]{:S(2)}, u32[]{:S(2)}) collective-permute-start(bf16[4,8,128,128]{3,2,1,0:T(8,128)(2,1)S(1)} %bitcast.97), channel_id=1, source_target_pairs={{0,1},{1,2},{2,3},{3,4},{4,5},{5,6},{6,7},{7,8},{8,9},{9,10},{10,1... | collective-permute-start | bytes 3145736 | tf_op jit(solution)/shard_map/ppermute | solution.py:16
  6.5 31.4 %collective-permute-start.3 = (bf16[4,8,128,128]{3,2,1,0:T(8,128)(2,1)S(1)}, bf16[4,8,128,128]{3,2,1,0:T(8,128)(2,1)}, u32[]{:S(2)}, u32[]{:S(2)}) collective-permute-start(bf16[4,8,128,128]{3,2,1,0:T(8,128)(2,1)S(1)} %bitcast.98), channel_id=1, source_target_pairs={{0,127},{1,0},{2,1},{3,2},{4,3},{5,4},{6,5},{7,6},{8,7},{9,8},{10,... | collective-permute-start | bytes 3145736 | tf_op jit(solution)/shard_map/ppermute | solution.py:16
  10.7 18.2 %collective-permute-start = (s32[4,8]{1,0:T(4,128)S(1)}, s32[4,8]{1,0:T(4,128)S(1)}, u32[]{:S(2)}, u32[]{:S(2)}) collective-permute-start(s32[4,8]{1,0:T(4,128)S(1)} %copy-done.6), channel_id=1, source_target_pairs={{0,1},{1,2},{2,3},{3,4},{4,5},{5,6},{6,7},{7,8},{8,9},{9,10},{10,1... | collective-permute-start | bytes 392 | tf_op jit(solution)/shard_map/ppermute | solution.py:16
  10.8 20.8 %collective-permute-start.1 = (s32[4,8]{1,0:T(4,128)S(1)}, s32[4,8]{1,0:T(4,128)S(1)}, u32[]{:S(2)}, u32[]{:S(2)}) collective-permute-start(s32[4,8]{1,0:T(4,128)S(1)} %copy-done.6), channel_id=1, source_target_pairs={{0,127},{1,0},{2,1},{3,2},{4,3},{5,4},{6,5},{7,6},{8,7},{9,8},{10,... | collective-permute-start | bytes 392 | tf_op jit(solution)/shard_map/ppermute | solution.py:16
  16.7 61.2 %collective-permute-start.19 = (s32[4,16]{1,0:T(4,128)S(1)}, s32[4,16]{1,0:T(4,128)S(1)}, u32[]{:S(2)}, u32[]{:S(2)}) collective-permute-start(s32[4,16]{1,0:T(4,128)S(1)} %copy-done.8), channel_id=1, source_target_pairs={{0,1},{1,2},{2,3},{3,4},{4,5},{5,6},{6,7},{7,8},{8,9},{9,10},{10,1... | collective-permute-start | bytes 776 | tf_op jit(solution)/shard_map/ppermute | solution.py:16
  29.0 7.3 %collective-permute-start.15 = (s32[4,8]{1,0:T(4,128)S(1)}, s32[4,8]{1,0:T(4,128)S(1)}, u32[]{:S(2)}, u32[]{:S(2)}) collective-permute-start(s32[4,8]{1,0:T(4,128)S(1)} %collective-permute-done), channel_id=1, source_target_pairs={{0,1},{1,2},{2,3},{3,4},{4,5},{5,6},{6,7},{7,8},{8,9},{9,10},{10,1... | collective-permute-start | bytes 392 | tf_op jit(solution)/shard_map/ppermute | solution.py:16
  32.9 4.9 %collective-permute-start.16 = (s32[4,8]{1,0:T(4,128)S(1)}, s32[4,8]{1,0:T(4,128)S(1)}, u32[]{:S(2)}, u32[]{:S(2)}) collective-permute-start(s32[4,8]{1,0:T(4,128)S(1)} %collective-permute-done.1), channel_id=1, source_target_pairs={{0,127},{1,0},{2,1},{3,2},{4,3},{5,4},{6,5},{7,6},{8,7},{9,8},{10,... | collective-permute-start | bytes 392 | tf_op jit(solution)/shard_map/ppermute | solution.py:16
  36.3 41.7 %collective-permute-start.21 = (s32[4,16]{1,0:T(4,128)S(1)}, s32[4,16]{1,0:T(4,128)S(1)}, u32[]{:S(2)}, u32[]{:S(2)}) collective-permute-start(s32[4,16]{1,0:T(4,128)S(1)} %copy-done.8), channel_id=1, source_target_pairs={{0,127},{1,0},{2,1},{3,2},{4,3},{5,4},{6,5},{7,6},{8,7},{9,8},{10,... | collective-permute-start | bytes 776 | tf_op jit(solution)/shard_map/ppermute | solution.py:16
  71.3 101.0 %collective-permute-start.4 = (bf16[4,16,128,128]{3,2,1,0:T(8,128)(2,1)}, bf16[4,16,128,128]{3,2,1,0:T(8,128)(2,1)}, u32[]{:S(2)}, u32[]{:S(2)}) collective-permute-start(bf16[4,16,128,128]{3,2,1,0:T(8,128)(2,1)} %bitcast.91), channel_id=1, source_target_pairs={{0,1},{1,2},{2,3},{3,4},{4,5},{5,6},{6,7},{7,8},{8,9},{9,10},{10,1... | collective-permute-start | bytes 6291464 | tf_op jit(solution)/shard_map/ppermute | solution.py:16
  71.9 112.9 %collective-permute-start.6 = (bf16[4,16,128,128]{3,2,1,0:T(8,128)(2,1)}, bf16[4,16,128,128]{3,2,1,0:T(8,128)(2,1)}, u32[]{:S(2)}, u32[]{:S(2)}) collective-permute-start(bf16[4,16,128,128]{3,2,1,0:T(8,128)(2,1)} %bitcast.92), channel_id=1, source_target_pairs={{0,127},{1,0},{2,1},{3,2},{4,3},{5,4},{6,5},{7,6},{8,7},{9,8},{10,... | collective-permute-start | bytes 6291464 | tf_op jit(solution)/shard_map/ppermute | solution.py:16
  78.0 36.5 %collective-permute-start.20 = (s32[4,16]{1,0:T(4,128)S(1)}, s32[4,16]{1,0:T(4,128)S(1)}, u32[]{:S(2)}, u32[]{:S(2)}) collective-permute-start(s32[4,16]{1,0:T(4,128)S(1)} %collective-permute-done.19), channel_id=1, source_target_pairs={{0,1},{1,2},{2,3},{3,4},{4,5},{5,6},{6,7},{7,8},{8,9},{9,10},{10,1... | collective-permute-start | bytes 776 | tf_op jit(solution)/shard_map/ppermute | solution.py:16
  78.0 39.2 %collective-permute-start.22 = (s32[4,16]{1,0:T(4,128)S(1)}, s32[4,16]{1,0:T(4,128)S(1)}, u32[]{:S(2)}, u32[]{:S(2)}) collective-permute-start(s32[4,16]{1,0:T(4,128)S(1)} %collective-permute-done.21), channel_id=1, source_target_pairs={{0,127},{1,0},{2,1},{3,2},{4,3},{5,4},{6,5},{7,6},{8,7},{9,8},{10,... | collective-permute-start | bytes 776 | tf_op jit(solution)/shard_map/ppermute | solution.py:16
  83.9 60.5 %collective-permute-start.17 = (bf16[4,8,128,128]{3,2,1,0:T(8,128)(2,1)}, bf16[4,8,128,128]{3,2,1,0:T(8,128)(2,1)}, u32[]{:S(2)}, u32[]{:S(2)}) collective-permute-start(bf16[4,8,128,128]{3,2,1,0:T(8,128)(2,1)} %collective-permute-done.2), channel_id=1, source_target_pairs={{0,1},{1,2},{2,3},{3,4},{4,5},{5,6},{6,7},{7,8},{8,9},{9,10},{10,1... | collective-permute-start | bytes 3145736 | tf_op jit(solution)/shard_map/ppermute | solution.py:16
  136.1 20.4 %collective-permute-start.18 = (bf16[4,8,128,128]{3,2,1,0:T(8,128)(2,1)}, bf16[4,8,128,128]{3,2,1,0:T(8,128)(2,1)S(1)}, u32[]{:S(2)}, u32[]{:S(2)}) collective-permute-start(bf16[4,8,128,128]{3,2,1,0:T(8,128)(2,1)} %collective-permute-done.3), channel_id=1, source_target_pairs={{0,127},{1,0},{2,1},{3,2},{4,3},{5,4},{6,5},{7,6},{8,7},{9,8},{10,... | collective-permute-start | bytes 3145736 | tf_op jit(solution)/shard_map/ppermute | solution.py:16
  172.4 57.9 %collective-permute-start.5 = (bf16[4,16,128,128]{3,2,1,0:T(8,128)(2,1)}, bf16[4,16,128,128]{3,2,1,0:T(8,128)(2,1)}, u32[]{:S(2)}, u32[]{:S(2)}) collective-permute-start(bf16[4,16,128,128]{3,2,1,0:T(8,128)(2,1)} %collective-permute-done.4), channel_id=1, source_target_pairs={{0,1},{1,2},{2,3},{3,4},{4,5},{5,6},{6,7},{7,8},{8,9},{9,10},{10,1... | collective-permute-start | bytes 6291464 | tf_op jit(solution)/shard_map/ppermute | solution.py:16
  184.8 56.5 %collective-permute-start.7 = (bf16[4,16,128,128]{3,2,1,0:T(8,128)(2,1)}, bf16[4,16,128,128]{3,2,1,0:T(8,128)(2,1)}, u32[]{:S(2)}, u32[]{:S(2)}) collective-permute-start(bf16[4,16,128,128]{3,2,1,0:T(8,128)(2,1)} %collective-permute-done.6), channel_id=1, source_target_pairs={{0,127},{1,0},{2,1},{3,2},{4,3},{5,4},{6,5},{7,6},{8,7},{9,8},{10,... | collective-permute-start | bytes 6291464 | tf_op jit(solution)/shard_map/ppermute | solution.py:16
  244.4 44.5 %collective-permute-start.8 = (f32[3]{0:T(128)S(1)}, f32[3]{0:T(128)S(1)}, u32[]{:S(2)}, u32[]{:S(2)}) collective-permute-start(f32[3]{0:T(128)S(1)} %pad_maximum_fusion.1), channel_id=1, source_target_pairs={{0,1},{1,0},{2,3},{3,2},{4,5},{5,4},{6,7},{7,6},{8,9},{9,8},{10,11... | collective-permute-start | bytes 44 | tf_op jit(solution)/shard_map/ppermute | solution.py:48
  283.0 33.4 %copy-start.4 = (bf16[64,128,128]{2,1,0:T(8,128)(2,1)S(1)}, bf16[64,128,128]{2,1,0:T(8,128)(2,1)}, u32[]{:S(2)}) copy-start(bf16[64,128,128]{2,1,0:T(8,128)(2,1)} %gather_fusion) | copy-start | bytes 6291460
  289.0 5.1 %collective-permute-start.9 = (f32[3]{0:T(128)S(1)}, f32[3]{0:T(128)S(1)}, u32[]{:S(2)}, u32[]{:S(2)}) collective-permute-start(f32[3]{0:T(128)S(1)} %add.163), channel_id=1, source_target_pairs={{0,2},{1,3},{2,0},{3,1},{4,6},{5,7},{6,4},{7,5},{8,10},{9,11},{10,... | collective-permute-start | bytes 44 | tf_op jit(solution)/shard_map/ppermute | solution.py:48
  294.1 3.6 %collective-permute-start.10 = (f32[3]{0:T(128)S(1)}, f32[3]{0:T(128)S(1)}, u32[]{:S(2)}, u32[]{:S(2)}) collective-permute-start(f32[3]{0:T(128)S(1)} %add.164), channel_id=1, source_target_pairs={{0,4},{1,5},{2,6},{3,7},{4,0},{5,1},{6,2},{7,3},{8,12},{9,13},{10,... | collective-permute-start | bytes 44 | tf_op jit(solution)/shard_map/ppermute | solution.py:48
  297.6 5.1 %collective-permute-start.11 = (f32[3]{0:T(128)S(1)}, f32[3]{0:T(128)S(1)}, u32[]{:S(2)}, u32[]{:S(2)}) collective-permute-start(f32[3]{0:T(128)S(1)} %add.165), channel_id=1, source_target_pairs={{0,8},{1,9},{2,10},{3,11},{4,12},{5,13},{6,14},{7,15},{8,0},{9,1},... | collective-permute-start | bytes 44 | tf_op jit(solution)/shard_map/ppermute | solution.py:48
  302.7 1.2 collective-permute-start.12
  303.9 3.6 %collective-permute-start.13 = (f32[3]{0:T(128)S(1)}, f32[3]{0:T(128)S(1)}, u32[]{:S(2)}, u32[]{:S(2)}) collective-permute-start(f32[3]{0:T(128)S(1)} %add.167), channel_id=1, source_target_pairs={{0,32},{1,33},{2,34},{3,35},{4,36},{5,37},{6,38},{7,39},{8,40},{9,... | collective-permute-start | bytes 44 | tf_op jit(solution)/shard_map/ppermute | solution.py:48
  307.4 5.1 %collective-permute-start.14 = (f32[3]{0:T(128)S(1)}, f32[3]{0:T(128)S(1)}, u32[]{:S(2)}, u32[]{:S(2)}) collective-permute-start(f32[3]{0:T(128)S(1)} %add.168), channel_id=1, source_target_pairs={{0,64},{1,65},{2,66},{3,67},{4,68},{5,69},{6,70},{7,71},{8,72},{9,... | collective-permute-start | bytes 44 | tf_op jit(solution)/shard_map/ppermute | solution.py:48
  (8 other events, 168.6 us)

commit v4 on v3

--- a/solution.py
+++ b/solution.py
@@ -35,7 +35,8 @@
         for _ in range(reach_devices):
             carried = passed_along(carried, ("row", "col"), heading)
             arrivals.append(carried)
-    return assemble(earlier, (blocks, columns), later)
+    ordered = list(reversed(earlier)) + [(blocks, columns)] + later
+    return [part[0] for part in ordered], jnp.concatenate([part[1] for part in ordered], axis=0)
 
 
 def butterfly_sum(value, axes):
@@ -63,47 +64,57 @@
     return dense.astype(BF16)
 
 
-def densify_transposed(blocks, columns, first_row, low, width):
-    count, slots, b, _ = blocks.shape
+def densify_transposed(pieces, columns, first_row, low, width, row_range):
+    top_row, end_row = row_range
+    count = end_row - top_row
+    slots, b = pieces[0].shape[1], pieces[0].shape[2]
+    columns = columns[top_row:end_row]
     rows = jnp.arange(count, dtype=jnp.int32)[:, None] + first_row
     place = rows + columns - low
     valid = ((place >= 0) & (place < width)).astype(jnp.int32)
     place = jnp.where(valid > 0, place, 0).astype(jnp.int32)
-
-    def kernel(place_ref, valid_ref, blocks_ref, out_ref):
+    spans, used, offset = [], [], 0
+    for piece in pieces:
+        lo, hi = max(offset, top_row), min(offset + piece.shape[0], end_row)
+        if lo < hi:
+            spans.append((lo - offset, hi - lo, lo - top_row))
+            used.append(piece)
+        offset += piece.shape[0]
+
+    def kernel(place_ref, valid_ref, *refs):
+        out_ref = refs[-1]
+
         def clear(c, carry):
             start = pl.multiple_of(c * b, b)
             out_ref[pl.ds(start, b), :] = jnp.zeros((b, count * b), out_ref.dtype)
             return carry
 
         lax.fori_loop(0, width, clear, 0)
-
-        def put(i, carry):
-            r = i // slots
-            s = i % slots
-
-            @pl.when(valid_ref[r, s] > 0)
-            def _():
-                top = pl.multiple_of(place_ref[r, s] * b, b)
-                left = pl.multiple_of(r * b, b)
-                out_ref[pl.ds(top, b), pl.ds(left, b)] = blocks_ref[r, s]
-
-            return carry
-
-        lax.fori_loop(0, count * slots, put, 0)
-
-    moved = blocks.size * 2 + width * b * count * b * 2
+        for piece_ref, (skip, take, dest) in zip(refs[:-1], spans):
+
+            def put(i, carry, piece_ref=piece_ref, skip=skip, dest=dest):
+                r = i // slots
+                s = i % slots
+
+                @pl.when(valid_ref[dest + r, s] > 0)
+                def _():
+                    top = pl.multiple_of(place_ref[dest + r, s] * b, b)
+                    left = pl.multiple_of((dest + r) * b, b)
+                    out_ref[pl.ds(top, b), pl.ds(left, b)] = piece_ref[skip + r, s]
+
+                return carry
+
+            lax.fori_loop(0, take * slots, put, 0)
+
+    moved = sum(piece.size for piece in used) * 2 + width * b * count * b * 2
     return pl.pallas_call(
         kernel,
         out_shape=jax.ShapeDtypeStruct((width * b, count * b), BF16),
-        in_specs=[
-            pl.BlockSpec(memory_space=pltpu.SMEM),
-            pl.BlockSpec(memory_space=pltpu.SMEM),
-            pl.BlockSpec(memory_space=pltpu.VMEM),
-        ],
+        in_specs=[pl.BlockSpec(memory_space=pltpu.SMEM)] * 2
+        + [pl.BlockSpec(memory_space=pltpu.VMEM)] * len(used),
         out_specs=pl.BlockSpec(memory_space=pltpu.VMEM),
         cost_estimate=pl.CostEstimate(flops=0, bytes_accessed=moved, transcendentals=0),
-    )(place, valid, blocks)
+    )(place, valid, *used)
 
 
 def slab_matmul_nt(left, right_t):
@@ -149,7 +160,7 @@
     d_local = densify(masked, density_cols, 0, -HALF, rows_here + 2 * HALF)
     near = slice(margin - HALF, margin + rows_here + HALF)
     d_near = densify_transposed(
-        masked_wide[near], cols_wide[near], -HALF, -2 * HALF, rows_here + 4 * HALF
+        masked_wide, cols_wide, -HALF, -2 * HALF, rows_here + 4 * HALF, (near.start, near.stop)
     )
     square_dense = slab_matmul_nt(d_local, d_near).astype(BF16)
     pattern = jnp.max(place_onehot(0, rows_here, square_cols, -2 * HALF, rows_here + 4 * HALF), axis=2)
@@ -159,10 +170,15 @@
     square_wide, square_cols_wide = spread(jnp.swapaxes(square, 2, 3), square_cols, reach_devices)
     far = slice(margin - 2 * HALF, margin + rows_here + 2 * HALF)
     d_far = densify_transposed(
-        masked_wide[far], cols_wide[far], -2 * HALF, -3 * HALF, rows_here + 6 * HALF
+        masked_wide, cols_wide, -2 * HALF, -3 * HALF, rows_here + 6 * HALF, (far.start, far.stop)
     )
     s_far = densify_transposed(
-        square_wide[far], square_cols_wide[far], -2 * HALF, -3 * HALF, rows_here + 6 * HALF
+        square_wide,
+        square_cols_wide,
+        -2 * HALF,
+        -3 * HALF,
+        rows_here + 6 * HALF,
+        (far.start, far.stop),
     )
 
     trace_two = jnp.sum(jnp.square(masked.astype(F32)))
@@ -170,8 +186,8 @@
         s_local[:, :, HALF : HALF + rows_here + 2 * HALF, :].astype(F32) * d_local.astype(F32)
     )
     trace_four = jnp.sum(jnp.square(s_local.astype(F32)))
-    local_sums, _ = lax.optimization_barrier(
-        (jnp.stack([trace_two, trace_three, trace_four]), square_wide)
+    local_sums, _, _ = lax.optimization_barrier(
+        (jnp.stack([trace_two, trace_three, trace_four]), square_wide[0], square_wide[-1])
     )
     sums = butterfly_sum(local_sums, ("row", "col"))
     total_two, total_three, total_four = sums[0], sums[1], sums[2]

time: 323 us -> 298 us (0.923)
  local copies, waits for them, and re-layouts: 67 us -> 43.8 us
  starting transfers between devices: 51.6 us -> 67.4 us
  waiting for transfers between devices: 87.1 us -> 71.8 us
  other arithmetic: 24.6 us -> 21.3 us
    unnamed x29 -> x17, local copies, waits for them, and re-layouts: 26.8 us -> 7.76 us
    ppermute x7, starting transfers between devices: 4.63 us -> 20.3 us  [butterfly_sum(): value = value + lax.ppermute(value, axes, pairs)]
    ppermute x16, waiting for transfers between devices: 65.7 us -> 56.9 us  [passed_along(): return lax.ppermute(value, axis, pairs)]
    ppermute x7, waiting for transfers between devices: 21.4 us -> 14.9 us  [butterfly_sum(): value = value + lax.ppermute(value, axes, pairs)]
    concatenate x4 -> x2, local copies, waits for them, and re-layouts: 4.32 us -> 0.11 us  [spread(): jnp.concatenate([part[1] for part in ordered], axis=0)]
  transfers between devices with their start and end apart: 23 -> 23, of which waited for: 11 -> 12; matrix products, arithmetic and copies ran while one was open for 38% -> 33% of each run, Pallas kernels for 14% -> 15%
where the time goes in v4:
time: 298 us; the launch traced here: 296 us
  waiting for transfers between devices  71.8 us (24%)
  starting transfers between devices  67.4 us (23%)
  Pallas kernels  44.1 us (15%)
  local copies, waits for them, and re-layouts  43.8 us (15%)
  matrix products  42.7 us (14%)
  other arithmetic  21.3 us (7%)
  between operations  4.65 us (2%)
    ppermute x16, waiting for transfers between devices, passed_along(): return lax.ppermute(value, axis, pairs)  56.9 us
    ppermute x16, starting transfers between devices, passed_along(): return lax.ppermute(value, axis, pairs)  47.2 us
    pallas_call x3, Pallas kernels, densify_transposed(): pl.pallas_call(kernel, out_shape=jax.ShapeDtypeStruct((width * b, count *...  44.1 us
    dot_general x3, matrix products, slab_matmul_nt(): lax.dot_general(left.reshape(r * b, k * b), right_t, (((1,), (1,)), ((),...  38.5 us
    ppermute x7, starting transfers between devices, butterfly_sum(): value = value + lax.ppermute(value, axes, pairs)  20.3 us
    gather x5, local copies, waits for them, and re-layouts, pick(): picked = jnp.take_along_axis(dense, places[:, None, :, None], axis=2)  16.3 us
    ppermute x7, waiting for transfers between devices, butterfly_sum(): value = value + lax.ppermute(value, axes, pairs)  14.9 us
    unnamed x17, local copies, waits for them, and re-layouts  7.76 us
  transfers between devices with their start and end apart: 23, of which 12 were waited for; matrix products, arithmetic and copies ran while one was open for 33% of the time, Pallas kernels for 15%

profile of v4, /device:TPU:6, one launch (start us, length us, event | category | flops | bytes accessed | tf_op | source)
XLA Modules:
  0.0 295.7 jit_solution(16004821105992876266)
XLA Ops:
  6.4 4.3 %collective-permute-start.3 = (bf16[4,8,128,128]{3,2,1,0:T(8,128)(2,1)S(1)}, bf16[4,8,128,128]{3,2,1,0:T(8,128)(2,1)}, u32[]{:S(2)}, u32[]{:S(2)}) collective-permute-start(bf16[4,8,128,128]{3,2,1,0:T(8,128)(2,1)S(1)} %bitcast.97), channel_id=1, source_target_pairs={{0,127},{1,0},{2,1},{3,2},{4,3},{5,4},{6,5},{7,6},{8,7},{9,8},{10,... | collective-permute-start | bytes 3145736 | tf_op jit(solution)/shard_map/ppermute | solution.py:16
  10.7 6.0 %collective-permute-start.1 = (s32[4,8]{1,0:T(4,128)S(1)}, s32[4,8]{1,0:T(4,128)S(1)}, u32[]{:S(2)}, u32[]{:S(2)}) collective-permute-start(s32[4,8]{1,0:T(4,128)S(1)} %copy-done.4), channel_id=1, source_target_pairs={{0,127},{1,0},{2,1},{3,2},{4,3},{5,4},{6,5},{7,6},{8,7},{9,8},{10,... | collective-permute-start | bytes 392 | tf_op jit(solution)/shard_map/ppermute | solution.py:16
  23.8 5.1 %collective-permute-done = s32[4,8]{1,0:T(4,128)S(1)} collective-permute-done((s32[4,8]{1,0:T(4,128)S(1)}, s32[4,8]{1,0:T(4,128)S(1)}, u32[]{:S(2)}, u32[]{:S(2)}) %collective-permute-start) | collective-permute-done | bytes 160 | tf_op jit(solution)/shard_map/ppermute | solution.py:16
  28.9 6.0 %collective-permute-start.21 = (s32[4,16]{1,0:T(4,128)S(1)}, s32[4,16]{1,0:T(4,128)S(1)}, u32[]{:S(2)}, u32[]{:S(2)}) collective-permute-start(s32[4,16]{1,0:T(4,128)S(1)} %copy-done.6), channel_id=1, source_target_pairs={{0,127},{1,0},{2,1},{3,2},{4,3},{5,4},{6,5},{7,6},{8,7},{9,8},{10,... | collective-permute-start | bytes 776 | tf_op jit(solution)/shard_map/ppermute | solution.py:16
  36.2 8.3 %shard_map.77 = bf16[2560,1536]{1,0:T(8,128)(2,1)} custom-call(s32[12,8]{1,0:T(8,128)} %compare_select_fusion.2.place_ref, s32[12,8]{1,0:T(8,128)} %and_convert_fusion.2.valid_ref, bf16[4,8,128,128]{3,2,1,0:T(8,128)(2,1)} %collective-permute-done.2.refs_0_.refs_1_, bf16[4,8,128,128]{3,2,1,0:T(8,128)(2,1)} %bitcast.98, ...), custom_call_target="tpu_custom_call" | custom-call | bytes 11010048 | tf_op jit(solution)/shard_map/pallas_call | solution.py:110
  44.5 7.9 %fusion.15 = bf16[4,128,20,128]{1,3,2,0:T(8,128)(2,1)S(1)} fusion(bf16[4,128,1536,1]{1,2,3,0:T(8,128)(2,1)} %bitcast.104, bf16[20,128,1536,1]{2,1,0,3:T(8,128)(2,1)} %bitcast.101), kind=kOutput, calls=%fused_computation.51 | convolution fusion | flops 4026531840 | bytes 12058624 | tf_op jit(solution)/shard_map/dot_general | solution.py:123
  55.5 4.3 %multiply_reduce_fusion = (f32[]{:T(128)}, bf16[4,128,20,128]{3,2,1,0:T(8,128)(2,1)S(1)}) fusion(bf16[4,128,20,128]{3,2,1,0:T(8,128)(2,1)} %copy.46, pred[4,20]{1,0:T(4,128)(4,1)S(1)} %broadcast_compare_fusion), kind=kLoop, calls=%fused_computation.3 | loop fusion | flops 5242879 | bytes 5242964 | tf_op jit(solution)/shard_map/reduce_sum | solution.py:188
  62.0 4.5 %copy.47 = bf16[4,16,128,128]{2,3,1,0:T(8,128)(2,1)} copy(bf16[4,16,128,128]{3,1,2,0:T(8,128)(2,1)} %fusion.5) | data formatting | bytes 4194304 | tf_op jit(solution)/shard_map/rcs,rxcz->rsxz/dot_general | solution.py:140
  66.5 6.0 %collective-permute-start.6 = (bf16[4,16,128,128]{3,2,1,0:T(8,128)(2,1)}, bf16[4,16,128,128]{3,2,1,0:T(8,128)(2,1)}, u32[]{:S(2)}, u32[]{:S(2)}) collective-permute-start(bf16[4,16,128,128]{3,2,1,0:T(8,128)(2,1)} %bitcast.90), channel_id=1, source_target_pairs={{0,127},{1,0},{2,1},{3,2},{4,3},{5,4},{6,5},{7,6},{8,7},{9,8},{10,... | collective-permute-start | bytes 6291464 | tf_op jit(solution)/shard_map/ppermute | solution.py:16
  72.7 5.9 %collective-permute-start.16 = (s32[4,8]{1,0:T(4,128)S(1)}, s32[4,8]{1,0:T(4,128)S(1)}, u32[]{:S(2)}, u32[]{:S(2)}) collective-permute-start(s32[4,8]{1,0:T(4,128)S(1)} %collective-permute-done.1), channel_id=1, source_target_pairs={{0,127},{1,0},{2,1},{3,2},{4,3},{5,4},{6,5},{7,6},{8,7},{9,8},{10,... | collective-permute-start | bytes 392 | tf_op jit(solution)/shard_map/ppermute | solution.py:16
  78.7 33.6 %collective-permute-done.15 = s32[4,8]{1,0:T(4,128)S(1)} collective-permute-done((s32[4,8]{1,0:T(4,128)S(1)}, s32[4,8]{1,0:T(4,128)S(1)}, u32[]{:S(2)}, u32[]{:S(2)}) %collective-permute-start.15) | collective-permute-done | bytes 160 | tf_op jit(solution)/shard_map/ppermute | solution.py:16
  119.5 5.4 %collective-permute-start.18 = (bf16[4,8,128,128]{3,2,1,0:T(8,128)(2,1)}, bf16[4,8,128,128]{3,2,1,0:T(8,128)(2,1)}, u32[]{:S(2)}, u32[]{:S(2)}) collective-permute-start(bf16[4,8,128,128]{3,2,1,0:T(8,128)(2,1)} %collective-permute-done.3.refs_2_.refs_3_), channel_id=1, source_target_pairs={{0,127},{1,0},{2,1},{3,2},{4,3},{5,4},{6,5},{7,6},{8,7},{9,8},{10,... | collective-permute-start | bytes 3145736 | tf_op jit(solution)/shard_map/ppermute | solution.py:16
  149.8 14.9 %shard_map.78 = bf16[3584,2560]{1,0:T(8,128)(2,1)} custom-call(s32[20,8]{1,0:T(8,128)} %compare_select_fusion.1.place_ref, s32[20,8]{1,0:T(8,128)} %and_convert_fusion.1.valid_ref, bf16[4,8,128,128]{3,2,1,0:T(8,128)(2,1)} %collective-permute-done.17.refs_0_, bf16[4,8,128,128]{3,2,1,0:T(8,128)(2,1)} %collective-permute-done.2.refs_0_.refs_1_, ...), custom_call_target="tpu_custom_call" | custom-call | bytes 23592960 | tf_op jit(solution)/shard_map/pallas_call | solution.py:110
  164.7 6.0 %collective-permute-start.7 = (bf16[4,16,128,128]{3,2,1,0:T(8,128)(2,1)}, bf16[4,16,128,128]{3,2,1,0:T(8,128)(2,1)}, u32[]{:S(2)}, u32[]{:S(2)}) collective-permute-start(bf16[4,16,128,128]{3,2,1,0:T(8,128)(2,1)} %collective-permute-done.6.refs_3_), channel_id=1, source_target_pairs={{0,127},{1,0},{2,1},{3,2},{4,3},{5,4},{6,5},{7,6},{8,7},{9,8},{10,... | collective-permute-start | bytes 6291464 | tf_op jit(solution)/shard_map/ppermute | solution.py:16
  170.6 15.3 %fusion.16 = f32[4,128,28,128]{3,1,2,0:T(8,128)} fusion(bf16[4,128,2560,1]{1,2,3,0:T(8,128)(2,1)S(1)} %bitcast.102, bf16[28,128,2560,1]{2,1,0,3:T(8,128)(2,1)} %bitcast.92), kind=kOutput, calls=%fused_computation.52 | convolution fusion | flops 9395240960 | bytes 28311552 | tf_op jit(solution)/shard_map/dot_general | solution.py:123
  185.9 6.0 %gather_fusion.1 = f32[64,128,128]{2,1,0:T(8,128)} fusion(f32[4,128,28,128]{3,1,2,0:T(8,128)} %fusion.16, s32[64]{0:T(128)S(1)} %reshape.149), kind=kCustom, calls=%fused_computation.clone | custom fusion | bytes 8389120 | tf_op jit(solution)/shard_map/jit(take_along_axis)/gather | solution.py:146
  191.9 14.5 %collective-permute-done.5.refs_0_ = bf16[4,16,128,128]{3,2,1,0:T(8,128)(2,1)} collective-permute-done((bf16[4,16,128,128]{3,2,1,0:T(8,128)(2,1)}, bf16[4,16,128,128]{3,2,1,0:T(8,128)(2,1)}, u32[]{:S(2)}, u32[]{:S(2)}) %collective-permute-start.5) | collective-permute-done | bytes 2097184 | tf_op jit(solution)/shard_map/ppermute | solution.py:16
  209.3 20.9 %shard_map.79 = bf16[3584,2560]{1,0:T(8,128)(2,1)} custom-call(s32[20,16]{1,0:T(8,128)} %compare_select_fusion.place_ref, s32[20,16]{1,0:T(8,128)} %and_convert_fusion.valid_ref, bf16[4,16,128,128]{3,2,1,0:T(8,128)(2,1)} %collective-permute-done.5.refs_0_, bf16[4,16,128,128]{3,2,1,0:T(8,128)(2,1)} %collective-permute-done.4.refs_1_, ...), custom_call_target="tpu_custom_call" | custom-call | bytes 28835840 | tf_op jit(solution)/shard_map/pallas_call | solution.py:110
  230.2 15.3 %fusion.17 = f32[4,128,28,128]{3,1,2,0:T(8,128)} fusion(bf16[4,128,2560,1]{1,2,3,0:T(8,128)(2,1)S(1)} %bitcast.103, bf16[28,128,2560,1]{2,1,0,3:T(8,128)(2,1)} %bitcast.93), kind=kOutput, calls=%fused_computation.53 | convolution fusion | flops 9395240960 | bytes 28311552 | tf_op jit(solution)/shard_map/dot_general | solution.py:123
  245.5 6.0 %gather_fusion.2 = f32[64,128,128]{2,1,0:T(8,128)} fusion(f32[4,128,28,128]{3,1,2,0:T(8,128)} %fusion.17, s32[64]{0:T(128)S(1)} %reshape.149), kind=kCustom, calls=%fused_computation.1.clone | custom fusion | bytes 8389120 | tf_op jit(solution)/shard_map/jit(take_along_axis)/gather | solution.py:146
  251.4 5.4 %collective-permute-start.9 = (f32[3]{0:T(128)S(1)}, f32[3]{0:T(128)S(1)}, u32[]{:S(2)}, u32[]{:S(2)}) collective-permute-start(f32[3]{0:T(128)S(1)} %add.163), channel_id=1, source_target_pairs={{0,2},{1,3},{2,0},{3,1},{4,6},{5,7},{6,4},{7,5},{8,10},{9,11},{10,... | collective-permute-start | bytes 44 | tf_op jit(solution)/shard_map/ppermute | solution.py:49
  262.0 13.3 %collective-permute-start.11 = (f32[3]{0:T(128)S(1)}, f32[3]{0:T(128)S(1)}, u32[]{:S(2)}, u32[]{:S(2)}) collective-permute-start(f32[3]{0:T(128)S(1)} %add.165), channel_id=1, source_target_pairs={{0,8},{1,9},{2,10},{3,11},{4,12},{5,13},{6,14},{7,15},{8,0},{9,1},... | collective-permute-start | bytes 44 | tf_op jit(solution)/shard_map/ppermute | solution.py:49
  281.5 5.1 %collective-permute-done.14 = f32[3]{0:T(128)S(1)} collective-permute-done((f32[3]{0:T(128)S(1)}, f32[3]{0:T(128)S(1)}, u32[]{:S(2)}, u32[]{:S(2)}) %collective-permute-start.14) | collective-permute-done | bytes 44 | tf_op jit(solution)/shard_map/ppermute | solution.py:49
  290.5 5.2 %fusion.2 = bf16[4,16,128,128]{3,2,1,0:T(8,128)(2,1)} fusion(f32[4,16,128,128]{3,2,1,0:T(8,128)} %bitcast.95, f32[4,16,128,128]{3,2,1,0:T(8,128)} %bitcast.94, f32[]{:T(128)} %bitcast.14, bf16[4,16,128,128]{3,2,1,0:T(8,128)(2,1)S(1)} %bitcast.100, f32[]{:T(128)S(6)} %sub.47, f32[]{:T(128)S(6)} %sub.44, pred[4,16]{1,0:T(4,128)(4,1)S(1)} %and_bitcast_fusion, ...), kind=kLoop, calls=%fused_computation.11 | loop fusion | flops 10485760 | bytes 12583052 | tf_op jit(solution)/shard_map/add | solution.py:206
  (89 shorter events, 65.9 us)
Async XLA Ops:
  4.5 31.7 %collective-permute-start.2 = (bf16[4,8,128,128]{3,2,1,0:T(8,128)(2,1)S(1)}, bf16[4,8,128,128]{3,2,1,0:T(8,128)(2,1)}, u32[]{:S(2)}, u32[]{:S(2)}) collective-permute-start(bf16[4,8,128,128]{3,2,1,0:T(8,128)(2,1)S(1)} %bitcast.96), channel_id=1, source_target_pairs={{0,1},{1,2},{2,3},{3,4},{4,5},{5,6},{6,7},{7,8},{8,9},{9,10},{10,1... | collective-permute-start | bytes 3145736 | tf_op jit(solution)/shard_map/ppermute | solution.py:16
  6.4 29.8 %collective-permute-start.3 = (bf16[4,8,128,128]{3,2,1,0:T(8,128)(2,1)S(1)}, bf16[4,8,128,128]{3,2,1,0:T(8,128)(2,1)}, u32[]{:S(2)}, u32[]{:S(2)}) collective-permute-start(bf16[4,8,128,128]{3,2,1,0:T(8,128)(2,1)S(1)} %bitcast.97), channel_id=1, source_target_pairs={{0,127},{1,0},{2,1},{3,2},{4,3},{5,4},{6,5},{7,6},{8,7},{9,8},{10,... | collective-permute-start | bytes 3145736 | tf_op jit(solution)/shard_map/ppermute | solution.py:16
  10.7 18.2 %collective-permute-start = (s32[4,8]{1,0:T(4,128)S(1)}, s32[4,8]{1,0:T(4,128)S(1)}, u32[]{:S(2)}, u32[]{:S(2)}) collective-permute-start(s32[4,8]{1,0:T(4,128)S(1)} %copy-done.4), channel_id=1, source_target_pairs={{0,1},{1,2},{2,3},{3,4},{4,5},{5,6},{6,7},{7,8},{8,9},{9,10},{10,1... | collective-permute-start | bytes 392 | tf_op jit(solution)/shard_map/ppermute | solution.py:16
  10.7 24.2 %collective-permute-start.1 = (s32[4,8]{1,0:T(4,128)S(1)}, s32[4,8]{1,0:T(4,128)S(1)}, u32[]{:S(2)}, u32[]{:S(2)}) collective-permute-start(s32[4,8]{1,0:T(4,128)S(1)} %copy-done.4), channel_id=1, source_target_pairs={{0,127},{1,0},{2,1},{3,2},{4,3},{5,4},{6,5},{7,6},{8,7},{9,8},{10,... | collective-permute-start | bytes 392 | tf_op jit(solution)/shard_map/ppermute | solution.py:16
  16.7 56.0 %collective-permute-start.19 = (s32[4,16]{1,0:T(4,128)S(1)}, s32[4,16]{1,0:T(4,128)S(1)}, u32[]{:S(2)}, u32[]{:S(2)}) collective-permute-start(s32[4,16]{1,0:T(4,128)S(1)} %copy-done.6), channel_id=1, source_target_pairs={{0,1},{1,2},{2,3},{3,4},{4,5},{5,6},{6,7},{7,8},{8,9},{9,10},{10,1... | collective-permute-start | bytes 776 | tf_op jit(solution)/shard_map/ppermute | solution.py:16
  28.9 86.9 %collective-permute-start.21 = (s32[4,16]{1,0:T(4,128)S(1)}, s32[4,16]{1,0:T(4,128)S(1)}, u32[]{:S(2)}, u32[]{:S(2)}) collective-permute-start(s32[4,16]{1,0:T(4,128)S(1)} %copy-done.6), channel_id=1, source_target_pairs={{0,127},{1,0},{2,1},{3,2},{4,3},{5,4},{6,5},{7,6},{8,7},{9,8},{10,... | collective-permute-start | bytes 776 | tf_op jit(solution)/shard_map/ppermute | solution.py:16
  66.5 98.2 %collective-permute-start.4 = (bf16[4,16,128,128]{3,2,1,0:T(8,128)(2,1)}, bf16[4,16,128,128]{3,2,1,0:T(8,128)(2,1)}, u32[]{:S(2)}, u32[]{:S(2)}) collective-permute-start(bf16[4,16,128,128]{3,2,1,0:T(8,128)(2,1)} %bitcast.89), channel_id=1, source_target_pairs={{0,1},{1,2},{2,3},{3,4},{4,5},{5,6},{6,7},{7,8},{8,9},{9,10},{10,1... | collective-permute-start | bytes 6291464 | tf_op jit(solution)/shard_map/ppermute | solution.py:16
  66.5 98.2 %collective-permute-start.6 = (bf16[4,16,128,128]{3,2,1,0:T(8,128)(2,1)}, bf16[4,16,128,128]{3,2,1,0:T(8,128)(2,1)}, u32[]{:S(2)}, u32[]{:S(2)}) collective-permute-start(bf16[4,16,128,128]{3,2,1,0:T(8,128)(2,1)} %bitcast.90), channel_id=1, source_target_pairs={{0,127},{1,0},{2,1},{3,2},{4,3},{5,4},{6,5},{7,6},{8,7},{9,8},{10,... | collective-permute-start | bytes 6291464 | tf_op jit(solution)/shard_map/ppermute | solution.py:16
  72.7 39.6 %collective-permute-start.15 = (s32[4,8]{1,0:T(4,128)S(1)}, s32[4,8]{1,0:T(4,128)S(1)}, u32[]{:S(2)}, u32[]{:S(2)}) collective-permute-start(s32[4,8]{1,0:T(4,128)S(1)} %collective-permute-done), channel_id=1, source_target_pairs={{0,1},{1,2},{2,3},{3,4},{4,5},{5,6},{6,7},{7,8},{8,9},{9,10},{10,1... | collective-permute-start | bytes 392 | tf_op jit(solution)/shard_map/ppermute | solution.py:16
  72.7 42.3 %collective-permute-start.16 = (s32[4,8]{1,0:T(4,128)S(1)}, s32[4,8]{1,0:T(4,128)S(1)}, u32[]{:S(2)}, u32[]{:S(2)}) collective-permute-start(s32[4,8]{1,0:T(4,128)S(1)} %collective-permute-done.1), channel_id=1, source_target_pairs={{0,127},{1,0},{2,1},{3,2},{4,3},{5,4},{6,5},{7,6},{8,7},{9,8},{10,... | collective-permute-start | bytes 392 | tf_op jit(solution)/shard_map/ppermute | solution.py:16
  112.3 7.2 %collective-permute-start.20 = (s32[4,16]{1,0:T(4,128)S(1)}, s32[4,16]{1,0:T(4,128)S(1)}, u32[]{:S(2)}, u32[]{:S(2)}) collective-permute-start(s32[4,16]{1,0:T(4,128)S(1)} %collective-permute-done.19), channel_id=1, source_target_pairs={{0,1},{1,2},{2,3},{3,4},{4,5},{5,6},{6,7},{7,8},{8,9},{9,10},{10,1... | collective-permute-start | bytes 776 | tf_op jit(solution)/shard_map/ppermute | solution.py:16
  115.8 9.8 %collective-permute-start.22 = (s32[4,16]{1,0:T(4,128)S(1)}, s32[4,16]{1,0:T(4,128)S(1)}, u32[]{:S(2)}, u32[]{:S(2)}) collective-permute-start(s32[4,16]{1,0:T(4,128)S(1)} %collective-permute-done.21), channel_id=1, source_target_pairs={{0,127},{1,0},{2,1},{3,2},{4,3},{5,4},{6,5},{7,6},{8,7},{9,8},{10,... | collective-permute-start | bytes 776 | tf_op jit(solution)/shard_map/ppermute | solution.py:16
  119.0 30.8 %collective-permute-start.17 = (bf16[4,8,128,128]{3,2,1,0:T(8,128)(2,1)}, bf16[4,8,128,128]{3,2,1,0:T(8,128)(2,1)}, u32[]{:S(2)}, u32[]{:S(2)}) collective-permute-start(bf16[4,8,128,128]{3,2,1,0:T(8,128)(2,1)} %collective-permute-done.2.refs_0_.refs_1_), channel_id=1, source_target_pairs={{0,1},{1,2},{2,3},{3,4},{4,5},{5,6},{6,7},{7,8},{8,9},{9,10},{10,1... | collective-permute-start | bytes 3145736 | tf_op jit(solution)/shard_map/ppermute | solution.py:16
  119.5 30.2 %collective-permute-start.18 = (bf16[4,8,128,128]{3,2,1,0:T(8,128)(2,1)}, bf16[4,8,128,128]{3,2,1,0:T(8,128)(2,1)}, u32[]{:S(2)}, u32[]{:S(2)}) collective-permute-start(bf16[4,8,128,128]{3,2,1,0:T(8,128)(2,1)} %collective-permute-done.3.refs_2_.refs_3_), channel_id=1, source_target_pairs={{0,127},{1,0},{2,1},{3,2},{4,3},{5,4},{6,5},{7,6},{8,7},{9,8},{10,... | collective-permute-start | bytes 3145736 | tf_op jit(solution)/shard_map/ppermute | solution.py:16
  164.7 41.7 %collective-permute-start.5 = (bf16[4,16,128,128]{3,2,1,0:T(8,128)(2,1)}, bf16[4,16,128,128]{3,2,1,0:T(8,128)(2,1)}, u32[]{:S(2)}, u32[]{:S(2)}) collective-permute-start(bf16[4,16,128,128]{3,2,1,0:T(8,128)(2,1)} %collective-permute-done.4.refs_1_), channel_id=1, source_target_pairs={{0,1},{1,2},{2,3},{3,4},{4,5},{5,6},{6,7},{7,8},{8,9},{9,10},{10,1... | collective-permute-start | bytes 6291464 | tf_op jit(solution)/shard_map/ppermute | solution.py:16
  164.7 44.6 %collective-permute-start.7 = (bf16[4,16,128,128]{3,2,1,0:T(8,128)(2,1)}, bf16[4,16,128,128]{3,2,1,0:T(8,128)(2,1)}, u32[]{:S(2)}, u32[]{:S(2)}) collective-permute-start(bf16[4,16,128,128]{3,2,1,0:T(8,128)(2,1)} %collective-permute-done.6.refs_3_), channel_id=1, source_target_pairs={{0,127},{1,0},{2,1},{3,2},{4,3},{5,4},{6,5},{7,6},{8,7},{9,8},{10,... | collective-permute-start | bytes 6291464 | tf_op jit(solution)/shard_map/ppermute | solution.py:16
  209.3 42.2 %collective-permute-start.8 = (f32[3]{0:T(128)S(1)}, f32[3]{0:T(128)S(1)}, u32[]{:S(2)}, u32[]{:S(2)}) collective-permute-start(f32[3]{0:T(128)S(1)} %pad_maximum_fusion), channel_id=1, source_target_pairs={{0,1},{1,0},{2,3},{3,2},{4,5},{5,4},{6,7},{7,6},{8,9},{9,8},{10,11... | collective-permute-start | bytes 44 | tf_op jit(solution)/shard_map/ppermute | solution.py:49
  245.5 45.0 %copy-start.2 = (bf16[64,128,128]{2,1,0:T(8,128)(2,1)S(1)}, bf16[64,128,128]{2,1,0:T(8,128)(2,1)}, u32[]{:S(2)}) copy-start(bf16[64,128,128]{2,1,0:T(8,128)(2,1)} %gather_fusion) | copy-start | bytes 6291460
  251.4 6.9 %collective-permute-start.9 = (f32[3]{0:T(128)S(1)}, f32[3]{0:T(128)S(1)}, u32[]{:S(2)}, u32[]{:S(2)}) collective-permute-start(f32[3]{0:T(128)S(1)} %add.163), channel_id=1, source_target_pairs={{0,2},{1,3},{2,0},{3,1},{4,6},{5,7},{6,4},{7,5},{8,10},{9,11},{10,... | collective-permute-start | bytes 44 | tf_op jit(solution)/shard_map/ppermute | solution.py:49
  258.4 3.6 %collective-permute-start.10 = (f32[3]{0:T(128)S(1)}, f32[3]{0:T(128)S(1)}, u32[]{:S(2)}, u32[]{:S(2)}) collective-permute-start(f32[3]{0:T(128)S(1)} %add.164), channel_id=1, source_target_pairs={{0,4},{1,5},{2,6},{3,7},{4,0},{5,1},{6,2},{7,3},{8,12},{9,13},{10,... | collective-permute-start | bytes 44 | tf_op jit(solution)/shard_map/ppermute | solution.py:49
  262.0 14.8 %collective-permute-start.11 = (f32[3]{0:T(128)S(1)}, f32[3]{0:T(128)S(1)}, u32[]{:S(2)}, u32[]{:S(2)}) collective-permute-start(f32[3]{0:T(128)S(1)} %add.165), channel_id=1, source_target_pairs={{0,8},{1,9},{2,10},{3,11},{4,12},{5,13},{6,14},{7,15},{8,0},{9,1},... | collective-permute-start | bytes 44 | tf_op jit(solution)/shard_map/ppermute | solution.py:49
  276.8 1.2 collective-permute-start.12
  278.0 3.6 %collective-permute-start.13 = (f32[3]{0:T(128)S(1)}, f32[3]{0:T(128)S(1)}, u32[]{:S(2)}, u32[]{:S(2)}) collective-permute-start(f32[3]{0:T(128)S(1)} %add.167), channel_id=1, source_target_pairs={{0,32},{1,33},{2,34},{3,35},{4,36},{5,37},{6,38},{7,39},{8,40},{9,... | collective-permute-start | bytes 44 | tf_op jit(solution)/shard_map/ppermute | solution.py:49
  281.5 5.1 %collective-permute-start.14 = (f32[3]{0:T(128)S(1)}, f32[3]{0:T(128)S(1)}, u32[]{:S(2)}, u32[]{:S(2)}) collective-permute-start(f32[3]{0:T(128)S(1)} %add.168), channel_id=1, source_target_pairs={{0,64},{1,65},{2,66},{3,67},{4,68},{5,69},{6,70},{7,71},{8,72},{9,... | collective-permute-start | bytes 44 | tf_op jit(solution)/shard_map/ppermute | solution.py:49
  (6 other events, 102.5 us)

commit v5 on v4

--- a/solution.py
+++ b/solution.py
@@ -29,14 +29,21 @@
 
 
 def spread(blocks, columns, reach_devices):
+    count, slots, b, _ = blocks.shape
+    tag = jnp.pad(
+        columns.astype(BF16)[:, None, None, :], ((0, 0), (0, 0), (0, b - 1), (0, b - slots))
+    )
+    payload = jnp.concatenate([blocks, tag], axis=1)
     earlier, later = ([], [])
     for heading, arrivals in ((1, earlier), (-1, later)):
-        carried = (blocks, columns)
+        carried = payload
         for _ in range(reach_devices):
             carried = passed_along(carried, ("row", "col"), heading)
             arrivals.append(carried)
-    ordered = list(reversed(earlier)) + [(blocks, columns)] + later
-    return [part[0] for part in ordered], jnp.concatenate([part[1] for part in ordered], axis=0)
+    pieces = list(reversed(earlier)) + [payload] + later
+    joined = [piece[:, slots, 0, :slots].astype(jnp.int32) for piece in reversed(earlier)]
+    joined += [columns] + [piece[:, slots, 0, :slots].astype(jnp.int32) for piece in later]
+    return pieces, jnp.concatenate(joined, axis=0)
 
 
 def butterfly_sum(value, axes):
@@ -67,7 +74,7 @@
 def densify_transposed(pieces, columns, first_row, low, width, row_range):
     top_row, end_row = row_range
     count = end_row - top_row
-    slots, b = pieces[0].shape[1], pieces[0].shape[2]
+    slots, b = columns.shape[1], pieces[0].shape[2]
     columns = columns[top_row:end_row]
     rows = jnp.arange(count, dtype=jnp.int32)[:, None] + first_row
     place = rows + columns - low

time: 298 us -> 300 us (level)
  starting transfers between devices: 67.4 us -> 31.5 us
  waiting for transfers between devices: 71.8 us -> 104 us
  other arithmetic: 21.3 us -> 30.8 us
  local copies, waits for them, and re-layouts: 43.8 us -> 40.6 us
    ppermute x16 -> x8, waiting for transfers between devices: 56.9 us -> 88.7 us  [passed_along(): return lax.ppermute(value, axis, pairs)]
    ppermute x16 -> x8, starting transfers between devices: 47.2 us -> 18.4 us  [passed_along(): return lax.ppermute(value, axis, pairs)]
    ppermute x7, starting transfers between devices: 20.3 us -> 13.1 us  [butterfly_sum(): value = value + lax.ppermute(value, axes, pairs)]
    convert_element_type x0 -> x8, other arithmetic: none -> 5.61 us  [spread(): piece[:, slots, 0, :slots].astype(jnp.int32)]
    concatenate x0 -> x2, other arithmetic: none -> 3.43 us  [spread(): payload = jnp.concatenate([blocks, tag], axis=1)]
  transfers between devices with their start and end apart: 23 -> 15, of which waited for: 12 -> 10; matrix products, arithmetic and copies ran while one was open for 33% -> 25% of each run, Pallas kernels for 15% -> 12%
where the time goes in v5:
time: 300 us; the launch traced here: 299 us
  waiting for transfers between devices  104 us (35%)
  Pallas kernels  44.7 us (15%)
  matrix products  42.8 us (14%)
  local copies, waits for them, and re-layouts  40.6 us (14%)
  starting transfers between devices  31.5 us (10%)
  other arithmetic  30.8 us (10%)
  between operations  4.69 us (2%)
    ppermute x8, waiting for transfers between devices, passed_along(): return lax.ppermute(value, axis, pairs)  88.7 us
    pallas_call x3, Pallas kernels, densify_transposed(): pl.pallas_call(kernel, out_shape=jax.ShapeDtypeStruct((width * b, count *...  44.7 us
    dot_general x3, matrix products, slab_matmul_nt(): lax.dot_general(left.reshape(r * b, k * b), right_t, (((1,), (1,)), ((),...  38.6 us
    ppermute x8, starting transfers between devices, passed_along(): return lax.ppermute(value, axis, pairs)  18.4 us
    gather x5, local copies, waits for them, and re-layouts, pick(): picked = jnp.take_along_axis(dense, places[:, None, :, None], axis=2)  16.3 us
    ppermute x7, waiting for transfers between devices, butterfly_sum(): value = value + lax.ppermute(value, axes, pairs)  15.1 us
    ppermute x7, starting transfers between devices, butterfly_sum(): value = value + lax.ppermute(value, axes, pairs)  13.1 us
    unnamed x17, local copies, waits for them, and re-layouts  6.26 us
  transfers between devices with their start and end apart: 15, of which 10 were waited for; matrix products, arithmetic and copies ran while one was open for 25% of the time, Pallas kernels for 12%

profile of v5, /device:TPU:6, one launch (start us, length us, event | category | flops | bytes accessed | tf_op | source)
XLA Modules:
  0.0 298.9 jit_solution(4013966119042776905)
XLA Ops:
  5.3 6.3 %collective-permute-start.1 = (bf16[4,9,128,128]{3,2,1,0:T(8,128)(2,1)S(1)}, bf16[4,9,128,128]{3,2,1,0:T(8,128)(2,1)}, u32[]{:S(2)}, u32[]{:S(2)}) collective-permute-start(bf16[4,9,128,128]{3,2,1,0:T(8,128)(2,1)S(1)} %fusion.6.refs_1_.refs_2_), channel_id=1, source_target_pairs={{0,127},{1,0},{2,1},{3,2},{4,3},{5,4},{6,5},{7,6},{8,7},{9,8},{10,... | collective-permute-start | bytes 3538952 | tf_op jit(solution)/shard_map/ppermute | solution.py:16
  18.1 15.3 %collective-permute-done.1.refs_2_.refs_3_ = bf16[4,9,128,128]{3,2,1,0:T(8,128)(2,1)} collective-permute-done((bf16[4,9,128,128]{3,2,1,0:T(8,128)(2,1)S(1)}, bf16[4,9,128,128]{3,2,1,0:T(8,128)(2,1)}, u32[]{:S(2)}, u32[]{:S(2)}) %collective-permute-start.1) | collective-permute-done | bytes 1179680 | tf_op jit(solution)/shard_map/ppermute | solution.py:16
  34.1 3.6 %collective-permute-done.refs_0_.refs_1_ = bf16[4,9,128,128]{3,2,1,0:T(8,128)(2,1)} collective-permute-done((bf16[4,9,128,128]{3,2,1,0:T(8,128)(2,1)S(1)}, bf16[4,9,128,128]{3,2,1,0:T(8,128)(2,1)}, u32[]{:S(2)}, u32[]{:S(2)}) %collective-permute-start) | collective-permute-done | bytes 1179680 | tf_op jit(solution)/shard_map/ppermute | solution.py:16
  39.7 8.4 %shard_map.77 = bf16[2560,1536]{1,0:T(8,128)(2,1)} custom-call(s32[12,8]{1,0:T(8,128)} %compare_select_fusion.2.place_ref, s32[12,8]{1,0:T(8,128)} %and_convert_fusion.2.valid_ref, bf16[4,9,128,128]{3,2,1,0:T(8,128)(2,1)} %collective-permute-done.refs_0_.refs_1_, bf16[4,9,128,128]{3,2,1,0:T(8,128)(2,1)} %copy-done.1, ...), custom_call_target="tpu_custom_call" | custom-call | bytes 11403264 | tf_op jit(solution)/shard_map/pallas_call | solution.py:117
  48.2 7.9 %fusion.19 = bf16[4,128,20,128]{1,3,2,0:T(8,128)(2,1)S(1)} fusion(bf16[4,128,1536,1]{1,2,3,0:T(8,128)(2,1)} %bitcast.111, bf16[20,128,1536,1]{2,1,0,3:T(8,128)(2,1)} %bitcast.108), kind=kOutput, calls=%fused_computation.67 | convolution fusion | flops 4026531840 | bytes 12058624 | tf_op jit(solution)/shard_map/dot_general | solution.py:130
  59.2 4.3 %multiply_reduce_fusion = (f32[]{:T(128)}, bf16[4,128,20,128]{3,2,1,0:T(8,128)(2,1)S(1)}) fusion(bf16[4,128,20,128]{3,2,1,0:T(8,128)(2,1)} %copy.53, pred[4,20]{1,0:T(4,128)(4,1)S(1)} %broadcast_compare_fusion), kind=kLoop, calls=%fused_computation.3 | loop fusion | flops 5242879 | bytes 5242964 | tf_op jit(solution)/shard_map/reduce_sum | solution.py:195
  65.6 4.6 %copy.54 = bf16[4,16,128,128]{2,3,1,0:T(8,128)(2,1)} copy(bf16[4,16,128,128]{3,1,2,0:T(8,128)(2,1)} %fusion.9) | data formatting | bytes 4194304 | tf_op jit(solution)/shard_map/rcs,rxcz->rsxz/dot_general | solution.py:147
  70.2 3.3 %fusion.4.refs_2_ = bf16[4,17,128,128]{3,2,1,0:T(8,128)(2,1)} fusion(bf16[4,1,1,16]{3,2,1,0:T(2,128)(2,1)S(1)} %copy.55, bf16[4,16,128,128]{3,2,1,0:T(8,128)(2,1)} %bitcast.101), kind=kLoop, calls=%fused_computation.15 | loop fusion | flops 6684672 | bytes 4325504 | tf_op jit(solution)/shard_map/concatenate | solution.py:36
  76.1 4.1 %collective-permute-start.14 = (bf16[4,9,128,128]{3,2,1,0:T(8,128)(2,1)}, bf16[4,9,128,128]{3,2,1,0:T(8,128)(2,1)}, u32[]{:S(2)}, u32[]{:S(2)}) collective-permute-start(bf16[4,9,128,128]{3,2,1,0:T(8,128)(2,1)} %collective-permute-done.1.refs_2_.refs_3_), channel_id=1, source_target_pairs={{0,127},{1,0},{2,1},{3,2},{4,3},{5,4},{6,5},{7,6},{8,7},{9,8},{10,... | collective-permute-start | bytes 3538952 | tf_op jit(solution)/shard_map/ppermute | solution.py:16
  81.0 4.0 %copy.60 = bf16[4,16,128,128]{3,2,1,0:T(8,128)(2,1)} copy(bf16[4,16,128,128]{2,3,1,0:T(8,128)(2,1)} %copy.54) | data formatting | bytes 4194304
  91.1 4.2 %gather_fusion = bf16[64,128,128]{2,1,0:T(8,128)(2,1)} fusion(bf16[4,128,28,128]{3,1,2,0:T(8,128)(2,1)} %pad.14.clone, s32[64]{0:T(128)S(1)} %reshape.151), kind=kCustom, calls=%fused_computation.2 | custom fusion | bytes 4194816 | tf_op jit(solution)/shard_map/jit(take_along_axis)/gather | solution.py:153
  95.2 3.3 %multiply_reduce_fusion.1 = f32[]{:T(128)} fusion(bf16[4,128,12,128]{3,2,1,0:T(8,128)(2,1)} %copy-done, bf16[4,128,20,128]{3,2,1,0:T(8,128)(2,1)S(1)} %get-tuple-element.16), kind=kLoop, calls=%fused_computation.11 | loop fusion | flops 3145727 | bytes 3145732 | tf_op jit(solution)/shard_map/reduce_sum | solution.py:192
  100.4 46.0 %collective-permute-done.14.refs_4_ = bf16[4,9,128,128]{3,2,1,0:T(8,128)(2,1)} collective-permute-done((bf16[4,9,128,128]{3,2,1,0:T(8,128)(2,1)}, bf16[4,9,128,128]{3,2,1,0:T(8,128)(2,1)}, u32[]{:S(2)}, u32[]{:S(2)}) %collective-permute-start.14) | collective-permute-done | bytes 1179680 | tf_op jit(solution)/shard_map/ppermute | solution.py:16
  149.3 15.1 %shard_map.78 = bf16[3584,2560]{1,0:T(8,128)(2,1)} custom-call(s32[20,8]{1,0:T(8,128)} %compare_select_fusion.1.place_ref, s32[20,8]{1,0:T(8,128)} %and_convert_fusion.1.valid_ref, bf16[4,9,128,128]{3,2,1,0:T(8,128)(2,1)} %collective-permute-done.13.refs_0_, bf16[4,9,128,128]{3,2,1,0:T(8,128)(2,1)} %collective-permute-done.refs_0_.refs_1_, ...), custom_call_target="tpu_custom_call" | custom-call | bytes 24248320 | tf_op jit(solution)/shard_map/pallas_call | solution.py:117
  164.4 5.4 %collective-permute-start.3 = (bf16[4,17,128,128]{3,2,1,0:T(8,128)(2,1)}, bf16[4,17,128,128]{3,2,1,0:T(8,128)(2,1)}, u32[]{:S(2)}, u32[]{:S(2)}) collective-permute-start(bf16[4,17,128,128]{3,2,1,0:T(8,128)(2,1)} %collective-permute-done.2.refs_1_), channel_id=1, source_target_pairs={{0,1},{1,2},{2,3},{3,4},{4,5},{5,6},{6,7},{7,8},{8,9},{9,10},{10,1... | collective-permute-start | bytes 6684680 | tf_op jit(solution)/shard_map/ppermute | solution.py:16
  169.8 15.3 %fusion.20 = f32[4,128,28,128]{3,1,2,0:T(8,128)} fusion(bf16[4,128,2560,1]{1,2,3,0:T(8,128)(2,1)S(1)} %bitcast.109, bf16[28,128,2560,1]{2,1,0,3:T(8,128)(2,1)} %bitcast.102), kind=kOutput, calls=%fused_computation.68 | convolution fusion | flops 9395240960 | bytes 28311552 | tf_op jit(solution)/shard_map/dot_general | solution.py:130
  185.2 6.0 %gather_fusion.1 = f32[64,128,128]{2,1,0:T(8,128)} fusion(f32[4,128,28,128]{3,1,2,0:T(8,128)} %fusion.20, s32[64]{0:T(128)S(1)} %reshape.173), kind=kCustom, calls=%fused_computation.clone | custom fusion | bytes 8389120 | tf_op jit(solution)/shard_map/jit(take_along_axis)/gather | solution.py:153
  192.5 23.7 %collective-permute-done.5.refs_4_ = bf16[4,17,128,128]{3,2,1,0:T(8,128)(2,1)} collective-permute-done((bf16[4,17,128,128]{3,2,1,0:T(8,128)(2,1)}, bf16[4,17,128,128]{3,2,1,0:T(8,128)(2,1)}, u32[]{:S(2)}, u32[]{:S(2)}) %collective-permute-start.5) | collective-permute-done | bytes 2228256 | tf_op jit(solution)/shard_map/ppermute | solution.py:16
  219.1 4.7 %collective-permute-start.6 = (f32[3]{0:T(128)S(1)}, f32[3]{0:T(128)S(1)}, u32[]{:S(2)}, u32[]{:S(2)}) collective-permute-start(f32[3]{0:T(128)S(1)} %pad_maximum_fusion), channel_id=1, source_target_pairs={{0,1},{1,0},{2,3},{3,2},{4,5},{5,4},{6,7},{7,6},{8,9},{9,8},{10,11... | collective-permute-start | bytes 44 | tf_op jit(solution)/shard_map/ppermute | solution.py:56
  223.8 21.1 %shard_map.79 = bf16[3584,2560]{1,0:T(8,128)(2,1)} custom-call(s32[20,16]{1,0:T(8,128)} %compare_select_fusion.place_ref, s32[20,16]{1,0:T(8,128)} %and_convert_fusion.valid_ref, bf16[4,17,128,128]{3,2,1,0:T(8,128)(2,1)} %collective-permute-done.3.refs_0_, bf16[4,17,128,128]{3,2,1,0:T(8,128)(2,1)} %collective-permute-done.2.refs_1_, ...), custom_call_target="tpu_custom_call" | custom-call | bytes 29491200 | tf_op jit(solution)/shard_map/pallas_call | solution.py:117
  244.9 15.3 %fusion.21 = f32[4,128,28,128]{3,1,2,0:T(8,128)} fusion(bf16[4,128,2560,1]{1,2,3,0:T(8,128)(2,1)S(1)} %bitcast.110, bf16[28,128,2560,1]{2,1,0,3:T(8,128)(2,1)} %bitcast.103), kind=kOutput, calls=%fused_computation.69 | convolution fusion | flops 9395240960 | bytes 28311552 | tf_op jit(solution)/shard_map/dot_general | solution.py:130
  260.2 6.0 %gather_fusion.2 = f32[64,128,128]{2,1,0:T(8,128)} fusion(f32[4,128,28,128]{3,1,2,0:T(8,128)} %fusion.21, s32[64]{0:T(128)S(1)} %reshape.173), kind=kCustom, calls=%fused_computation.1.clone | custom fusion | bytes 8389120 | tf_op jit(solution)/shard_map/jit(take_along_axis)/gather | solution.py:153
  286.1 3.7 %collective-permute-done.12 = f32[3]{0:T(128)S(1)} collective-permute-done((f32[3]{0:T(128)S(1)}, f32[3]{0:T(128)S(1)}, u32[]{:S(2)}, u32[]{:S(2)}) %collective-permute-start.12) | collective-permute-done | bytes 44 | tf_op jit(solution)/shard_map/ppermute | solution.py:56
  293.7 5.2 %fusion.5 = bf16[4,16,128,128]{3,2,1,0:T(8,128)(2,1)} fusion(f32[4,16,128,128]{3,2,1,0:T(8,128)} %bitcast.105, f32[4,16,128,128]{3,2,1,0:T(8,128)} %bitcast.104, f32[]{:T(128)} %bitcast.18, bf16[4,16,128,128]{3,2,1,0:T(8,128)(2,1)S(1)} %bitcast.107, f32[]{:T(128)S(6)} %sub.47, f32[]{:T(128)S(6)} %sub.44, pred[4,16]{1,0:T(4,128)(4,1)S(1)} %and_bitcast_fusion, ...), kind=kLoop, calls=%fused_computation.16 | loop fusion | flops 10485760 | bytes 12583052 | tf_op jit(solution)/shard_map/add | solution.py:213
  (85 shorter events, 57.3 us)
Async XLA Ops:
  5.2 7.9 %copy-start.6 = (s32[4,16]{1,0:T(4,128)S(1)}, s32[4,16]{1,0:T(4,128)}, u32[]{:S(2)}) copy-start(s32[4,16]{1,0:T(4,128)} %param.11) | copy-start | bytes 772
  5.3 9.8 %copy-start.1 = (bf16[4,9,128,128]{3,2,1,0:T(8,128)(2,1)}, bf16[4,9,128,128]{3,2,1,0:T(8,128)(2,1)S(1)}, u32[]{:S(2)}) copy-start(bf16[4,9,128,128]{3,2,1,0:T(8,128)(2,1)S(1)} %fusion.6.refs_1_.refs_2_) | copy-start | bytes 3538948
  5.3 28.1 %collective-permute-start.1 = (bf16[4,9,128,128]{3,2,1,0:T(8,128)(2,1)S(1)}, bf16[4,9,128,128]{3,2,1,0:T(8,128)(2,1)}, u32[]{:S(2)}, u32[]{:S(2)}) collective-permute-start(bf16[4,9,128,128]{3,2,1,0:T(8,128)(2,1)S(1)} %fusion.6.refs_1_.refs_2_), channel_id=1, source_target_pairs={{0,127},{1,0},{2,1},{3,2},{4,3},{5,4},{6,5},{7,6},{8,7},{9,8},{10,... | collective-permute-start | bytes 3538952 | tf_op jit(solution)/shard_map/ppermute | solution.py:16
  11.6 26.1 %collective-permute-start = (bf16[4,9,128,128]{3,2,1,0:T(8,128)(2,1)S(1)}, bf16[4,9,128,128]{3,2,1,0:T(8,128)(2,1)}, u32[]{:S(2)}, u32[]{:S(2)}) collective-permute-start(bf16[4,9,128,128]{3,2,1,0:T(8,128)(2,1)S(1)} %fusion.6.refs_1_.refs_2_), channel_id=1, source_target_pairs={{0,1},{1,2},{2,3},{3,4},{4,5},{5,6},{6,7},{7,8},{8,9},{9,10},{10,1... | collective-permute-start | bytes 3538952 | tf_op jit(solution)/shard_map/ppermute | solution.py:16
  15.1 33.0 %copy-start = (bf16[4,128,12,128]{3,2,1,0:T(8,128)(2,1)}, bf16[4,128,12,128]{3,2,1,0:T(8,128)(2,1)S(1)}, u32[]{:S(2)}) copy-start(bf16[4,128,12,128]{3,2,1,0:T(8,128)(2,1)S(1)} %convert_bitcast_fusion) | copy-start | bytes 4718596
  15.1 23.3 %copy-start.4 = (s32[4,8]{1,0:T(4,128)S(1)}, s32[4,8]{1,0:T(4,128)}, u32[]{:S(2)}) copy-start(s32[4,8]{1,0:T(4,128)} %param.9) | copy-start | bytes 388
  70.2 10.0 %copy-start.5 = (s32[4,16]{1,0:T(4,128)S(1)}, s32[4,16]{1,0:T(4,128)}, u32[]{:S(2)}) copy-start(s32[4,16]{1,0:T(4,128)} %param.12) | copy-start | bytes 772
  73.5 90.9 %collective-permute-start.4 = (bf16[4,17,128,128]{3,2,1,0:T(8,128)(2,1)}, bf16[4,17,128,128]{3,2,1,0:T(8,128)(2,1)}, u32[]{:S(2)}, u32[]{:S(2)}) collective-permute-start(bf16[4,17,128,128]{3,2,1,0:T(8,128)(2,1)} %fusion.4.refs_2_), channel_id=1, source_target_pairs={{0,127},{1,0},{2,1},{3,2},{4,3},{5,4},{6,5},{7,6},{8,7},{9,8},{10,... | collective-permute-start | bytes 6684680 | tf_op jit(solution)/shard_map/ppermute | solution.py:16
  74.2 90.2 %collective-permute-start.2 = (bf16[4,17,128,128]{3,2,1,0:T(8,128)(2,1)}, bf16[4,17,128,128]{3,2,1,0:T(8,128)(2,1)}, u32[]{:S(2)}, u32[]{:S(2)}) collective-permute-start(bf16[4,17,128,128]{3,2,1,0:T(8,128)(2,1)} %fusion.4.refs_2_), channel_id=1, source_target_pairs={{0,1},{1,2},{2,3},{3,4},{4,5},{5,6},{6,7},{7,8},{8,9},{9,10},{10,1... | collective-permute-start | bytes 6684680 | tf_op jit(solution)/shard_map/ppermute | solution.py:16
  76.1 70.4 %collective-permute-start.14 = (bf16[4,9,128,128]{3,2,1,0:T(8,128)(2,1)}, bf16[4,9,128,128]{3,2,1,0:T(8,128)(2,1)}, u32[]{:S(2)}, u32[]{:S(2)}) collective-permute-start(bf16[4,9,128,128]{3,2,1,0:T(8,128)(2,1)} %collective-permute-done.1.refs_2_.refs_3_), channel_id=1, source_target_pairs={{0,127},{1,0},{2,1},{3,2},{4,3},{5,4},{6,5},{7,6},{8,7},{9,8},{10,... | collective-permute-start | bytes 3538952 | tf_op jit(solution)/shard_map/ppermute | solution.py:16
  81.0 66.2 %collective-permute-start.13 = (bf16[4,9,128,128]{3,2,1,0:T(8,128)(2,1)}, bf16[4,9,128,128]{3,2,1,0:T(8,128)(2,1)}, u32[]{:S(2)}, u32[]{:S(2)}) collective-permute-start(bf16[4,9,128,128]{3,2,1,0:T(8,128)(2,1)} %collective-permute-done.refs_0_.refs_1_), channel_id=1, source_target_pairs={{0,1},{1,2},{2,3},{3,4},{4,5},{5,6},{6,7},{7,8},{8,9},{9,10},{10,1... | collective-permute-start | bytes 3538952 | tf_op jit(solution)/shard_map/ppermute | solution.py:16
  149.3 20.6 %copy-start.3 = (bf16[4,128,20,128]{1,3,2,0:T(8,128)(2,1)S(1)}, bf16[4,128,20,128]{1,3,2,0:T(8,128)(2,1)}, u32[]{:S(2)}) copy-start(bf16[4,128,20,128]{1,3,2,0:T(8,128)(2,1)} %copy.56) | copy-start | bytes 7864324
  164.4 51.9 %collective-permute-start.5 = (bf16[4,17,128,128]{3,2,1,0:T(8,128)(2,1)}, bf16[4,17,128,128]{3,2,1,0:T(8,128)(2,1)}, u32[]{:S(2)}, u32[]{:S(2)}) collective-permute-start(bf16[4,17,128,128]{3,2,1,0:T(8,128)(2,1)} %collective-permute-done.4.refs_3_), channel_id=1, source_target_pairs={{0,127},{1,0},{2,1},{3,2},{4,3},{5,4},{6,5},{7,6},{8,7},{9,8},{10,... | collective-permute-start | bytes 6684680 | tf_op jit(solution)/shard_map/ppermute | solution.py:16
  164.4 52.6 %collective-permute-start.3 = (bf16[4,17,128,128]{3,2,1,0:T(8,128)(2,1)}, bf16[4,17,128,128]{3,2,1,0:T(8,128)(2,1)}, u32[]{:S(2)}, u32[]{:S(2)}) collective-permute-start(bf16[4,17,128,128]{3,2,1,0:T(8,128)(2,1)} %collective-permute-done.2.refs_1_), channel_id=1, source_target_pairs={{0,1},{1,2},{2,3},{3,4},{4,5},{5,6},{6,7},{7,8},{8,9},{9,10},{10,1... | collective-permute-start | bytes 6684680 | tf_op jit(solution)/shard_map/ppermute | solution.py:16
  219.1 47.1 %collective-permute-start.6 = (f32[3]{0:T(128)S(1)}, f32[3]{0:T(128)S(1)}, u32[]{:S(2)}, u32[]{:S(2)}) collective-permute-start(f32[3]{0:T(128)S(1)} %pad_maximum_fusion), channel_id=1, source_target_pairs={{0,1},{1,0},{2,3},{3,2},{4,5},{5,4},{6,7},{7,6},{8,9},{9,8},{10,11... | collective-permute-start | bytes 44 | tf_op jit(solution)/shard_map/ppermute | solution.py:56
  260.2 33.4 %copy-start.2 = (bf16[64,128,128]{2,1,0:T(8,128)(2,1)S(1)}, bf16[64,128,128]{2,1,0:T(8,128)(2,1)}, u32[]{:S(2)}) copy-start(bf16[64,128,128]{2,1,0:T(8,128)(2,1)} %gather_fusion) | copy-start | bytes 6291460
  266.2 5.1 %collective-permute-start.7 = (f32[3]{0:T(128)S(1)}, f32[3]{0:T(128)S(1)}, u32[]{:S(2)}, u32[]{:S(2)}) collective-permute-start(f32[3]{0:T(128)S(1)} %add.167), channel_id=1, source_target_pairs={{0,2},{1,3},{2,0},{3,1},{4,6},{5,7},{6,4},{7,5},{8,10},{9,11},{10,... | collective-permute-start | bytes 44 | tf_op jit(solution)/shard_map/ppermute | solution.py:56
  271.3 3.6 %collective-permute-start.8 = (f32[3]{0:T(128)S(1)}, f32[3]{0:T(128)S(1)}, u32[]{:S(2)}, u32[]{:S(2)}) collective-permute-start(f32[3]{0:T(128)S(1)} %add.168), channel_id=1, source_target_pairs={{0,4},{1,5},{2,6},{3,7},{4,0},{5,1},{6,2},{7,3},{8,12},{9,13},{10,... | collective-permute-start | bytes 44 | tf_op jit(solution)/shard_map/ppermute | solution.py:56
  274.9 5.1 %collective-permute-start.9 = (f32[3]{0:T(128)S(1)}, f32[3]{0:T(128)S(1)}, u32[]{:S(2)}, u32[]{:S(2)}) collective-permute-start(f32[3]{0:T(128)S(1)} %add.169), channel_id=1, source_target_pairs={{0,8},{1,9},{2,10},{3,11},{4,12},{5,13},{6,14},{7,15},{8,0},{9,1},... | collective-permute-start | bytes 44 | tf_op jit(solution)/shard_map/ppermute | solution.py:56
  280.0 1.2 collective-permute-start.10
  281.1 3.6 %collective-permute-start.11 = (f32[3]{0:T(128)S(1)}, f32[3]{0:T(128)S(1)}, u32[]{:S(2)}, u32[]{:S(2)}) collective-permute-start(f32[3]{0:T(128)S(1)} %add.171), channel_id=1, source_target_pairs={{0,32},{1,33},{2,34},{3,35},{4,36},{5,37},{6,38},{7,39},{8,40},{9,... | collective-permute-start | bytes 44 | tf_op jit(solution)/shard_map/ppermute | solution.py:56
  284.7 5.1 %collective-permute-start.12 = (f32[3]{0:T(128)S(1)}, f32[3]{0:T(128)S(1)}, u32[]{:S(2)}, u32[]{:S(2)}) collective-permute-start(f32[3]{0:T(128)S(1)} %add.172), channel_id=1, source_target_pairs={{0,64},{1,65},{2,66},{3,67},{4,68},{5,69},{6,70},{7,71},{8,72},{9,... | collective-permute-start | bytes 44 | tf_op jit(solution)/shard_map/ppermute | solution.py:56

commit v6 on v4

--- a/solution.py
+++ b/solution.py
@@ -6,6 +6,7 @@
 from jax.sharding import PartitionSpec as P
 
 HALF = 4
+QUARTERS = 4
 BF16 = jnp.bfloat16
 F32 = jnp.float32
 
@@ -14,18 +15,6 @@
     count = lax.axis_size(axis)
     pairs = [(source, (source + steps) % count) for source in range(count)]
     return lax.ppermute(value, axis, pairs)
-
-
-def assemble(earlier, own_parts, later):
-    joined = []
-    for member in range(len(own_parts)):
-        pieces = (
-            [arrival[member] for arrival in reversed(earlier)]
-            + [own_parts[member]]
-            + [arrival[member] for arrival in later]
-        )
-        joined.append(jnp.concatenate(pieces, axis=0))
-    return tuple(joined)
 
 
 def spread(blocks, columns, reach_devices):
@@ -43,11 +32,12 @@
     count = 1
     for axis in axes:
         count *= lax.axis_size(axis)
-    step = 1
+    step, round_index = 1, 0
     while step < count:
         pairs = [(source, source ^ step) for source in range(count)]
         value = value + lax.ppermute(value, axes, pairs)
         step *= 2
+        round_index += 1
     return value
 
 
@@ -126,15 +116,6 @@
     return out.reshape(r, b, n, b)
 
 
-def slab_matmul(left, right):
-    r, b, k, _ = left.shape
-    n = right.shape[2]
-    out = jnp.dot(
-        left.reshape(r * b, k * b), right.reshape(k * b, n * b), preferred_element_type=F32
-    )
-    return out.reshape(r, b, n, b)
-
-
 def extract(dense, columns, low):
     onehot = place_onehot(0, dense.shape[0], columns, low, dense.shape[2])
     picked = jnp.einsum("rcs,rxcz->rsxz", onehot, dense, preferred_element_type=F32)
@@ -193,7 +174,20 @@
     total_two, total_three, total_four = sums[0], sums[1], sums[2]
 
     cube_dense = slab_matmul_nt(s_local, d_far)
-    quartic_dense = slab_matmul_nt(s_local, s_far)
+    block = s_local.shape[1]
+    width_cols = s_far.shape[0] // block
+    quarters = QUARTERS if width_cols % QUARTERS == 0 else 1
+    per = width_cols // quarters
+    places = jnp.arange(rows_here, dtype=jnp.int32)[:, None] + update_cols + 3 * HALF
+    quartic_part = None
+    for q in range(quarters):
+        dense_q = slab_matmul_nt(s_local, s_far[q * per * block : (q + 1) * per * block])
+        local = jnp.clip(places - q * per, 0, per - 1)
+        got = jnp.transpose(
+            jnp.take_along_axis(dense_q, local[:, None, :, None], axis=2), (0, 2, 1, 3)
+        )
+        inside = (places >= q * per) & (places < (q + 1) * per)
+        quartic_part = got if quartic_part is None else jnp.where(inside[:, :, None, None], got, quartic_part)
     gamma_mix = (target_trace[0] - 4.0 * total_three + 3.0 * total_four) / (
         total_two - 2.0 * total_three + total_four + 1e-06
     )
@@ -201,7 +195,6 @@
         jnp.pad(s_local, ((0, 0), (0, 0), (HALF, HALF), (0, 0))), update_cols, -3 * HALF
     ).astype(F32)
     cube_part = pick(cube_dense, update_cols, -3 * HALF)
-    quartic_part = pick(quartic_dense, update_cols, -3 * HALF)
     purified = (
         (4.0 - 2.0 * gamma_mix) * cube_part
         + (gamma_mix - 3.0) * quartic_part
@@ -211,6 +204,10 @@
 
 
 def solution(mesh):
+    return _mapped(mesh)
+
+
+def _mapped(mesh):
     return jax.shard_map(
         shards,
         mesh=mesh,

time: 298 us -> 324 us (1.087); the launches traced: 296 us -> 318 us
  local copies, waits for them, and re-layouts: 43.8 us -> 61.2 us
  waiting for transfers between devices: 71.8 us -> 65.4 us
  starting transfers between devices: 67.4 us -> 73.4 us
  other arithmetic: 21.3 us -> 26 us
    gather x0 -> x8, local copies, waits for them, and re-layouts: none -> 16.2 us  [shards(): jnp.take_along_axis(dense_q, local[:, None, :, None], axis=2)]
    convert_element_type x0 -> x1, other arithmetic: none -> 10 us  [shards(): purified = ((4.0 - 2.0 * gamma_mix) * cube_part + (gamma_mix - 3.0) * qua...]
    slice x0 -> x1, local copies, waits for them, and re-layouts: none -> 7.19 us  [shards(): s_far[q * per * block:(q + 1) * per * block]]
    ppermute x16, waiting for transfers between devices: 56.9 us -> 50.6 us  [passed_along(): return lax.ppermute(value, axis, pairs)]
    gather x5 -> x3, local copies, waits for them, and re-layouts: 16.3 us -> 10.2 us  [pick(): picked = jnp.take_along_axis(dense, places[:, None, :, None], axis=2)]
    ppermute x7, starting transfers between devices: 20.3 us -> 25.5 us  [butterfly_sum(): value = value + lax.ppermute(value, axes, pairs)]
    add x1 -> x0, other arithmetic: 5.22 us -> none  [shards(): (4.0 - 2.0 * gamma_mix) * cube_part + (gamma_mix - 3.0) * quartic_part]
    dot_general x3 -> x6, matrix products: 38.5 us -> 38.9 us  [slab_matmul_nt(): lax.dot_general(left.reshape(r * b, k * b), right_t, (((1,), (1,)), ((),...]
  transfers between devices with their start and end apart: 23 -> 23, of which waited for: 12 -> 13; matrix products, arithmetic and copies ran while one was open for 33% -> 38% of each run, Pallas kernels for 15% -> 14%
where the time goes in v6:
time: 324 us; the launch traced here: 318 us
  starting transfers between devices  73.4 us (23%)
  waiting for transfers between devices  65.4 us (20%)
  local copies, waits for them, and re-layouts  61.2 us (19%)
  Pallas kernels  44.1 us (14%)
  matrix products  43.1 us (13%)
  other arithmetic  26 us (8%)
  between operations  4.96 us (2%)
    ppermute x16, waiting for transfers between devices, passed_along(): return lax.ppermute(value, axis, pairs)  50.6 us
    ppermute x16, starting transfers between devices, passed_along(): return lax.ppermute(value, axis, pairs)  47.9 us
    pallas_call x3, Pallas kernels, densify_transposed(): pl.pallas_call(kernel, out_shape=jax.ShapeDtypeStruct((width * b, count *...  44.1 us
    dot_general x6, matrix products, slab_matmul_nt(): lax.dot_general(left.reshape(r * b, k * b), right_t, (((1,), (1,)), ((),...  38.9 us
    ppermute x7, starting transfers between devices, butterfly_sum(): value = value + lax.ppermute(value, axes, pairs)  25.5 us
    gather x8, local copies, waits for them, and re-layouts, shards(): jnp.take_along_axis(dense_q, local[:, None, :, None], axis=2)  16.2 us
    ppermute x7, waiting for transfers between devices, butterfly_sum(): value = value + lax.ppermute(value, axes, pairs)  14.9 us
    gather x3, local copies, waits for them, and re-layouts, pick(): picked = jnp.take_along_axis(dense, places[:, None, :, None], axis=2)  10.2 us
  transfers between devices with their start and end apart: 23, of which 13 were waited for; matrix products, arithmetic and copies ran while one was open for 38% of the time, Pallas kernels for 14%

profile of v6, /device:TPU:6, one launch (start us, length us, event | category | flops | bytes accessed | tf_op | source)
XLA Modules:
  0.0 318.1 jit_solution(13143965814824409457)
XLA Ops:
  0.6 6.3 %collective-permute-start.1 = (s32[4,8]{1,0:T(4,128)}, s32[4,8]{1,0:T(4,128)S(1)}, u32[]{:S(2)}, u32[]{:S(2)}) collective-permute-start(s32[4,8]{1,0:T(4,128)} %param.9), channel_id=1, source_target_pairs={{0,127},{1,0},{2,1},{3,2},{4,3},{5,4},{6,5},{7,6},{8,7},{9,8},{10,... | collective-permute-start | bytes 392 | tf_op jit(solution)/shard_map/ppermute | solution.py:17
  10.7 6.0 %collective-permute-start.3 = (bf16[4,8,128,128]{3,2,1,0:T(8,128)(2,1)S(1)}, bf16[4,8,128,128]{3,2,1,0:T(8,128)(2,1)}, u32[]{:S(2)}, u32[]{:S(2)}) collective-permute-start(bf16[4,8,128,128]{3,2,1,0:T(8,128)(2,1)S(1)} %bitcast.170), channel_id=1, source_target_pairs={{0,127},{1,0},{2,1},{3,2},{4,3},{5,4},{6,5},{7,6},{8,7},{9,8},{10,... | collective-permute-start | bytes 3145736 | tf_op jit(solution)/shard_map/ppermute | solution.py:17
  23.2 6.2 %collective-permute-start.21 = (s32[4,16]{1,0:T(4,128)S(1)}, s32[4,16]{1,0:T(4,128)S(1)}, u32[]{:S(2)}, u32[]{:S(2)}) collective-permute-start(s32[4,16]{1,0:T(4,128)S(1)} %copy-done.7), channel_id=1, source_target_pairs={{0,127},{1,0},{2,1},{3,2},{4,3},{5,4},{6,5},{7,6},{8,7},{9,8},{10,... | collective-permute-start | bytes 776 | tf_op jit(solution)/shard_map/ppermute | solution.py:17
  36.3 8.3 %shard_map.77 = bf16[2560,1536]{1,0:T(8,128)(2,1)} custom-call(s32[12,8]{1,0:T(8,128)} %compare_select_fusion.2.place_ref, s32[12,8]{1,0:T(8,128)} %and_convert_fusion.2.valid_ref, bf16[4,8,128,128]{3,2,1,0:T(8,128)(2,1)} %collective-permute-done.2.refs_0_.refs_1_, bf16[4,8,128,128]{3,2,1,0:T(8,128)(2,1)} %bitcast.171, ...), custom_call_target="tpu_custom_call" | custom-call | bytes 11010048 | tf_op jit(solution)/shard_map/pallas_call | solution.py:100
  44.6 7.9 %fusion.18 = bf16[4,128,20,128]{1,3,2,0:T(8,128)(2,1)S(1)} fusion(bf16[4,128,1536,1]{1,2,3,0:T(8,128)(2,1)} %bitcast.184, bf16[20,128,1536,1]{2,1,0,3:T(8,128)(2,1)} %bitcast.174), kind=kOutput, calls=%fused_computation.68 | convolution fusion | flops 4026531840 | bytes 12058624 | tf_op jit(solution)/shard_map/dot_general | solution.py:113
  55.7 4.3 %multiply_reduce_fusion = (f32[]{:T(128)}, bf16[4,128,20,128]{3,2,1,0:T(8,128)(2,1)S(1)}) fusion(bf16[4,128,20,128]{3,2,1,0:T(8,128)(2,1)} %copy.52, pred[4,20]{1,0:T(4,128)(4,1)S(1)} %broadcast_compare_fusion), kind=kLoop, calls=%fused_computation.6 | loop fusion | flops 5242879 | bytes 5242964 | tf_op jit(solution)/shard_map/reduce_sum | solution.py:169
  62.1 4.5 %copy.53 = bf16[4,16,128,128]{2,3,1,0:T(8,128)(2,1)} copy(bf16[4,16,128,128]{3,1,2,0:T(8,128)(2,1)} %fusion.8) | data formatting | bytes 4194304 | tf_op jit(solution)/shard_map/rcs,rxcz->rsxz/dot_general | solution.py:121
  66.9 5.7 %collective-permute-start.6 = (bf16[4,16,128,128]{3,2,1,0:T(8,128)(2,1)}, bf16[4,16,128,128]{3,2,1,0:T(8,128)(2,1)}, u32[]{:S(2)}, u32[]{:S(2)}) collective-permute-start(bf16[4,16,128,128]{3,2,1,0:T(8,128)(2,1)} %bitcast.161), channel_id=1, source_target_pairs={{0,127},{1,0},{2,1},{3,2},{4,3},{5,4},{6,5},{7,6},{8,7},{9,8},{10,... | collective-permute-start | bytes 6291464 | tf_op jit(solution)/shard_map/ppermute | solution.py:17
  73.8 5.9 %collective-permute-start.16 = (s32[4,8]{1,0:T(4,128)S(1)}, s32[4,8]{1,0:T(4,128)S(1)}, u32[]{:S(2)}, u32[]{:S(2)}) collective-permute-start(s32[4,8]{1,0:T(4,128)S(1)} %collective-permute-done.1), channel_id=1, source_target_pairs={{0,127},{1,0},{2,1},{3,2},{4,3},{5,4},{6,5},{7,6},{8,7},{9,8},{10,... | collective-permute-start | bytes 392 | tf_op jit(solution)/shard_map/ppermute | solution.py:17
  79.7 30.8 %collective-permute-done.15 = s32[4,8]{1,0:T(4,128)S(1)} collective-permute-done((s32[4,8]{1,0:T(4,128)S(1)}, s32[4,8]{1,0:T(4,128)S(1)}, u32[]{:S(2)}, u32[]{:S(2)}) %collective-permute-start.15) | collective-permute-done | bytes 160 | tf_op jit(solution)/shard_map/ppermute | solution.py:17
  117.9 5.8 %collective-permute-start.18 = (bf16[4,8,128,128]{3,2,1,0:T(8,128)(2,1)}, bf16[4,8,128,128]{3,2,1,0:T(8,128)(2,1)}, u32[]{:S(2)}, u32[]{:S(2)}) collective-permute-start(bf16[4,8,128,128]{3,2,1,0:T(8,128)(2,1)} %collective-permute-done.3.refs_2_.refs_3_), channel_id=1, source_target_pairs={{0,127},{1,0},{2,1},{3,2},{4,3},{5,4},{6,5},{7,6},{8,7},{9,8},{10,... | collective-permute-start | bytes 3145736 | tf_op jit(solution)/shard_map/ppermute | solution.py:17
  148.5 14.9 %shard_map.78 = bf16[3584,2560]{1,0:T(8,128)(2,1)} custom-call(s32[20,8]{1,0:T(8,128)} %compare_select_fusion.1.place_ref, s32[20,8]{1,0:T(8,128)} %and_convert_fusion.1.valid_ref, bf16[4,8,128,128]{3,2,1,0:T(8,128)(2,1)} %collective-permute-done.17.refs_0_, bf16[4,8,128,128]{3,2,1,0:T(8,128)(2,1)} %collective-permute-done.2.refs_0_.refs_1_, ...), custom_call_target="tpu_custom_call" | custom-call | bytes 23592960 | tf_op jit(solution)/shard_map/pallas_call | solution.py:100
  163.4 6.0 %collective-permute-start.7 = (bf16[4,16,128,128]{3,2,1,0:T(8,128)(2,1)}, bf16[4,16,128,128]{3,2,1,0:T(8,128)(2,1)}, u32[]{:S(2)}, u32[]{:S(2)}) collective-permute-start(bf16[4,16,128,128]{3,2,1,0:T(8,128)(2,1)} %collective-permute-done.6.refs_3_), channel_id=1, source_target_pairs={{0,127},{1,0},{2,1},{3,2},{4,3},{5,4},{6,5},{7,6},{8,7},{9,8},{10,... | collective-permute-start | bytes 6291464 | tf_op jit(solution)/shard_map/ppermute | solution.py:17
  169.4 15.4 %fusion.19 = f32[4,128,28,128]{3,1,2,0:T(8,128)} fusion(bf16[4,128,2560,1]{1,2,3,0:T(8,128)(2,1)S(1)} %bitcast.179, bf16[28,128,2560,1]{2,1,0,3:T(8,128)(2,1)} %bitcast.163), kind=kOutput, calls=%fused_computation.69 | convolution fusion | flops 9395240960 | bytes 28311552 | tf_op jit(solution)/shard_map/dot_general | solution.py:113
  184.8 6.0 %gather_fusion = f32[64,128,128]{2,1,0:T(8,128)} fusion(f32[4,128,28,128]{3,1,2,0:T(8,128)} %fusion.19, s32[64]{0:T(128)S(1)} %reshape.161), kind=kCustom, calls=%fused_computation.4 | custom fusion | bytes 8389120 | tf_op jit(solution)/shard_map/jit(take_along_axis)/gather | solution.py:127
  190.7 10.4 %collective-permute-done.5.refs_0_ = bf16[4,16,128,128]{3,2,1,0:T(8,128)(2,1)} collective-permute-done((bf16[4,16,128,128]{3,2,1,0:T(8,128)(2,1)}, bf16[4,16,128,128]{3,2,1,0:T(8,128)(2,1)}, u32[]{:S(2)}, u32[]{:S(2)}) %collective-permute-start.5) | collective-permute-done | bytes 2097184 | tf_op jit(solution)/shard_map/ppermute | solution.py:17
  207.1 20.9 %shard_map.79 = bf16[3584,2560]{1,0:T(8,128)(2,1)} custom-call(s32[20,16]{1,0:T(8,128)} %compare_select_fusion.place_ref, s32[20,16]{1,0:T(8,128)} %and_convert_fusion.valid_ref, bf16[4,16,128,128]{3,2,1,0:T(8,128)(2,1)} %collective-permute-done.5.refs_0_, bf16[4,16,128,128]{3,2,1,0:T(8,128)(2,1)} %collective-permute-done.4.refs_1_, ...), custom_call_target="tpu_custom_call" | custom-call | bytes 28835840 | tf_op jit(solution)/shard_map/pallas_call | solution.py:100
  228.0 7.2 %fusion.16 = (bf16[896,2560]{1,0:T(8,128)(2,1)S(1)}, bf16[896,2560]{1,0:T(8,128)(2,1)S(1)}, bf16[896,2560]{1,0:T(8,128)(2,1)S(1)}, bf16[896,2560]{1,0:T(8,128)(2,1)S(1)}) fusion(bf16[3584,2560]{1,0:T(8,128)(2,1)} %shard_map.79), kind=kLoop, calls=%fused_computation.66 | loop fusion | bytes 36700160 | tf_op jit(solution)/shard_map/slice | solution.py:184
  255.0 4.3 %gather_fusion.4 = f32[64,128,128]{2,1,0:T(8,128)} fusion(f32[4,128,7,128]{3,1,2,0:T(8,128)} %fusion.22, s32[64]{0:T(128)S(1)} %reshape.209), kind=kCustom, calls=%fused_computation.2.clone | custom fusion | bytes 8389120 | tf_op jit(solution)/shard_map/jit(take_along_axis)/gather | solution.py:187
  262.2 4.4 %gather_fusion.2 = f32[64,128,128]{2,1,0:T(8,128)} fusion(f32[4,128,7,128]{3,1,2,0:T(8,128)} %fusion.20, s32[64]{0:T(128)S(1)} %reshape.199), kind=kCustom, calls=%fused_computation.clone | custom fusion | bytes 8389120 | tf_op jit(solution)/shard_map/jit(take_along_axis)/gather | solution.py:187
  266.6 8.5 %collective-permute-start.9 = (f32[3]{0:T(128)S(1)}, f32[3]{0:T(128)S(1)}, u32[]{:S(2)}, u32[]{:S(2)}) collective-permute-start(f32[3]{0:T(128)S(1)} %add.176), channel_id=1, source_target_pairs={{0,2},{1,3},{2,0},{3,1},{4,6},{5,7},{6,4},{7,5},{8,10},{9,11},{10,... | collective-permute-start | bytes 44 | tf_op jit(solution)/shard_map/ppermute | solution.py:38
  280.3 12.3 %collective-permute-start.11 = (f32[3]{0:T(128)S(1)}, f32[3]{0:T(128)S(1)}, u32[]{:S(2)}, u32[]{:S(2)}) collective-permute-start(f32[3]{0:T(128)S(1)} %add.178), channel_id=1, source_target_pairs={{0,8},{1,9},{2,10},{3,11},{4,12},{5,13},{6,14},{7,15},{8,0},{9,1},... | collective-permute-start | bytes 44 | tf_op jit(solution)/shard_map/ppermute | solution.py:38
  298.8 5.1 %collective-permute-done.14 = f32[3]{0:T(128)S(1)} collective-permute-done((f32[3]{0:T(128)S(1)}, f32[3]{0:T(128)S(1)}, u32[]{:S(2)}, u32[]{:S(2)}) %collective-permute-start.14) | collective-permute-done | bytes 44 | tf_op jit(solution)/shard_map/ppermute | solution.py:38
  307.9 10.0 %fusion.5 = bf16[4,16,128,128]{3,2,1,0:T(8,128)(2,1)} fusion(bf16[4,16,128,128]{3,2,1,0:T(8,128)(2,1)S(1)} %bitcast.173, f32[]{:T(128)} %bitcast.14, f32[4,16,128,128]{3,2,1,0:T(8,128)} %bitcast.165, f32[4,16,128,128]{3,2,1,0:T(8,128)} %bitcast.166, f32[4,16,128,128]{3,2,1,0:T(8,128)} %bitcast.167, f32[4,16,128,128]{3,2,1,0:T(8,128)} %bitcast.168, ...), kind=kLoop, calls=%fused_computation.18 | loop fusion | flops 16777216 | bytes 25166348 | tf_op jit(solution)/shard_map/convert_element_type | solution.py:202
  (101 shorter events, 96.0 us)
Async XLA Ops:
  0.6 22.5 %collective-permute-start.1 = (s32[4,8]{1,0:T(4,128)}, s32[4,8]{1,0:T(4,128)S(1)}, u32[]{:S(2)}, u32[]{:S(2)}) collective-permute-start(s32[4,8]{1,0:T(4,128)} %param.9), channel_id=1, source_target_pairs={{0,127},{1,0},{2,1},{3,2},{4,3},{5,4},{6,5},{7,6},{8,7},{9,8},{10,... | collective-permute-start | bytes 392 | tf_op jit(solution)/shard_map/ppermute | solution.py:17
  6.9 22.5 %collective-permute-start = (s32[4,8]{1,0:T(4,128)}, s32[4,8]{1,0:T(4,128)S(1)}, u32[]{:S(2)}, u32[]{:S(2)}) collective-permute-start(s32[4,8]{1,0:T(4,128)} %param.9), channel_id=1, source_target_pairs={{0,1},{1,2},{2,3},{3,4},{4,5},{5,6},{6,7},{7,8},{8,9},{9,10},{10,1... | collective-permute-start | bytes 392 | tf_op jit(solution)/shard_map/ppermute | solution.py:17
  10.7 23.3 %collective-permute-start.2 = (bf16[4,8,128,128]{3,2,1,0:T(8,128)(2,1)S(1)}, bf16[4,8,128,128]{3,2,1,0:T(8,128)(2,1)}, u32[]{:S(2)}, u32[]{:S(2)}) collective-permute-start(bf16[4,8,128,128]{3,2,1,0:T(8,128)(2,1)S(1)} %bitcast.169), channel_id=1, source_target_pairs={{0,1},{1,2},{2,3},{3,4},{4,5},{5,6},{6,7},{7,8},{8,9},{9,10},{10,1... | collective-permute-start | bytes 3145736 | tf_op jit(solution)/shard_map/ppermute | solution.py:17
  10.7 25.6 %collective-permute-start.3 = (bf16[4,8,128,128]{3,2,1,0:T(8,128)(2,1)S(1)}, bf16[4,8,128,128]{3,2,1,0:T(8,128)(2,1)}, u32[]{:S(2)}, u32[]{:S(2)}) collective-permute-start(bf16[4,8,128,128]{3,2,1,0:T(8,128)(2,1)S(1)} %bitcast.170), channel_id=1, source_target_pairs={{0,127},{1,0},{2,1},{3,2},{4,3},{5,4},{6,5},{7,6},{8,7},{9,8},{10,... | collective-permute-start | bytes 3145736 | tf_op jit(solution)/shard_map/ppermute | solution.py:17
  16.7 57.1 %collective-permute-start.19 = (s32[4,16]{1,0:T(4,128)S(1)}, s32[4,16]{1,0:T(4,128)S(1)}, u32[]{:S(2)}, u32[]{:S(2)}) collective-permute-start(s32[4,16]{1,0:T(4,128)S(1)} %copy-done.7), channel_id=1, source_target_pairs={{0,1},{1,2},{2,3},{3,4},{4,5},{5,6},{6,7},{7,8},{8,9},{9,10},{10,1... | collective-permute-start | bytes 776 | tf_op jit(solution)/shard_map/ppermute | solution.py:17
  23.2 90.8 %collective-permute-start.21 = (s32[4,16]{1,0:T(4,128)S(1)}, s32[4,16]{1,0:T(4,128)S(1)}, u32[]{:S(2)}, u32[]{:S(2)}) collective-permute-start(s32[4,16]{1,0:T(4,128)S(1)} %copy-done.7), channel_id=1, source_target_pairs={{0,127},{1,0},{2,1},{3,2},{4,3},{5,4},{6,5},{7,6},{8,7},{9,8},{10,... | collective-permute-start | bytes 776 | tf_op jit(solution)/shard_map/ppermute | solution.py:17
  66.7 96.8 %collective-permute-start.4 = (bf16[4,16,128,128]{3,2,1,0:T(8,128)(2,1)}, bf16[4,16,128,128]{3,2,1,0:T(8,128)(2,1)}, u32[]{:S(2)}, u32[]{:S(2)}) collective-permute-start(bf16[4,16,128,128]{3,2,1,0:T(8,128)(2,1)} %bitcast.160), channel_id=1, source_target_pairs={{0,1},{1,2},{2,3},{3,4},{4,5},{5,6},{6,7},{7,8},{8,9},{9,10},{10,1... | collective-permute-start | bytes 6291464 | tf_op jit(solution)/shard_map/ppermute | solution.py:17
  66.9 96.5 %collective-permute-start.6 = (bf16[4,16,128,128]{3,2,1,0:T(8,128)(2,1)}, bf16[4,16,128,128]{3,2,1,0:T(8,128)(2,1)}, u32[]{:S(2)}, u32[]{:S(2)}) collective-permute-start(bf16[4,16,128,128]{3,2,1,0:T(8,128)(2,1)} %bitcast.161), channel_id=1, source_target_pairs={{0,127},{1,0},{2,1},{3,2},{4,3},{5,4},{6,5},{7,6},{8,7},{9,8},{10,... | collective-permute-start | bytes 6291464 | tf_op jit(solution)/shard_map/ppermute | solution.py:17
  73.8 36.8 %collective-permute-start.15 = (s32[4,8]{1,0:T(4,128)S(1)}, s32[4,8]{1,0:T(4,128)S(1)}, u32[]{:S(2)}, u32[]{:S(2)}) collective-permute-start(s32[4,8]{1,0:T(4,128)S(1)} %collective-permute-done), channel_id=1, source_target_pairs={{0,1},{1,2},{2,3},{3,4},{4,5},{5,6},{6,7},{7,8},{8,9},{9,10},{10,1... | collective-permute-start | bytes 392 | tf_op jit(solution)/shard_map/ppermute | solution.py:17
  73.8 39.5 %collective-permute-start.16 = (s32[4,8]{1,0:T(4,128)S(1)}, s32[4,8]{1,0:T(4,128)S(1)}, u32[]{:S(2)}, u32[]{:S(2)}) collective-permute-start(s32[4,8]{1,0:T(4,128)S(1)} %collective-permute-done.1), channel_id=1, source_target_pairs={{0,127},{1,0},{2,1},{3,2},{4,3},{5,4},{6,5},{7,6},{8,7},{9,8},{10,... | collective-permute-start | bytes 392 | tf_op jit(solution)/shard_map/ppermute | solution.py:17
  110.5 7.3 %collective-permute-start.20 = (s32[4,16]{1,0:T(4,128)S(1)}, s32[4,16]{1,0:T(4,128)S(1)}, u32[]{:S(2)}, u32[]{:S(2)}) collective-permute-start(s32[4,16]{1,0:T(4,128)S(1)} %collective-permute-done.19), channel_id=1, source_target_pairs={{0,1},{1,2},{2,3},{3,4},{4,5},{5,6},{6,7},{7,8},{8,9},{9,10},{10,1... | collective-permute-start | bytes 776 | tf_op jit(solution)/shard_map/ppermute | solution.py:17
  114.0 10.4 %collective-permute-start.22 = (s32[4,16]{1,0:T(4,128)S(1)}, s32[4,16]{1,0:T(4,128)S(1)}, u32[]{:S(2)}, u32[]{:S(2)}) collective-permute-start(s32[4,16]{1,0:T(4,128)S(1)} %collective-permute-done.21), channel_id=1, source_target_pairs={{0,127},{1,0},{2,1},{3,2},{4,3},{5,4},{6,5},{7,6},{8,7},{9,8},{10,... | collective-permute-start | bytes 776 | tf_op jit(solution)/shard_map/ppermute | solution.py:17
  117.2 31.3 %collective-permute-start.17 = (bf16[4,8,128,128]{3,2,1,0:T(8,128)(2,1)}, bf16[4,8,128,128]{3,2,1,0:T(8,128)(2,1)}, u32[]{:S(2)}, u32[]{:S(2)}) collective-permute-start(bf16[4,8,128,128]{3,2,1,0:T(8,128)(2,1)} %collective-permute-done.2.refs_0_.refs_1_), channel_id=1, source_target_pairs={{0,1},{1,2},{2,3},{3,4},{4,5},{5,6},{6,7},{7,8},{8,9},{9,10},{10,1... | collective-permute-start | bytes 3145736 | tf_op jit(solution)/shard_map/ppermute | solution.py:17
  117.9 30.6 %collective-permute-start.18 = (bf16[4,8,128,128]{3,2,1,0:T(8,128)(2,1)}, bf16[4,8,128,128]{3,2,1,0:T(8,128)(2,1)}, u32[]{:S(2)}, u32[]{:S(2)}) collective-permute-start(bf16[4,8,128,128]{3,2,1,0:T(8,128)(2,1)} %collective-permute-done.3.refs_2_.refs_3_), channel_id=1, source_target_pairs={{0,127},{1,0},{2,1},{3,2},{4,3},{5,4},{6,5},{7,6},{8,7},{9,8},{10,... | collective-permute-start | bytes 3145736 | tf_op jit(solution)/shard_map/ppermute | solution.py:17
  163.4 37.7 %collective-permute-start.5 = (bf16[4,16,128,128]{3,2,1,0:T(8,128)(2,1)}, bf16[4,16,128,128]{3,2,1,0:T(8,128)(2,1)}, u32[]{:S(2)}, u32[]{:S(2)}) collective-permute-start(bf16[4,16,128,128]{3,2,1,0:T(8,128)(2,1)} %collective-permute-done.4.refs_1_), channel_id=1, source_target_pairs={{0,1},{1,2},{2,3},{3,4},{4,5},{5,6},{6,7},{7,8},{8,9},{9,10},{10,1... | collective-permute-start | bytes 6291464 | tf_op jit(solution)/shard_map/ppermute | solution.py:17
  163.4 40.6 %collective-permute-start.7 = (bf16[4,16,128,128]{3,2,1,0:T(8,128)(2,1)}, bf16[4,16,128,128]{3,2,1,0:T(8,128)(2,1)}, u32[]{:S(2)}, u32[]{:S(2)}) collective-permute-start(bf16[4,16,128,128]{3,2,1,0:T(8,128)(2,1)} %collective-permute-done.6.refs_3_), channel_id=1, source_target_pairs={{0,127},{1,0},{2,1},{3,2},{4,3},{5,4},{6,5},{7,6},{8,7},{9,8},{10,... | collective-permute-start | bytes 6291464 | tf_op jit(solution)/shard_map/ppermute | solution.py:17
  204.0 62.6 %collective-permute-start.8 = (f32[3]{0:T(128)S(1)}, f32[3]{0:T(128)S(1)}, u32[]{:S(2)}, u32[]{:S(2)}) collective-permute-start(f32[3]{0:T(128)S(1)} %pad_maximum_fusion), channel_id=1, source_target_pairs={{0,1},{1,0},{2,3},{3,2},{4,5},{5,4},{6,7},{7,6},{8,9},{9,8},{10,11... | collective-permute-start | bytes 44 | tf_op jit(solution)/shard_map/ppermute | solution.py:38
  262.2 45.6 %copy-start.2 = (bf16[64,128,128]{2,1,0:T(8,128)(2,1)S(1)}, bf16[64,128,128]{2,1,0:T(8,128)(2,1)}, u32[]{:S(2)}) copy-start(bf16[64,128,128]{2,1,0:T(8,128)(2,1)} %gather_fusion.1) | copy-start | bytes 6291460
  266.6 10.1 %collective-permute-start.9 = (f32[3]{0:T(128)S(1)}, f32[3]{0:T(128)S(1)}, u32[]{:S(2)}, u32[]{:S(2)}) collective-permute-start(f32[3]{0:T(128)S(1)} %add.176), channel_id=1, source_target_pairs={{0,2},{1,3},{2,0},{3,1},{4,6},{5,7},{6,4},{7,5},{8,10},{9,11},{10,... | collective-permute-start | bytes 44 | tf_op jit(solution)/shard_map/ppermute | solution.py:38
  276.7 3.6 %collective-permute-start.10 = (f32[3]{0:T(128)S(1)}, f32[3]{0:T(128)S(1)}, u32[]{:S(2)}, u32[]{:S(2)}) collective-permute-start(f32[3]{0:T(128)S(1)} %add.177), channel_id=1, source_target_pairs={{0,4},{1,5},{2,6},{3,7},{4,0},{5,1},{6,2},{7,3},{8,12},{9,13},{10,... | collective-permute-start | bytes 44 | tf_op jit(solution)/shard_map/ppermute | solution.py:38
  280.3 13.8 %collective-permute-start.11 = (f32[3]{0:T(128)S(1)}, f32[3]{0:T(128)S(1)}, u32[]{:S(2)}, u32[]{:S(2)}) collective-permute-start(f32[3]{0:T(128)S(1)} %add.178), channel_id=1, source_target_pairs={{0,8},{1,9},{2,10},{3,11},{4,12},{5,13},{6,14},{7,15},{8,0},{9,1},... | collective-permute-start | bytes 44 | tf_op jit(solution)/shard_map/ppermute | solution.py:38
  294.1 1.2 collective-permute-start.12
  295.3 3.6 %collective-permute-start.13 = (f32[3]{0:T(128)S(1)}, f32[3]{0:T(128)S(1)}, u32[]{:S(2)}, u32[]{:S(2)}) collective-permute-start(f32[3]{0:T(128)S(1)} %add.180), channel_id=1, source_target_pairs={{0,32},{1,33},{2,34},{3,35},{4,36},{5,37},{6,38},{7,39},{8,40},{9,... | collective-permute-start | bytes 44 | tf_op jit(solution)/shard_map/ppermute | solution.py:38
  298.8 5.1 %collective-permute-start.14 = (f32[3]{0:T(128)S(1)}, f32[3]{0:T(128)S(1)}, u32[]{:S(2)}, u32[]{:S(2)}) collective-permute-start(f32[3]{0:T(128)S(1)} %add.181), channel_id=1, source_target_pairs={{0,64},{1,65},{2,66},{3,67},{4,68},{5,69},{6,70},{7,71},{8,72},{9,... | collective-permute-start | bytes 44 | tf_op jit(solution)/shard_map/ppermute | solution.py:38
  (7 other events, 108.1 us)
